TPU v7x, 512 devices: a whole 4x8x8 slice. The times are simulated.
512 devices in a mesh: dp: 32 (over y, x_lo, core), expert: 16 (over x_hi, z).
Axes of the slice: x: 4 (x_hi: 2, x_lo: 2; x = x_hi * 2 + x_lo), y: 8, z: 8, core: 2. Of those that a mesh axis runs over, the one named last changes fastest.
Arguments:
- tokens: bfloat16 [65536, 1024], P(('dp', 'expert')), may hold values from -24 to 24
- routing: int32 [65536, 2], P(('dp', 'expert')), may hold values from 0 to 15, as said below
- combine: float32 [65536, 2], P(('dp', 'expert')), may hold values from 0.1 to 1
- upstream: bfloat16 [65536, 1024], P(('dp', 'expert')), may hold values from -6 to 6
- gate_weight: bfloat16 [16, 1024, 384], P('expert', 'dp'), may hold values from -0.1875 to 0.1875
- up_weight: bfloat16 [16, 1024, 384], P('expert', 'dp'), may hold values from -0.1875 to 0.1875
- down_weight: bfloat16 [16, 1024, 384], P('expert', 'dp'), may hold values from -0.3125 to 0.3125
Outputs:
- layer_output: bfloat16 [65536, 1024], P(('dp', 'expert'))
- token_grad: bfloat16 [65536, 1024], P(('dp', 'expert'))
- combine_grad: float32 [65536, 2], P(('dp', 'expert'))
- gate_grad: float32 [16, 1024, 384], P('expert', 'dp')
- up_grad: float32 [16, 1024, 384], P('expert', 'dp')
Inputs may be any that keep to these rules, and one draw needn't show every extreme that they name: `routing`: each row names 2 different experts. The rows fall into blocks of 128 (the rows of one device), and 16 consecutive blocks form a data group. In each data group one expert, the group's hot expert, is named by exactly 64 rows of every block of the group; a second expert of the group is named by exactly 24 rows of every block of the group; every other expert is named by at most 24 rows of a block.
All inputs are finite; a program needn't handle non-finite values.
Results may differ from a plain program's by a relative error of at most 0.0065.
Values may be sent and summed in bfloat16 or wider, within the bound.
No kernel may reach another device: no remote copies, remote signals or barrier semaphores. Data moves between devices by JAX's collectives and lax.ppermute only.
A program may use at most 64 MiB of HBM per device.

v0:
```python
import jax
import jax.numpy as jnp
from jax import lax
from jax.sharding import PartitionSpec as P


def expert_forward(input_rows, gate_full, up_full, down_full):
    gate_pre = jnp.dot(input_rows, gate_full, preferred_element_type=jnp.float32)
    up_pre = jnp.dot(input_rows, up_full, preferred_element_type=jnp.float32)
    hidden = (jax.nn.silu(gate_pre) * up_pre).astype(jnp.bfloat16)
    results = lax.dot_general(
        hidden, down_full, (((1,), (1,)), ((), ())), preferred_element_type=jnp.float32
    )
    return (results.astype(jnp.bfloat16), gate_pre, up_pre)


def expert_backward(cotangent, gate_pre, up_pre, stacked, down_full):
    hidden_grad = jnp.dot(cotangent, down_full, preferred_element_type=jnp.float32)
    sigmoid_value = jax.nn.sigmoid(gate_pre)
    gate_delta = (
        hidden_grad * up_pre * sigmoid_value * (1.0 + gate_pre * (1.0 - sigmoid_value))
    ).astype(jnp.bfloat16)
    up_delta = (hidden_grad * jax.nn.silu(gate_pre)).astype(jnp.bfloat16)
    deltas = jnp.concatenate([gate_delta, up_delta], axis=1)
    input_grads = lax.dot_general(
        deltas, stacked, (((1,), (1,)), ((), ())), preferred_element_type=jnp.float32
    )
    return (input_grads.astype(jnp.bfloat16), deltas)


def trade_rows(buffer):
    return lax.all_to_all(buffer, "expert", split_axis=0, concat_axis=0, tiled=True)


def pick_slots(routing, expert_total):
    flat_ids = routing.reshape(-1)
    match_table = (flat_ids[:, None] == jnp.arange(expert_total, dtype=jnp.int32)[None, :]).astype(
        jnp.int32
    )
    position = jnp.sum((jnp.cumsum(match_table, axis=0) - 1) * match_table, axis=1)
    expert_loads = jnp.sum(match_table, axis=0)
    return (flat_ids, position, expert_loads)


def reduce_grads(arrived, deltas):
    piece = lax.dot_general(
        arrived, deltas, (((0,), (0,)), ((), ())), preferred_element_type=jnp.float32
    )
    return lax.psum_scatter(piece, "dp", scatter_dimension=0, tiled=True)


def shards(tokens, routing, combine, upstream, gate_weight, up_weight, down_weight):
    tok_count = tokens.shape[0]
    top_count = routing.shape[1]
    pick_total = tok_count * top_count
    feature_total = tokens.shape[1]
    hidden_total = gate_weight.shape[2]
    expert_total = lax.axis_size("expert")
    group_total = lax.axis_size("dp")
    capacity = max(tok_count // 2, top_count * tok_count // expert_total + tok_count // 4)
    gate_full, up_full, down_full = (
        lax.all_gather(gate_weight, "dp", axis=1, tiled=True),
        lax.all_gather(up_weight, "dp", axis=1, tiled=True),
        lax.all_gather(down_weight, "dp", axis=1, tiled=True),
    )
    gate_full = gate_full[0]
    up_full = up_full[0]
    down_full = down_full[0]
    stacked = jnp.concatenate([gate_full, up_full], axis=1)
    flat_ids, position, expert_loads = pick_slots(routing, expert_total)
    pick_index = jnp.arange(pick_total, dtype=jnp.int32)
    owners = pick_index // top_count
    upstream_wide = upstream.astype(jnp.float32)
    pick_cotangent = (
        (combine[:, :, None] * upstream_wide[:, None, :])
        .reshape(pick_total, feature_total)
        .astype(jnp.bfloat16)
    )
    slot_index = jnp.where(flat_ids >= 0, flat_ids * capacity + position, expert_total * capacity)
    token_source = (
        jnp.full((expert_total * capacity,), tok_count, jnp.int32)
        .at[slot_index]
        .set(owners, mode="drop")
    )
    pick_source = (
        jnp.full((expert_total * capacity,), pick_total, jnp.int32)
        .at[slot_index]
        .set(pick_index, mode="drop")
    )
    sending = jnp.take(tokens, token_source, axis=0, mode="fill", fill_value=0)
    arrived = trade_rows(sending.reshape(expert_total, capacity, feature_total)).reshape(
        expert_total * capacity, feature_total
    )
    results, gate_pre, up_pre = expert_forward(arrived, gate_full, up_full, down_full)
    returned = trade_rows(results.reshape(expert_total, capacity, feature_total)).reshape(
        expert_total * capacity, feature_total
    )
    pick_rows = jnp.take(returned, slot_index, axis=0, mode="fill", fill_value=0)
    cot_send = jnp.take(pick_cotangent, pick_source, axis=0, mode="fill", fill_value=0)
    cot_arrived = trade_rows(cot_send.reshape(expert_total, capacity, feature_total)).reshape(
        expert_total * capacity, feature_total
    )
    input_grads, deltas = expert_backward(cot_arrived, gate_pre, up_pre, stacked, down_full)
    grads_back = trade_rows(input_grads.reshape(expert_total, capacity, feature_total)).reshape(
        expert_total * capacity, feature_total
    )
    pick_grads = jnp.take(grads_back, slot_index, axis=0, mode="fill", fill_value=0)
    pick_rows, pick_grads, arrived, deltas = (pick_rows, pick_grads, arrived, deltas)
    summed = reduce_grads(arrived, deltas) / group_total
    gate_grad = summed[:, :hidden_total][None]
    up_grad = summed[:, hidden_total:][None]
    pick_wide = pick_rows.reshape(tok_count, top_count, feature_total).astype(jnp.float32)
    layer_output = jnp.sum(combine[:, :, None] * pick_wide, axis=1).astype(jnp.bfloat16)
    combine_grad = jnp.sum(upstream_wide[:, None, :] * pick_wide, axis=2)
    token_grad = jnp.sum(
        pick_grads.reshape(tok_count, top_count, feature_total).astype(jnp.float32), axis=1
    ).astype(jnp.bfloat16)
    return (layer_output, token_grad, combine_grad, gate_grad, up_grad)


def solution(mesh):
    placed = (
        P(("dp", "expert"), None),
        P(("dp", "expert"), None),
        P(("dp", "expert"), None),
        P(("dp", "expert"), None),
        P("expert", "dp", None),
        P("expert", "dp", None),
        P("expert", "dp", None),
    )
    return jax.shard_map(
        shards,
        mesh=mesh,
        in_specs=placed,
        out_specs=(
            P(("dp", "expert"), None),
            P(("dp", "expert"), None),
            P(("dp", "expert"), None),
            P("expert", "dp", None),
            P("expert", "dp", None),
        ),
        check_vma=False,
    )
```

profile of v0, /device:TPU:155, one launch (start us, length us, event | category | flops | bytes accessed | tf_op | source)
XLA Modules:
  0.0 421.1 jit_solution(15127562620850006732)
XLA Ops:
  11.1 1.4 scatter_custom_fusion
  12.7 4.1 gather_fusion
  16.7 1.6 broadcast_select_fusion.1
  18.3 10.2 %all-to-all-start = ((bf16[16,64,1024]{2,1,0:T(8,128)(2,1)}), bf16[16,64,1024]{2,1,0:T(8,128)(2,1)S(1)}, u32[]{:S(2)}, u32[]{:S(2)}) async-start(bf16[16,64,1024]{2,1,0:T(8,128)(2,1)} %broadcast_select_fusion.1), calls=%async_computation | async-start | bytes 4194304 | tf_op jit(solution)/shard_map/all_to_all | solution.py:32
  28.5 49.1 %all_gather.10 = bf16[1,1024,384]{2,1,0:T(8,128)(2,1)S(1)} all-gather(bf16[1,32,384]{2,1,0:T(8,128)(2,1)S(1)} %copy-done.10), channel_id=1, replica_groups=mesh['dp'=32,'expert'=16] {'dp'}, dimensions={1}, use_global_device_ids=true | all-gather | bytes 811008 | tf_op jit(solution)/shard_map/all_gather | solution.py:63
  77.6 36.6 %all_gather.9 = bf16[1,1024,384]{2,1,0:T(8,128)(2,1)} all-gather(bf16[1,32,384]{2,1,0:T(8,128)(2,1)S(1)} %copy-done.11), channel_id=1, replica_groups=mesh['dp'=32,'expert'=16] {'dp'}, dimensions={1}, use_global_device_ids=true | all-gather | bytes 811008 | tf_op jit(solution)/shard_map/all_gather | solution.py:62
  114.2 35.7 %all_gather.11 = bf16[1,1024,384]{2,1,0:T(8,128)(2,1)} all-gather(bf16[1,32,384]{2,1,0:T(8,128)(2,1)S(1)} %copy-done.12), channel_id=1, replica_groups=mesh['dp'=32,'expert'=16] {'dp'}, dimensions={1}, use_global_device_ids=true | all-gather | bytes 811008 | tf_op jit(solution)/shard_map/all_gather | solution.py:64
  149.9 1.0 fusion.20
  151.5 1.0 fusion.22
  153.2 2.6 convolution_convert_fusion
  155.8 6.1 %all-to-all-start.1 = ((bf16[16,64,1024]{2,1,0:T(8,128)(2,1)}), bf16[16,64,1024]{2,1,0:T(8,128)(2,1)S(1)}, u32[]{:S(2)}, u32[]{:S(2)}) async-start(bf16[16,64,1024]{2,1,0:T(8,128)(2,1)} %bitcast.53), calls=%async_computation.1 | async-start | bytes 4194304 | tf_op jit(solution)/shard_map/all_to_all | solution.py:32
  162.2 1.2 mul.91
  163.4 1.7 mul.92
  165.2 1.4 scatter_custom_fusion.1
  166.7 42.2 %all-to-all-done.1 = bf16[16,64,1024]{2,1,0:T(8,128)(2,1)S(1)} async-done(((bf16[16,64,1024]{2,1,0:T(8,128)(2,1)}), bf16[16,64,1024]{2,1,0:T(8,128)(2,1)S(1)}, u32[]{:S(2)}, u32[]{:S(2)}) %all-to-all-start.1) | async-done | bytes 2097184 | tf_op jit(solution)/shard_map/all_to_all | solution.py:32
  208.9 1.2 gather_fusion.2
  210.1 1.5 multiply_reduce_fusion
  211.6 4.1 gather_fusion.1
  215.9 56.3 %all_to_all.20 = bf16[16,64,1024]{2,1,0:T(8,128)(2,1)S(1)} all-to-all(bf16[16,64,1024]{2,1,0:T(8,128)(2,1)S(1)} %broadcast_select_fusion), channel_id=1, replica_groups=mesh['dp'=32,'expert'=16] {'expert'}, dimensions={0} | all-to-all | bytes 4194304 | tf_op jit(solution)/shard_map/all_to_all | solution.py:32
  272.2 1.5 multiply_convert_fusion.1
  273.8 0.9 copy-done.18
  274.7 3.5 fusion.4
  278.2 1.1 copy-done.5
  279.6 4.3 %convolution_convert_fusion.1 = bf16[1024,1024]{1,0:T(8,128)(2,1)} fusion(bf16[1024,384]{1,0:T(8,128)(2,1)S(1)} %bitcast.56, bf16[1024,384]{1,0:T(8,128)(2,1)S(1)} %bitcast.57, bf16[1024,384]{0,1:T(8,128)(2,1)} %copy-done.18, bf16[1024,384]{0,1:T(8,128)(2,1)S(1)} %get-tuple-element.13), kind=kOutput, calls=%fused_computation.9 | convolution fusion | flops 1617952768 | bytes 5242880 | tf_op jit(solution)/shard_map/dot_general | solution.py:25
  283.9 8.4 %all-to-all-start.3 = ((bf16[16,64,1024]{2,1,0:T(8,128)(2,1)}), bf16[16,64,1024]{2,1,0:T(8,128)(2,1)S(1)}, u32[]{:S(2)}, u32[]{:S(2)}) async-start(bf16[16,64,1024]{2,1,0:T(8,128)(2,1)} %bitcast.54), calls=%async_computation.3 | async-start | bytes 4194304 | tf_op jit(solution)/shard_map/all_to_all | solution.py:32
  293.0 45.4 %all-to-all-done.3 = bf16[16,64,1024]{2,1,0:T(8,128)(2,1)S(1)} async-done(((bf16[16,64,1024]{2,1,0:T(8,128)(2,1)}), bf16[16,64,1024]{2,1,0:T(8,128)(2,1)S(1)}, u32[]{:S(2)}, u32[]{:S(2)}) %all-to-all-start.3) | async-done | bytes 2097184 | tf_op jit(solution)/shard_map/all_to_all | solution.py:32
  338.5 1.2 gather_fusion.3
  339.6 1.0 broadcast_select_fusion.2
  341.9 2.1 reduce_sum.46
  343.9 2.1 multiply_reduce_fusion.1
  346.0 66.7 %reduce-scatter.2.cloned.1.call-done = f32[32,768]{1,0:T(8,128)} async-done(((f32[1024,768]{1,0:T(8,128)}), f32[32,768]{1,0:T(8,128)}) %reduce-scatter.2.cloned.1.call-update) | async-done | bytes 98320 | tf_op jit(solution)/shard_map/reduce_scatter | solution.py:49
  412.8 0.9 broadcast_multiply_fusion
  (73 shorter events, 8.9 us)
Async XLA Ops:
  7.2 5.5 %copy-start = (bf16[128,1024]{1,0:T(8,128)(2,1)S(1)}, bf16[128,1024]{1,0:T(8,128)(2,1)}, u32[]{:S(2)}) copy-start(bf16[128,1024]{1,0:T(8,128)(2,1)} %param.9) | copy-start | bytes 786436
  18.3 10.2 %copy-start.10 = (bf16[1,32,384]{2,1,0:T(8,128)(2,1)S(1)}, bf16[1,32,384]{2,1,0:T(8,128)(2,1)}, u32[]{:S(2)}) copy-start(bf16[1,32,384]{2,1,0:T(8,128)(2,1)} %param.14) | copy-start | bytes 73732
  18.3 59.3 %copy-start.11 = (bf16[1,32,384]{2,1,0:T(8,128)(2,1)S(1)}, bf16[1,32,384]{2,1,0:T(8,128)(2,1)}, u32[]{:S(2)}) copy-start(bf16[1,32,384]{2,1,0:T(8,128)(2,1)} %param.13) | copy-start | bytes 73732
  18.3 95.9 %copy-start.12 = (bf16[1,32,384]{2,1,0:T(8,128)(2,1)S(1)}, bf16[1,32,384]{2,1,0:T(8,128)(2,1)}, u32[]{:S(2)}) copy-start(bf16[1,32,384]{2,1,0:T(8,128)(2,1)} %param.15) | copy-start | bytes 73732
  18.3 131.5 %all-to-all-start = ((bf16[16,64,1024]{2,1,0:T(8,128)(2,1)}), bf16[16,64,1024]{2,1,0:T(8,128)(2,1)S(1)}, u32[]{:S(2)}, u32[]{:S(2)}) async-start(bf16[16,64,1024]{2,1,0:T(8,128)(2,1)} %broadcast_select_fusion.1), calls=%async_computation | async-start | bytes 4194304 | tf_op jit(solution)/shard_map/all_to_all | solution.py:32
  77.6 73.3 %copy-start.4 = (bf16[1,1024,384]{2,1,0:T(8,128)(2,1)}, bf16[1,1024,384]{2,1,0:T(8,128)(2,1)S(1)}, u32[]{:S(2)}) copy-start(bf16[1,1024,384]{2,1,0:T(8,128)(2,1)S(1)} %all_gather.10) | copy-start | bytes 2359300
  149.8 1.3 copy-start.1
  149.8 1.7 copy-start.6
  151.5 1.2 copy-start.14
  151.5 1.7 copy-start.8
  153.2 2.6 copy-start.16
  155.8 6.1 %copy-start.13 = (f32[128,2]{0,1:T(2,128)S(1)}, f32[128,2]{0,1:T(2,128)}, u32[]{:S(2)}) copy-start(f32[128,2]{0,1:T(2,128)} %param.11) | copy-start | bytes 3076
  155.8 53.1 %all-to-all-start.1 = ((bf16[16,64,1024]{2,1,0:T(8,128)(2,1)}), bf16[16,64,1024]{2,1,0:T(8,128)(2,1)S(1)}, u32[]{:S(2)}, u32[]{:S(2)}) async-start(bf16[16,64,1024]{2,1,0:T(8,128)(2,1)} %bitcast.53), calls=%async_computation.1 | async-start | bytes 4194304 | tf_op jit(solution)/shard_map/all_to_all | solution.py:32
  161.9 250.9 %reduce-scatter.2.cloned.1.call-start = ((), (), s32[]{:S(2)}) async-start(), calls=%async_computation.5 | async-start | bytes 3244032 | tf_op jit(solution)/shard_map/reduce_scatter | solution.py:49
  215.9 56.3 %copy-start.9 = (bf16[1,1024,384]{2,1,0:T(8,128)(2,1)S(1)}, bf16[1,1024,384]{2,1,0:T(8,128)(2,1)}, u32[]{:S(2)}) copy-start(bf16[1,1024,384]{2,1,0:T(8,128)(2,1)} %all_gather.11) | copy-start | bytes 2359300
  215.9 56.3 %copy-start.15 = (f32[1024,384]{0,1:T(8,128)S(1)}, f32[1024,384]{0,1:T(8,128)}, u32[]{:S(2)}) copy-start(f32[1024,384]{0,1:T(8,128)} %copy-done.14) | copy-start | bytes 4718596
  215.9 56.3 %copy-start.17 = (f32[1024,384]{0,1:T(8,128)S(1)}, f32[1024,384]{0,1:T(8,128)}, u32[]{:S(2)}) copy-start(f32[1024,384]{0,1:T(8,128)} %copy-done.16) | copy-start | bytes 4718596
  272.2 2.5 copy-start.2
  273.8 0.9 copy-start.18
  278.2 1.1 copy-start.5
  278.2 1.4 copy-start.7
  283.9 54.6 %all-to-all-start.3 = ((bf16[16,64,1024]{2,1,0:T(8,128)(2,1)}), bf16[16,64,1024]{2,1,0:T(8,128)(2,1)S(1)}, u32[]{:S(2)}, u32[]{:S(2)}) async-start(bf16[16,64,1024]{2,1,0:T(8,128)(2,1)} %bitcast.54), calls=%async_computation.3 | async-start | bytes 4194304 | tf_op jit(solution)/shard_map/all_to_all | solution.py:32
  340.6 1.0 copy-start.3
Sparse Core Ops, SparseCore 0:
  278.3 134.3 reduce-scatter.1
where the time goes:
time: 423 us; the launch traced here: 421 us
  blocking collectives  178 us (42%)
  waiting for transfers between devices  154 us (36%)
  local copies, waits for them, and re-layouts  24.7 us (6%)
  starting transfers between devices  24.7 us (6%)
  between operations  14.3 us (3%)
  matrix products  14 us (3%)
  other arithmetic  11.5 us (3%)
    all_to_all x3, waiting for transfers between devices, trade_rows(): lax.all_to_all(buffer, 'expert', split_axis=0, concat_axis=0, tiled=True)  87.6 us
    reduce_scatter x1, waiting for transfers between devices, reduce_grads(): return lax.psum_scatter(piece, 'dp', scatter_dimension=0, tiled=True)  66.7 us
    all_to_all x1, blocking collectives, trade_rows(): lax.all_to_all(buffer, 'expert', split_axis=0, concat_axis=0, tiled=True)  56.3 us
    all_gather x1, blocking collectives, shards(): lax.all_gather(up_weight, 'dp', axis=1, tiled=True)  49.1 us
    all_gather x1, blocking collectives, shards(): lax.all_gather(gate_weight, 'dp', axis=1, tiled=True)  36.6 us
    all_gather x1, blocking collectives, shards(): lax.all_gather(down_weight, 'dp', axis=1, tiled=True)  35.7 us
    all_to_all x3, starting transfers between devices, trade_rows(): lax.all_to_all(buffer, 'expert', split_axis=0, concat_axis=0, tiled=True)  24.6 us
  transfers between devices with their start and end apart: 4, of which 3 were waited for; matrix products, arithmetic and copies ran while one was open for 4% of the time, Pallas kernels for 0%

commit v1 on v0

--- a/solution.py
+++ b/solution.py
@@ -42,13 +42,6 @@
     return (flat_ids, position, expert_loads)
 
 
-def reduce_grads(arrived, deltas):
-    piece = lax.dot_general(
-        arrived, deltas, (((0,), (0,)), ((), ())), preferred_element_type=jnp.float32
-    )
-    return lax.psum_scatter(piece, "dp", scatter_dimension=0, tiled=True)
-
-
 def shards(tokens, routing, combine, upstream, gate_weight, up_weight, down_weight):
     tok_count = tokens.shape[0]
     top_count = routing.shape[1]
@@ -58,15 +51,12 @@
     expert_total = lax.axis_size("expert")
     group_total = lax.axis_size("dp")
     capacity = max(tok_count // 2, top_count * tok_count // expert_total + tok_count // 4)
-    gate_full, up_full, down_full = (
-        lax.all_gather(gate_weight, "dp", axis=1, tiled=True),
-        lax.all_gather(up_weight, "dp", axis=1, tiled=True),
-        lax.all_gather(down_weight, "dp", axis=1, tiled=True),
-    )
-    gate_full = gate_full[0]
-    up_full = up_full[0]
-    down_full = down_full[0]
-    stacked = jnp.concatenate([gate_full, up_full], axis=1)
+    local_weights = jnp.concatenate([gate_weight[0], up_weight[0], down_weight[0]], axis=1)
+    full_weights = lax.all_gather(local_weights, "dp", axis=0, tiled=True)
+    gate_full = full_weights[:, :hidden_total]
+    up_full = full_weights[:, hidden_total : 2 * hidden_total]
+    down_full = full_weights[:, 2 * hidden_total :]
+    stacked = full_weights[:, : 2 * hidden_total]
     flat_ids, position, expert_loads = pick_slots(routing, expert_total)
     pick_index = jnp.arange(pick_total, dtype=jnp.int32)
     owners = pick_index // top_count
@@ -87,26 +77,31 @@
         .at[slot_index]
         .set(pick_index, mode="drop")
     )
-    sending = jnp.take(tokens, token_source, axis=0, mode="fill", fill_value=0)
-    arrived = trade_rows(sending.reshape(expert_total, capacity, feature_total)).reshape(
-        expert_total * capacity, feature_total
+    sending = jnp.concatenate(
+        [
+            jnp.take(tokens, token_source, axis=0, mode="fill", fill_value=0),
+            jnp.take(pick_cotangent, pick_source, axis=0, mode="fill", fill_value=0),
+        ],
+        axis=1,
     )
+    arrived_both = trade_rows(
+        sending.reshape(expert_total, capacity, 2 * feature_total)
+    ).reshape(expert_total * capacity, 2 * feature_total)
+    arrived = arrived_both[:, :feature_total]
+    cot_arrived = arrived_both[:, feature_total:]
     results, gate_pre, up_pre = expert_forward(arrived, gate_full, up_full, down_full)
-    returned = trade_rows(results.reshape(expert_total, capacity, feature_total)).reshape(
-        expert_total * capacity, feature_total
+    input_grads, deltas = expert_backward(cot_arrived, gate_pre, up_pre, stacked, down_full)
+    piece = lax.dot_general(
+        arrived, deltas, (((0,), (0,)), ((), ())), preferred_element_type=jnp.float32
     )
-    pick_rows = jnp.take(returned, slot_index, axis=0, mode="fill", fill_value=0)
-    cot_send = jnp.take(pick_cotangent, pick_source, axis=0, mode="fill", fill_value=0)
-    cot_arrived = trade_rows(cot_send.reshape(expert_total, capacity, feature_total)).reshape(
-        expert_total * capacity, feature_total
+    summed = lax.psum_scatter(piece, "dp", scatter_dimension=0, tiled=True) / group_total
+    back = jnp.concatenate([results, input_grads], axis=1)
+    returned = trade_rows(back.reshape(expert_total, capacity, 2 * feature_total)).reshape(
+        expert_total * capacity, 2 * feature_total
     )
-    input_grads, deltas = expert_backward(cot_arrived, gate_pre, up_pre, stacked, down_full)
-    grads_back = trade_rows(input_grads.reshape(expert_total, capacity, feature_total)).reshape(
-        expert_total * capacity, feature_total
-    )
-    pick_grads = jnp.take(grads_back, slot_index, axis=0, mode="fill", fill_value=0)
-    pick_rows, pick_grads, arrived, deltas = (pick_rows, pick_grads, arrived, deltas)
-    summed = reduce_grads(arrived, deltas) / group_total
+    pick_both = jnp.take(returned, slot_index, axis=0, mode="fill", fill_value=0)
+    pick_rows = pick_both[:, :feature_total]
+    pick_grads = pick_both[:, feature_total:]
     gate_grad = summed[:, :hidden_total][None]
     up_grad = summed[:, hidden_total:][None]
     pick_wide = pick_rows.reshape(tok_count, top_count, feature_total).astype(jnp.float32)

time: 423 us -> 336 us (0.79)
  the two profiles are of different devices: /device:TPU:155 before, /device:TPU:260 now
where the time goes in v1:
time: 336 us; the launch traced here: 335 us
  waiting for transfers between devices  237 us (71%)
  local copies, waits for them, and re-layouts  31.6 us (9%)
  starting transfers between devices  19.9 us (6%)
  matrix products  17.1 us (5%)
  other arithmetic  15.1 us (4%)
  between operations  14.3 us (4%)
    reduce_scatter x1, waiting for transfers between devices, shards(): lax.psum_scatter(piece, 'dp', scatter_dimension=0, tiled=True) / group_total  144 us
    all_gather x1, waiting for transfers between devices, shards(): full_weights = lax.all_gather(local_weights, 'dp', axis=0, tiled=True)  92 us
    all_to_all x2, starting transfers between devices, trade_rows(): lax.all_to_all(buffer, 'expert', split_axis=0, concat_axis=0, tiled=True)  19.4 us
  transfers between devices with their start and end apart: 4, of which 3 were waited for; matrix products, arithmetic and copies ran while one was open for 2% of the time, Pallas kernels for 0%

profile of v1, /device:TPU:260, one launch (start us, length us, event | category | flops | bytes accessed | tf_op | source)
XLA Modules:
  0.0 335.1 jit_solution(15905471799969970802)
XLA Ops:
  7.2 0.8 copy.15
  8.3 0.7 broadcast_multiply_fusion.1
  9.0 0.7 broadcast_compare_fusion
  11.2 1.4 scatter_custom_fusion
  12.6 1.4 scatter_custom_fusion.1
  14.0 1.2 mul.90
  15.3 0.7 mul.91
  16.6 5.4 %gather_fusion.1 = bf16[1024,1024]{1,0:T(8,128)(2,1)} fusion(bf16[256,1024]{1,0:T(8,128)(2,1)S(1)} %multiply_convert_fusion.3, s32[1024]{0:T(1024)S(1)} %fusion.19), kind=kCustom, calls=%fused_computation.1 | custom fusion | bytes 4198400 | tf_op jit(solution)/shard_map/jit(_take)/gather | solution.py:83
  21.9 5.4 %gather_fusion = bf16[1024,1024]{1,0:T(8,128)(2,1)} fusion(bf16[128,1024]{1,0:T(8,128)(2,1)S(1)} %copy-done, s32[1024]{0:T(1024)S(1)} %fusion.18), kind=kCustom, calls=%fused_computation | custom fusion | bytes 4198400 | tf_op jit(solution)/shard_map/jit(_take)/gather | solution.py:82
  27.3 1.8 broadcast_select_fusion
  29.1 2.4 pad_maximum_fusion
  31.5 9.8 %all-to-all-start = ((bf16[16,64,2048]{2,1,0:T(8,128)(2,1)}), bf16[16,64,2048]{2,1,0:T(8,128)(2,1)}, u32[]{:S(2)}, u32[]{:S(2)}) async-start(bf16[16,64,2048]{2,1,0:T(8,128)(2,1)} %pad_maximum_fusion), calls=%async_computation | async-start | bytes 8388608 | tf_op jit(solution)/shard_map/all_to_all | solution.py:32
  41.6 0.6 pad_maximum_fusion.5
  42.3 92.0 %all-gather.2.cloned.1.call-done = bf16[1024,1152]{1,0:T(8,128)(2,1)} async-done(((bf16[32,1152]{1,0:T(8,128)(2,1)}), bf16[1024,1152]{1,0:T(8,128)(2,1)}) %all-gather.2.cloned.1.call-update) | async-done | bytes 2359312 | tf_op jit(solution)/shard_map/all_gather | solution.py:55
  134.2 1.5 all-to-all-done
  135.8 2.9 fusion.4
  138.7 2.6 fusion
  141.3 3.2 multiply_convert_fusion.1
  144.6 1.4 convolution_convert_fusion
  145.9 1.8 convolution_convert_fusion.1
  147.8 2.4 pad_maximum_fusion.1
  150.2 6.5 %copy.21 = bf16[1024,2048]{1,0:T(8,128)(2,1)} copy(bf16[1024,2048]{0,1:T(8,128)(2,1)} %pad_maximum_fusion.1) | data formatting | bytes 8388608 | tf_op jit(solution)/shard_map/concatenate | solution.py:98
  156.7 9.6 %all-to-all-start.1 = ((bf16[16,64,2048]{2,1,0:T(8,128)(2,1)}), bf16[16,64,2048]{2,1,0:T(8,128)(2,1)}, u32[]{:S(2)}, u32[]{:S(2)}) async-start(bf16[16,64,2048]{2,1,0:T(8,128)(2,1)} %bitcast.29), calls=%async_computation.1 | async-start | bytes 8388608 | tf_op jit(solution)/shard_map/all_to_all | solution.py:32
  166.6 5.1 %fusion.2 = f32[1024,768]{1,0:T(8,128)} fusion(bf16[1024,2048]{1,0:T(8,128)(2,1)} %bitcast.5, bf16[1024,384]{0,1:T(8,128)(2,1)S(1)} %get-tuple-element.11, bf16[1024,384]{0,1:T(8,128)(2,1)S(1)} %get-tuple-element.10), kind=kOutput, calls=%fused_computation.13 | convolution fusion | flops 1613758464 | bytes 6815744 | tf_op jit(solution)/shard_map/dot_general | solution.py:94
  171.8 143.6 %reduce-scatter.2.cloned.1.call-done = f32[32,768]{1,0:T(8,128)} async-done(((f32[1024,768]{1,0:T(8,128)}), f32[32,768]{1,0:T(8,128)}) %reduce-scatter.2.cloned.1.call-update) | async-done | bytes 98320 | tf_op jit(solution)/shard_map/reduce_scatter | solution.py:97
  315.4 0.9 broadcast_multiply_fusion
  316.3 0.6 slice_bitcast_fusion
  316.9 5.1 %gather_fusion.2 = bf16[256,2048]{1,0:T(8,128)(2,1)S(1)} fusion(bf16[1024,2048]{1,0:T(8,128)(2,1)} %bitcast.10, s32[1024]{0:T(1024)S(1)} %pad_clamp_fusion), kind=kCustom, calls=%fused_computation.2 | custom fusion | bytes 2098176 | tf_op jit(solution)/shard_map/jit(_take)/gather | solution.py:102
  322.5 0.6 reshape.134
  323.2 2.1 multiply_reduce_fusion.1
  325.6 0.6 copy.22
  326.2 2.1 reduce_sum.46
  (50 shorter events, 3.7 us)
Async XLA Ops:
  7.2 14.8 %copy-start = (bf16[128,1024]{1,0:T(8,128)(2,1)S(1)}, bf16[128,1024]{1,0:T(8,128)(2,1)}, u32[]{:S(2)}) copy-start(bf16[128,1024]{1,0:T(8,128)(2,1)} %param.7) | copy-start | bytes 786436
  7.2 8.8 %copy-start.5 = (f32[128,2]{0,1:T(2,128)S(1)}, f32[128,2]{0,1:T(2,128)}, u32[]{:S(2)}) copy-start(f32[128,2]{0,1:T(2,128)} %param.9) | copy-start | bytes 3076
  21.9 5.4 %copy-start.1 = (bf16[1024,1024]{1,0:T(8,128)(2,1)S(1)}, bf16[1024,1024]{1,0:T(8,128)(2,1)}, u32[]{:S(2)}) copy-start(bf16[1024,1024]{1,0:T(8,128)(2,1)} %gather_fusion.1) | copy-start | bytes 6291460
  31.5 10.0 %copy-start.2 = (bf16[1,32,384]{2,1,0:T(8,128)(2,1)S(1)}, bf16[1,32,384]{2,1,0:T(8,128)(2,1)}, u32[]{:S(2)}) copy-start(bf16[1,32,384]{2,1,0:T(8,128)(2,1)} %param.13) | copy-start | bytes 73732
  31.5 10.0 %copy-start.3 = (bf16[1,32,384]{2,1,0:T(8,128)(2,1)S(1)}, bf16[1,32,384]{2,1,0:T(8,128)(2,1)}, u32[]{:S(2)}) copy-start(bf16[1,32,384]{2,1,0:T(8,128)(2,1)} %param.12) | copy-start | bytes 73732
  31.5 10.0 %copy-start.4 = (bf16[1,32,384]{2,1,0:T(8,128)(2,1)S(1)}, bf16[1,32,384]{2,1,0:T(8,128)(2,1)}, u32[]{:S(2)}) copy-start(bf16[1,32,384]{2,1,0:T(8,128)(2,1)} %param.11) | copy-start | bytes 73732
  31.5 104.2 %all-to-all-start = ((bf16[16,64,2048]{2,1,0:T(8,128)(2,1)}), bf16[16,64,2048]{2,1,0:T(8,128)(2,1)}, u32[]{:S(2)}, u32[]{:S(2)}) async-start(bf16[16,64,2048]{2,1,0:T(8,128)(2,1)} %pad_maximum_fusion), calls=%async_computation | async-start | bytes 8388608 | tf_op jit(solution)/shard_map/all_to_all | solution.py:32
  41.3 92.9 %all-gather.2.cloned.1.call-start = ((), (), s32[]{:S(2)}) async-start(), calls=%async_computation.3 | async-start | bytes 2433024 | tf_op jit(solution)/shard_map/all_gather | solution.py:55
  135.8 2.9 copy-start.6
  156.7 160.2 %all-to-all-start.1 = ((bf16[16,64,2048]{2,1,0:T(8,128)(2,1)}), bf16[16,64,2048]{2,1,0:T(8,128)(2,1)}, u32[]{:S(2)}, u32[]{:S(2)}) async-start(bf16[16,64,2048]{2,1,0:T(8,128)(2,1)} %bitcast.29), calls=%async_computation.1 | async-start | bytes 8388608 | tf_op jit(solution)/shard_map/all_to_all | solution.py:32
  166.3 149.1 %reduce-scatter.2.cloned.1.call-start = ((), (), s32[]{:S(2)}) async-start(), calls=%async_computation.4 | async-start | bytes 3244032 | tf_op jit(solution)/shard_map/reduce_scatter | solution.py:97
Sparse Core Ops, SparseCore 0:
  44.9 89.3 all-gather.1
  171.9 143.4 reduce-scatter.1

commit v2 on v1

--- a/solution.py
+++ b/solution.py
@@ -1,7 +1,13 @@
 import jax
 import jax.numpy as jnp
 from jax import lax
+from jax.sharding import Mesh
 from jax.sharding import PartitionSpec as P
+
+DP_AXES = ("y", "xl", "c")
+CHIP_AXES = ("y", "xl")
+EXPERT_AXES = ("xh", "z")
+TOKEN_AXES = DP_AXES + EXPERT_AXES
 
 
 def expert_forward(input_rows, gate_full, up_full, down_full):
@@ -29,7 +35,7 @@
 
 
 def trade_rows(buffer):
-    return lax.all_to_all(buffer, "expert", split_axis=0, concat_axis=0, tiled=True)
+    return lax.all_to_all(buffer, EXPERT_AXES, split_axis=0, concat_axis=0, tiled=True)
 
 
 def pick_slots(routing, expert_total):
@@ -48,11 +54,14 @@
     pick_total = tok_count * top_count
     feature_total = tokens.shape[1]
     hidden_total = gate_weight.shape[2]
-    expert_total = lax.axis_size("expert")
-    group_total = lax.axis_size("dp")
+    expert_total = lax.axis_size(EXPERT_AXES)
+    group_total = lax.axis_size(DP_AXES)
+    core_total = lax.axis_size("c")
     capacity = max(tok_count // 2, top_count * tok_count // expert_total + tok_count // 4)
     local_weights = jnp.concatenate([gate_weight[0], up_weight[0], down_weight[0]], axis=1)
-    full_weights = lax.all_gather(local_weights, "dp", axis=0, tiled=True)
+    chip_weights = lax.all_gather(local_weights, CHIP_AXES, axis=0, tiled=False)
+    both_weights = lax.all_gather(chip_weights, "c", axis=0, tiled=False)
+    full_weights = jnp.swapaxes(both_weights, 0, 1).reshape(-1, local_weights.shape[1])
     gate_full = full_weights[:, :hidden_total]
     up_full = full_weights[:, hidden_total : 2 * hidden_total]
     down_full = full_weights[:, 2 * hidden_total :]
@@ -94,7 +103,18 @@
     piece = lax.dot_general(
         arrived, deltas, (((0,), (0,)), ((), ())), preferred_element_type=jnp.float32
     )
-    summed = lax.psum_scatter(piece, "dp", scatter_dimension=0, tiled=True) / group_total
+    slice_rows = gate_weight.shape[1]
+    by_core = jnp.swapaxes(
+        piece.reshape(group_total // core_total, core_total, slice_rows, 2 * hidden_total), 0, 1
+    )
+    core_summed = lax.psum_scatter(by_core, "c", scatter_dimension=0, tiled=True)
+    summed = lax.psum_scatter(
+        core_summed.reshape(group_total // core_total, slice_rows, 2 * hidden_total),
+        CHIP_AXES,
+        scatter_dimension=0,
+        tiled=True,
+    )
+    summed = summed.reshape(slice_rows, 2 * hidden_total) / group_total
     back = jnp.concatenate([results, input_grads], axis=1)
     returned = trade_rows(back.reshape(expert_total, capacity, 2 * feature_total)).reshape(
         expert_total * capacity, 2 * feature_total
@@ -114,25 +134,31 @@
 
 
 def solution(mesh):
+    dp_size = mesh.shape["dp"]
+    expert_size = mesh.shape["expert"]
+    fine = Mesh(
+        mesh.devices.reshape(dp_size // 4, 2, 2, 2, expert_size // 2),
+        DP_AXES + EXPERT_AXES,
+    )
     placed = (
-        P(("dp", "expert"), None),
-        P(("dp", "expert"), None),
-        P(("dp", "expert"), None),
-        P(("dp", "expert"), None),
-        P("expert", "dp", None),
-        P("expert", "dp", None),
-        P("expert", "dp", None),
+        P(TOKEN_AXES, None),
+        P(TOKEN_AXES, None),
+        P(TOKEN_AXES, None),
+        P(TOKEN_AXES, None),
+        P(EXPERT_AXES, DP_AXES, None),
+        P(EXPERT_AXES, DP_AXES, None),
+        P(EXPERT_AXES, DP_AXES, None),
     )
     return jax.shard_map(
         shards,
-        mesh=mesh,
+        mesh=fine,
         in_specs=placed,
         out_specs=(
-            P(("dp", "expert"), None),
-            P(("dp", "expert"), None),
-            P(("dp", "expert"), None),
-            P("expert", "dp", None),
-            P("expert", "dp", None),
+            P(TOKEN_AXES, None),
+            P(TOKEN_AXES, None),
+            P(TOKEN_AXES, None),
+            P(EXPERT_AXES, DP_AXES, None),
+            P(EXPERT_AXES, DP_AXES, None),
         ),
         check_vma=False,
     )

time: 336 us -> 337 us (level)
  the two profiles are of different devices: /device:TPU:260 before, /device:TPU:1 now
where the time goes in v2:
time: 337 us; the launch traced here: 336 us
  waiting for transfers between devices  223 us (66%)
  local copies, waits for them, and re-layouts  40 us (12%)
  starting transfers between devices  22.8 us (7%)
  matrix products  18.9 us (6%)
  other arithmetic  17.3 us (5%)
  between operations  14.1 us (4%)
    all_to_all x2, waiting for transfers between devices, trade_rows(): lax.all_to_all(buffer, EXPERT_AXES, split_axis=0, concat_axis=0, tiled=True)  96.5 us
    all_gather x1, waiting for transfers between devices, shards(): chip_weights = lax.all_gather(local_weights, CHIP_AXES, axis=0, tiled=False)  84.8 us
    all_gather x1, waiting for transfers between devices, shards(): both_weights = lax.all_gather(chip_weights, 'c', axis=0, tiled=False)  41 us
    all_to_all x2, starting transfers between devices, trade_rows(): lax.all_to_all(buffer, EXPERT_AXES, split_axis=0, concat_axis=0, tiled=True)  22.3 us
  transfers between devices with their start and end apart: 6, of which 3 were waited for; matrix products, arithmetic and copies ran while one was open for 10% of the time, Pallas kernels for 0%

profile of v2, /device:TPU:1, one launch (start us, length us, event | category | flops | bytes accessed | tf_op | source)
XLA Modules:
  0.0 335.8 jit_solution(12346286818321666135)
XLA Ops:
  7.2 0.8 copy.37
  8.3 0.7 broadcast_multiply_fusion
  11.2 1.4 scatter_custom_fusion
  12.6 1.4 scatter_custom_fusion.1
  14.0 1.2 mul.90
  15.3 0.7 mul.91
  16.6 5.3 %gather_fusion.1 = bf16[1024,1024]{1,0:T(8,128)(2,1)} fusion(bf16[256,1024]{1,0:T(8,128)(2,1)S(1)} %multiply_convert_fusion.3, s32[1024]{0:T(1024)S(1)} %fusion.19), kind=kCustom, calls=%fused_computation.1 | custom fusion | bytes 4198400 | tf_op jit(solution)/shard_map/jit(_take)/gather | solution.py:92
  21.9 5.4 %gather_fusion = bf16[1024,1024]{1,0:T(8,128)(2,1)} fusion(bf16[128,1024]{1,0:T(8,128)(2,1)S(1)} %copy-done, s32[1024]{0:T(1024)S(1)} %fusion.18), kind=kCustom, calls=%fused_computation | custom fusion | bytes 4198400 | tf_op jit(solution)/shard_map/jit(_take)/gather | solution.py:91
  27.3 1.8 broadcast_select_fusion
  29.1 2.5 pad_maximum_fusion
  31.6 13.6 %all-to-all-start = ((bf16[16,64,2048]{2,1,0:T(8,128)(2,1)}), bf16[16,64,2048]{2,1,0:T(8,128)(2,1)}, u32[]{:S(2)}, u32[]{:S(2)}) async-start(bf16[16,64,2048]{2,1,0:T(8,128)(2,1)} %pad_maximum_fusion), calls=%async_computation | async-start | bytes 8388608 | tf_op jit(solution)/shard_map/all_to_all | solution.py:38
  46.0 84.8 %all-gather.5.cloned.1.call-done = bf16[512,1152]{1,0:T(8,128)(2,1)} async-done(((bf16[32,1152]{1,0:T(8,128)(2,1)}), bf16[512,1152]{1,0:T(8,128)(2,1)}) %all-gather.5.cloned.1.call-update) | async-done | bytes 1179664 | tf_op jit(solution)/shard_map/all_gather | solution.py:62
  131.1 41.0 %all-gather.7.cloned.1.call-done = bf16[32,32,1152]{2,1,0:T(8,128)(2,1)} async-done(((bf16[16,32,1152]{2,1,0:T(8,128)(2,1)}), bf16[32,32,1152]{2,1,0:T(8,128)(2,1)}) %all-gather.7.cloned.1.call-update) | async-done | bytes 2359312 | tf_op jit(solution)/shard_map/all_gather | solution.py:63
  172.1 3.4 %copy.43 = bf16[16,2,32,1152]{3,2,1,0:T(8,128)(2,1)} copy(bf16[16,2,32,1152]{3,2,0,1:T(8,128)(2,1)} %bitcast.51) | data formatting | bytes 4718592 | tf_op jit(solution)/shard_map/transpose | solution.py:64
  175.5 2.9 fusion.4
  178.5 2.6 fusion
  181.1 4.4 %multiply_convert_fusion.1 = (bf16[1024,384]{0,1:T(8,128)(2,1)S(1)}, bf16[1024,384]{0,1:T(8,128)(2,1)S(1)}, f32[1024,384]{0,1:T(8,128)}) fusion(f32[1024,384]{0,1:T(8,128)S(1)} %fusion, f32[1024,384]{0,1:T(8,128)S(1)} %fusion.4, bf16[1024,1152]{1,0:T(8,128)(2,1)S(1)} %bitcast.49, bf16[1024,2048]{1,0:T(8,128)(2,1)} %bitcast.5), kind=kOutput, calls=%fused_computation.23 | convolution fusion | flops 810418176 | bytes 9175040 | tf_op jit(solution)/shard_map/dot_general | solution.py:14
  185.5 4.0 %fusion.2 = f32[1024,768]{1,0:T(8,128)S(1)} fusion(bf16[1024,2048]{1,0:T(8,128)(2,1)} %bitcast.5, bf16[1024,384]{0,1:T(8,128)(2,1)S(1)} %get-tuple-element.21, bf16[1024,384]{0,1:T(8,128)(2,1)S(1)} %get-tuple-element.20), kind=kOutput, calls=%fused_computation.14 | convolution fusion | flops 1613758464 | bytes 6815744 | tf_op jit(solution)/shard_map/dot_general | solution.py:103
  189.5 1.8 copy.50
  191.4 3.2 convolution_convert_fusion
  194.7 1.8 convolution_convert_fusion.1
  196.5 2.4 pad_maximum_fusion.1
  198.9 6.6 %copy.44 = bf16[1024,2048]{1,0:T(8,128)(2,1)} copy(bf16[1024,2048]{0,1:T(8,128)(2,1)} %pad_maximum_fusion.1) | data formatting | bytes 8388608 | tf_op jit(solution)/shard_map/concatenate | solution.py:118
  205.5 8.7 %all-to-all-start.1 = ((bf16[16,64,2048]{2,1,0:T(8,128)(2,1)}), bf16[16,64,2048]{2,1,0:T(8,128)(2,1)}, u32[]{:S(2)}, u32[]{:S(2)}) async-start(bf16[16,64,2048]{2,1,0:T(8,128)(2,1)} %bitcast.41), calls=%async_computation.1 | async-start | bytes 8388608 | tf_op jit(solution)/shard_map/all_to_all | solution.py:38
  214.8 96.5 %all-to-all-done.1 = bf16[16,64,2048]{2,1,0:T(8,128)(2,1)} async-done(((bf16[16,64,2048]{2,1,0:T(8,128)(2,1)}), bf16[16,64,2048]{2,1,0:T(8,128)(2,1)}, u32[]{:S(2)}, u32[]{:S(2)}) %all-to-all-start.1) | async-done | bytes 4194336 | tf_op jit(solution)/shard_map/all_to_all | solution.py:38
  311.2 5.1 %gather_fusion.2 = bf16[256,2048]{1,0:T(8,128)(2,1)S(1)} fusion(bf16[1024,2048]{1,0:T(8,128)(2,1)} %bitcast.14, s32[1024]{0:T(1024)S(1)} %pad_clamp_fusion), kind=kCustom, calls=%fused_computation.2 | custom fusion | bytes 2098176 | tf_op jit(solution)/shard_map/jit(_take)/gather | solution.py:122
  316.5 1.3 fusion.27
  317.8 1.8 reshape.149
  319.6 2.0 reshape.146
  322.6 3.0 reduce_sum.46
  325.6 2.1 multiply_reduce_fusion.1
  327.7 0.9 multiply_bitcast_fusion
  (68 shorter events, 6.3 us)
Async XLA Ops:
  7.2 14.7 %copy-start = (bf16[128,1024]{1,0:T(8,128)(2,1)S(1)}, bf16[128,1024]{1,0:T(8,128)(2,1)}, u32[]{:S(2)}) copy-start(bf16[128,1024]{1,0:T(8,128)(2,1)} %param.7) | copy-start | bytes 786436
  7.2 8.8 %copy-start.7 = (f32[128,2]{0,1:T(2,128)S(1)}, f32[128,2]{0,1:T(2,128)}, u32[]{:S(2)}) copy-start(f32[128,2]{0,1:T(2,128)} %param.9) | copy-start | bytes 3076
  21.9 5.4 %copy-start.1 = (bf16[1024,1024]{1,0:T(8,128)(2,1)S(1)}, bf16[1024,1024]{1,0:T(8,128)(2,1)}, u32[]{:S(2)}) copy-start(bf16[1024,1024]{1,0:T(8,128)(2,1)} %gather_fusion.1) | copy-start | bytes 6291460
  31.6 13.7 %copy-start.4 = (bf16[1,32,384]{2,1,0:T(8,128)(2,1)S(1)}, bf16[1,32,384]{2,1,0:T(8,128)(2,1)}, u32[]{:S(2)}) copy-start(bf16[1,32,384]{2,1,0:T(8,128)(2,1)} %param.13) | copy-start | bytes 73732
  31.6 13.7 %copy-start.5 = (bf16[1,32,384]{2,1,0:T(8,128)(2,1)S(1)}, bf16[1,32,384]{2,1,0:T(8,128)(2,1)}, u32[]{:S(2)}) copy-start(bf16[1,32,384]{2,1,0:T(8,128)(2,1)} %param.12) | copy-start | bytes 73732
  31.6 13.7 %copy-start.6 = (bf16[1,32,384]{2,1,0:T(8,128)(2,1)S(1)}, bf16[1,32,384]{2,1,0:T(8,128)(2,1)}, u32[]{:S(2)}) copy-start(bf16[1,32,384]{2,1,0:T(8,128)(2,1)} %param.11) | copy-start | bytes 73732
  31.6 143.9 %all-to-all-start = ((bf16[16,64,2048]{2,1,0:T(8,128)(2,1)}), bf16[16,64,2048]{2,1,0:T(8,128)(2,1)}, u32[]{:S(2)}, u32[]{:S(2)}) async-start(bf16[16,64,2048]{2,1,0:T(8,128)(2,1)} %pad_maximum_fusion), calls=%async_computation | async-start | bytes 8388608 | tf_op jit(solution)/shard_map/all_to_all | solution.py:38
  45.2 85.6 %all-gather.5.cloned.1.call-start = ((), (), s32[]{:S(2)}) async-start(), calls=%async_computation.6 | async-start | bytes 1253376 | tf_op jit(solution)/shard_map/all_gather | solution.py:62
  46.0 126.1 %all-gather.7.cloned.1.call-start = ((), (), s32[]{:S(2)}) async-start(), calls=%async_computation.7 | async-start | bytes 3538944 | tf_op jit(solution)/shard_map/all_gather | solution.py:63
  130.9 83.5 %reduce-scatter.3.cloned.1.call-start = ((), (), s32[]{:S(2)}) async-start(), calls=%async_computation.4 | async-start | bytes 4718592 | tf_op jit(solution)/shard_map/reduce_scatter | solution.py:110
  175.5 2.9 copy-start.2
  185.5 4.0 %copy-start.8 = (bf16[1024,384]{0,1:T(8,128)(2,1)}, bf16[1024,384]{0,1:T(8,128)(2,1)S(1)}, u32[]{:S(2)}) copy-start(bf16[1024,384]{0,1:T(8,128)(2,1)S(1)} %get-tuple-element.20) | copy-start | bytes 2359300
  185.5 4.0 %copy-start.10 = (bf16[1024,384]{0,1:T(8,128)(2,1)}, bf16[1024,384]{0,1:T(8,128)(2,1)S(1)}, u32[]{:S(2)}) copy-start(bf16[1024,384]{0,1:T(8,128)(2,1)S(1)} %get-tuple-element.21) | copy-start | bytes 2359300
  191.4 3.2 copy-start.3
  191.4 3.2 copy-start.9
  191.4 3.2 copy-start.11
  205.5 105.8 %all-to-all-start.1 = ((bf16[16,64,2048]{2,1,0:T(8,128)(2,1)}), bf16[16,64,2048]{2,1,0:T(8,128)(2,1)}, u32[]{:S(2)}, u32[]{:S(2)}) async-start(bf16[16,64,2048]{2,1,0:T(8,128)(2,1)} %bitcast.41), calls=%async_computation.1 | async-start | bytes 8388608 | tf_op jit(solution)/shard_map/all_to_all | solution.py:38
  214.1 113.6 %reduce-scatter.5.cloned.1.call-start = ((), (), s32[]{:S(2)}) async-start(), calls=%async_computation.5 | async-start | bytes 1671168 | tf_op jit(solution)/shard_map/reduce_scatter | solution.py:111
Sparse Core Ops, SparseCore 0:
  48.7 82.1 all-gather.4
  133.0 39.1 all-gather.6
  191.5 19.9 reduce-scatter.2
  217.7 83.6 reduce-scatter.4

commit v3 on v2

--- a/solution.py
+++ b/solution.py
@@ -59,9 +59,7 @@
     core_total = lax.axis_size("c")
     capacity = max(tok_count // 2, top_count * tok_count // expert_total + tok_count // 4)
     local_weights = jnp.concatenate([gate_weight[0], up_weight[0], down_weight[0]], axis=1)
-    chip_weights = lax.all_gather(local_weights, CHIP_AXES, axis=0, tiled=False)
-    both_weights = lax.all_gather(chip_weights, "c", axis=0, tiled=False)
-    full_weights = jnp.swapaxes(both_weights, 0, 1).reshape(-1, local_weights.shape[1])
+    full_weights = lax.all_gather(local_weights, DP_AXES, axis=0, tiled=True)
     gate_full = full_weights[:, :hidden_total]
     up_full = full_weights[:, hidden_total : 2 * hidden_total]
     down_full = full_weights[:, 2 * hidden_total :]

time: 337 us -> 301 us (0.89)
  waiting for transfers between devices: 223 us -> 191 us
  local copies, waits for them, and re-layouts: 40 us -> 36.6 us
    all_gather x2 -> x1, waiting for transfers between devices: 126 us -> 75.5 us  [shards(): full_weights = lax.all_gather(local_weights, DP_AXES, axis=0, tiled=True)]
    all_to_all x2, waiting for transfers between devices: 96.5 us -> 115 us  [trade_rows(): lax.all_to_all(buffer, EXPERT_AXES, split_axis=0, concat_axis=0, tiled=True)]
    transpose x1 -> x0, local copies, waits for them, and re-layouts: 3.39 us -> none  [shards(): jnp.swapaxes(both_weights, 0, 1).reshape(-1, local_weights.shape[1])]
  transfers between devices with their start and end apart: 6 -> 5, of which waited for: 3 -> 3; matrix products, arithmetic and copies ran while one was open for 10% -> 10% of each run, Pallas kernels for 0% -> 0%
where the time goes in v3:
time: 301 us; the launch traced here: 300 us
  waiting for transfers between devices  191 us (63%)
  local copies, waits for them, and re-layouts  36.6 us (12%)
  starting transfers between devices  21.9 us (7%)
  matrix products  18.9 us (6%)
  other arithmetic  17.3 us (6%)
  between operations  14.1 us (5%)
    all_to_all x2, waiting for transfers between devices, trade_rows(): lax.all_to_all(buffer, EXPERT_AXES, split_axis=0, concat_axis=0, tiled=True)  115 us
    all_gather x1, waiting for transfers between devices, shards(): full_weights = lax.all_gather(local_weights, DP_AXES, axis=0, tiled=True)  75.5 us
    all_to_all x2, starting transfers between devices, trade_rows(): lax.all_to_all(buffer, EXPERT_AXES, split_axis=0, concat_axis=0, tiled=True)  21.4 us
    concatenate x1, local copies, waits for them, and re-layouts, shards(): back = jnp.concatenate([results, input_grads], axis=1)  6.57 us
  transfers between devices with their start and end apart: 5, of which 3 were waited for; matrix products, arithmetic and copies ran while one was open for 10% of the time, Pallas kernels for 0%

profile of v3, /device:TPU:1, one launch (start us, length us, event | category | flops | bytes accessed | tf_op | source)
XLA Modules:
  0.0 299.9 jit_solution(11957078927160275018)
XLA Ops:
  7.2 0.8 copy.16
  8.3 0.7 broadcast_multiply_fusion
  9.0 0.7 broadcast_compare_fusion
  11.2 1.4 scatter_custom_fusion
  12.6 1.4 scatter_custom_fusion.1
  14.0 1.2 mul.90
  15.3 0.7 mul.91
  16.6 5.4 %gather_fusion.1 = bf16[1024,1024]{1,0:T(8,128)(2,1)} fusion(bf16[256,1024]{1,0:T(8,128)(2,1)S(1)} %multiply_convert_fusion.3, s32[1024]{0:T(1024)S(1)} %fusion.19), kind=kCustom, calls=%fused_computation.1 | custom fusion | bytes 4198400 | tf_op jit(solution)/shard_map/jit(_take)/gather | solution.py:90
  21.9 5.4 %gather_fusion = bf16[1024,1024]{1,0:T(8,128)(2,1)} fusion(bf16[128,1024]{1,0:T(8,128)(2,1)S(1)} %copy-done, s32[1024]{0:T(1024)S(1)} %fusion.18), kind=kCustom, calls=%fused_computation | custom fusion | bytes 4198400 | tf_op jit(solution)/shard_map/jit(_take)/gather | solution.py:89
  27.3 1.8 broadcast_select_fusion
  29.1 2.5 pad_maximum_fusion
  31.6 13.6 %all-to-all-start = ((bf16[16,64,2048]{2,1,0:T(8,128)(2,1)}), bf16[16,64,2048]{2,1,0:T(8,128)(2,1)}, u32[]{:S(2)}, u32[]{:S(2)}) async-start(bf16[16,64,2048]{2,1,0:T(8,128)(2,1)} %pad_maximum_fusion), calls=%async_computation | async-start | bytes 8388608 | tf_op jit(solution)/shard_map/all_to_all | solution.py:38
  46.2 75.5 %all-gather.2.cloned.1.call-done = bf16[1024,1152]{1,0:T(8,128)(2,1)} async-done(((bf16[32,1152]{1,0:T(8,128)(2,1)}), bf16[1024,1152]{1,0:T(8,128)(2,1)}) %all-gather.2.cloned.1.call-update) | async-done | bytes 2359312 | tf_op jit(solution)/shard_map/all_gather | solution.py:62
  121.7 19.7 %all-to-all-done = bf16[16,64,2048]{2,1,0:T(8,128)(2,1)} async-done(((bf16[16,64,2048]{2,1,0:T(8,128)(2,1)}), bf16[16,64,2048]{2,1,0:T(8,128)(2,1)}, u32[]{:S(2)}, u32[]{:S(2)}) %all-to-all-start) | async-done | bytes 4194336 | tf_op jit(solution)/shard_map/all_to_all | solution.py:38
  141.5 2.9 fusion.4
  144.4 2.6 fusion
  147.0 4.4 %multiply_convert_fusion.1 = (bf16[1024,384]{0,1:T(8,128)(2,1)S(1)}, bf16[1024,384]{0,1:T(8,128)(2,1)S(1)}, f32[1024,384]{0,1:T(8,128)}) fusion(f32[1024,384]{0,1:T(8,128)S(1)} %fusion, f32[1024,384]{0,1:T(8,128)S(1)} %fusion.4, bf16[1024,1152]{1,0:T(8,128)(2,1)S(1)} %copy-done.6, bf16[1024,2048]{1,0:T(8,128)(2,1)} %bitcast.5), kind=kOutput, calls=%fused_computation.23 | convolution fusion | flops 810418176 | bytes 9175040 | tf_op jit(solution)/shard_map/dot_general | solution.py:14
  151.4 4.0 %fusion.2 = f32[1024,768]{1,0:T(8,128)S(1)} fusion(bf16[1024,2048]{1,0:T(8,128)(2,1)} %bitcast.5, bf16[1024,384]{0,1:T(8,128)(2,1)S(1)} %get-tuple-element.11, bf16[1024,384]{0,1:T(8,128)(2,1)S(1)} %get-tuple-element.10), kind=kOutput, calls=%fused_computation.14 | convolution fusion | flops 1613758464 | bytes 6815744 | tf_op jit(solution)/shard_map/dot_general | solution.py:101
  155.5 1.8 copy.28
  157.4 3.2 %convolution_convert_fusion = bf16[1024,1024]{0,1:T(8,128)(2,1)S(1)} fusion(f32[1024,384]{0,1:T(8,128)S(1)} %fusion.4, bf16[1024,1152]{1,0:T(8,128)(2,1)} %all-gather.2.cloned.1.call-done, f32[1024,384]{0,1:T(8,128)} %get-tuple-element.16), kind=kOutput, calls=%fused_computation.12 | convolution fusion | flops 808714240 | bytes 6029312 | tf_op jit(solution)/shard_map/dot_general | solution.py:17
  160.6 1.8 convolution_convert_fusion.1
  162.4 2.4 pad_maximum_fusion.1
  164.8 6.6 %copy.22 = bf16[1024,2048]{1,0:T(8,128)(2,1)} copy(bf16[1024,2048]{0,1:T(8,128)(2,1)} %pad_maximum_fusion.1) | data formatting | bytes 8388608 | tf_op jit(solution)/shard_map/concatenate | solution.py:116
  171.4 7.8 %all-to-all-start.1 = ((bf16[16,64,2048]{2,1,0:T(8,128)(2,1)}), bf16[16,64,2048]{2,1,0:T(8,128)(2,1)}, u32[]{:S(2)}, u32[]{:S(2)}) async-start(bf16[16,64,2048]{2,1,0:T(8,128)(2,1)} %bitcast.36), calls=%async_computation.1 | async-start | bytes 8388608 | tf_op jit(solution)/shard_map/all_to_all | solution.py:38
  179.9 95.4 %all-to-all-done.1 = bf16[16,64,2048]{2,1,0:T(8,128)(2,1)} async-done(((bf16[16,64,2048]{2,1,0:T(8,128)(2,1)}), bf16[16,64,2048]{2,1,0:T(8,128)(2,1)}, u32[]{:S(2)}, u32[]{:S(2)}) %all-to-all-start.1) | async-done | bytes 4194336 | tf_op jit(solution)/shard_map/all_to_all | solution.py:38
  275.4 5.1 %gather_fusion.2 = bf16[256,2048]{1,0:T(8,128)(2,1)S(1)} fusion(bf16[1024,2048]{1,0:T(8,128)(2,1)} %bitcast.10, s32[1024]{0:T(1024)S(1)} %pad_clamp_fusion), kind=kCustom, calls=%fused_computation.2 | custom fusion | bytes 2098176 | tf_op jit(solution)/shard_map/jit(_take)/gather | solution.py:120
  280.6 1.3 fusion.27
  281.9 1.8 reshape.145
  283.7 2.0 reshape.142
  286.7 3.0 %reduce_sum.46 = bf16[128,1024]{1,0:T(8,128)(2,1)} reduce(bf16[128,2,1024]{2,1,0:T(2,128)(2,1)} %reshape.142, bf16[]{:T(256)} %constant.78.clone.1), dimensions={1}, to_apply=%region_6.7 | reduce | flops 131072 | bytes 786434 | tf_op jit(solution)/shard_map/reduce_sum | solution.py:128
  289.8 2.1 multiply_reduce_fusion.1
  291.8 0.9 multiply_bitcast_fusion
  (64 shorter events, 5.8 us)
Async XLA Ops:
  7.2 14.8 %copy-start = (bf16[128,1024]{1,0:T(8,128)(2,1)S(1)}, bf16[128,1024]{1,0:T(8,128)(2,1)}, u32[]{:S(2)}) copy-start(bf16[128,1024]{1,0:T(8,128)(2,1)} %param.7) | copy-start | bytes 786436
  7.2 8.8 %copy-start.5 = (f32[128,2]{0,1:T(2,128)S(1)}, f32[128,2]{0,1:T(2,128)}, u32[]{:S(2)}) copy-start(f32[128,2]{0,1:T(2,128)} %param.9) | copy-start | bytes 3076
  21.9 5.4 %copy-start.1 = (bf16[1024,1024]{1,0:T(8,128)(2,1)S(1)}, bf16[1024,1024]{1,0:T(8,128)(2,1)}, u32[]{:S(2)}) copy-start(bf16[1024,1024]{1,0:T(8,128)(2,1)} %gather_fusion.1) | copy-start | bytes 6291460
  31.6 13.7 %copy-start.2 = (bf16[1,32,384]{2,1,0:T(8,128)(2,1)S(1)}, bf16[1,32,384]{2,1,0:T(8,128)(2,1)}, u32[]{:S(2)}) copy-start(bf16[1,32,384]{2,1,0:T(8,128)(2,1)} %param.13) | copy-start | bytes 73732
  31.6 13.7 %copy-start.3 = (bf16[1,32,384]{2,1,0:T(8,128)(2,1)S(1)}, bf16[1,32,384]{2,1,0:T(8,128)(2,1)}, u32[]{:S(2)}) copy-start(bf16[1,32,384]{2,1,0:T(8,128)(2,1)} %param.12) | copy-start | bytes 73732
  31.6 13.7 %copy-start.4 = (bf16[1,32,384]{2,1,0:T(8,128)(2,1)S(1)}, bf16[1,32,384]{2,1,0:T(8,128)(2,1)}, u32[]{:S(2)}) copy-start(bf16[1,32,384]{2,1,0:T(8,128)(2,1)} %param.11) | copy-start | bytes 73732
  31.6 109.8 %all-to-all-start = ((bf16[16,64,2048]{2,1,0:T(8,128)(2,1)}), bf16[16,64,2048]{2,1,0:T(8,128)(2,1)}, u32[]{:S(2)}, u32[]{:S(2)}) async-start(bf16[16,64,2048]{2,1,0:T(8,128)(2,1)} %pad_maximum_fusion), calls=%async_computation | async-start | bytes 8388608 | tf_op jit(solution)/shard_map/all_to_all | solution.py:38
  45.2 76.5 %all-gather.2.cloned.1.call-start = ((), (), s32[]{:S(2)}) async-start(), calls=%async_computation.4 | async-start | bytes 2433024 | tf_op jit(solution)/shard_map/all_gather | solution.py:62
  46.0 133.5 %reduce-scatter.3.cloned.1.call-start = ((), (), s32[]{:S(2)}) async-start(), calls=%async_computation.5 | async-start | bytes 4718592 | tf_op jit(solution)/shard_map/reduce_scatter | solution.py:108
  141.5 2.9 copy-start.6
  151.4 4.0 %copy-start.8 = (bf16[1024,384]{0,1:T(8,128)(2,1)}, bf16[1024,384]{0,1:T(8,128)(2,1)S(1)}, u32[]{:S(2)}) copy-start(bf16[1024,384]{0,1:T(8,128)(2,1)S(1)} %get-tuple-element.10) | copy-start | bytes 2359300
  151.4 4.0 %copy-start.10 = (bf16[1024,384]{0,1:T(8,128)(2,1)}, bf16[1024,384]{0,1:T(8,128)(2,1)S(1)}, u32[]{:S(2)}) copy-start(bf16[1024,384]{0,1:T(8,128)(2,1)S(1)} %get-tuple-element.11) | copy-start | bytes 2359300
  157.3 3.2 %copy-start.7 = (bf16[1024,1152]{1,0:T(8,128)(2,1)S(1)}, bf16[1024,1152]{1,0:T(8,128)(2,1)}, u32[]{:S(2)}) copy-start(bf16[1024,1152]{1,0:T(8,128)(2,1)} %all-gather.2.cloned.1.call-done) | copy-start | bytes 7077892
  157.3 3.2 %copy-start.9 = (bf16[1024,384]{0,1:T(8,128)(2,1)S(1)}, bf16[1024,384]{0,1:T(8,128)(2,1)}, u32[]{:S(2)}) copy-start(bf16[1024,384]{0,1:T(8,128)(2,1)} %copy-done.8) | copy-start | bytes 2359300
  157.4 3.2 %copy-start.11 = (bf16[1024,384]{0,1:T(8,128)(2,1)S(1)}, bf16[1024,384]{0,1:T(8,128)(2,1)}, u32[]{:S(2)}) copy-start(bf16[1024,384]{0,1:T(8,128)(2,1)} %copy-done.10) | copy-start | bytes 2359300
  171.4 104.0 %all-to-all-start.1 = ((bf16[16,64,2048]{2,1,0:T(8,128)(2,1)}), bf16[16,64,2048]{2,1,0:T(8,128)(2,1)}, u32[]{:S(2)}, u32[]{:S(2)}) async-start(bf16[16,64,2048]{2,1,0:T(8,128)(2,1)} %bitcast.36), calls=%async_computation.1 | async-start | bytes 8388608 | tf_op jit(solution)/shard_map/all_to_all | solution.py:38
  179.2 112.7 %reduce-scatter.5.cloned.1.call-start = ((), (), s32[]{:S(2)}) async-start(), calls=%async_computation.6 | async-start | bytes 1671168 | tf_op jit(solution)/shard_map/reduce_scatter | solution.py:109
Sparse Core Ops, SparseCore 0:
  48.8 72.8 all-gather.1
  157.5 19.8 reduce-scatter.2
  183.1 84.6 reduce-scatter.4

commit v4 on v3

--- a/solution.py
+++ b/solution.py
@@ -84,23 +84,38 @@
         .at[slot_index]
         .set(pick_index, mode="drop")
     )
-    sending = jnp.concatenate(
-        [
-            jnp.take(tokens, token_source, axis=0, mode="fill", fill_value=0),
-            jnp.take(pick_cotangent, pick_source, axis=0, mode="fill", fill_value=0),
-        ],
-        axis=1,
-    )
-    arrived_both = trade_rows(
-        sending.reshape(expert_total, capacity, 2 * feature_total)
-    ).reshape(expert_total * capacity, 2 * feature_total)
-    arrived = arrived_both[:, :feature_total]
-    cot_arrived = arrived_both[:, feature_total:]
-    results, gate_pre, up_pre = expert_forward(arrived, gate_full, up_full, down_full)
-    input_grads, deltas = expert_backward(cot_arrived, gate_pre, up_pre, stacked, down_full)
-    piece = lax.dot_general(
-        arrived, deltas, (((0,), (0,)), ((), ())), preferred_element_type=jnp.float32
-    )
+    chunk_total = 2
+    chunk_rows = capacity // chunk_total
+    token_slots = token_source.reshape(expert_total, capacity)
+    pick_slots_of = pick_source.reshape(expert_total, capacity)
+    returned_parts = []
+    pieces = []
+    for chunk in range(chunk_total):
+        window = slice(chunk * chunk_rows, (chunk + 1) * chunk_rows)
+        sending = jnp.concatenate(
+            [
+                jnp.take(tokens, token_slots[:, window], axis=0, mode="fill", fill_value=0),
+                jnp.take(pick_cotangent, pick_slots_of[:, window], axis=0, mode="fill", fill_value=0),
+            ],
+            axis=2,
+        )
+        arrived_both = trade_rows(sending).reshape(expert_total * chunk_rows, 2 * feature_total)
+        arrived = arrived_both[:, :feature_total]
+        cot_arrived = arrived_both[:, feature_total:]
+        results, gate_pre, up_pre = expert_forward(arrived, gate_full, up_full, down_full)
+        input_grads, deltas = expert_backward(cot_arrived, gate_pre, up_pre, stacked, down_full)
+        pieces.append(
+            lax.dot_general(
+                arrived, deltas, (((0,), (0,)), ((), ())), preferred_element_type=jnp.float32
+            )
+        )
+        back = jnp.concatenate([results, input_grads], axis=1)
+        returned_parts.append(
+            trade_rows(back.reshape(expert_total, chunk_rows, 2 * feature_total))
+        )
+    piece = pieces[0]
+    for extra in pieces[1:]:
+        piece = piece + extra
     slice_rows = gate_weight.shape[1]
     by_core = jnp.swapaxes(
         piece.reshape(group_total // core_total, core_total, slice_rows, 2 * hidden_total), 0, 1
@@ -113,8 +128,7 @@
         tiled=True,
     )
     summed = summed.reshape(slice_rows, 2 * hidden_total) / group_total
-    back = jnp.concatenate([results, input_grads], axis=1)
-    returned = trade_rows(back.reshape(expert_total, capacity, 2 * feature_total)).reshape(
+    returned = jnp.concatenate(returned_parts, axis=1).reshape(
         expert_total * capacity, 2 * feature_total
     )
     pick_both = jnp.take(returned, slot_index, axis=0, mode="fill", fill_value=0)

time: 301 us -> 324 us (1.076)
  the two profiles are of different devices: /device:TPU:1 before, /device:TPU:68 now
where the time goes in v4:
time: 324 us; the launch traced here: 323 us
  waiting for transfers between devices  191 us (59%)
  starting transfers between devices  38.1 us (12%)
  local copies, waits for them, and re-layouts  33.4 us (10%)
  other arithmetic  23.9 us (7%)
  matrix products  22.9 us (7%)
  between operations  14.2 us (4%)
    all_to_all x4, waiting for transfers between devices, trade_rows(): lax.all_to_all(buffer, EXPERT_AXES, split_axis=0, concat_axis=0, tiled=True)  149 us
    all_to_all x4, starting transfers between devices, trade_rows(): lax.all_to_all(buffer, EXPERT_AXES, split_axis=0, concat_axis=0, tiled=True)  37.6 us
    reduce_scatter x1, waiting for transfers between devices, shards(): lax.psum_scatter(core_summed.reshape(group_total // core_total, slice_row...  22.1 us
    all_gather x1, waiting for transfers between devices, shards(): full_weights = lax.all_gather(local_weights, DP_AXES, axis=0, tiled=True)  19.7 us
  transfers between devices with their start and end apart: 7, of which 6 were waited for; matrix products, arithmetic and copies ran while one was open for 14% of the time, Pallas kernels for 0%

profile of v4, /device:TPU:68, one launch (start us, length us, event | category | flops | bytes accessed | tf_op | source)
XLA Modules:
  0.0 323.2 jit_solution(13016801605720796413)
XLA Ops:
  17.0 2.1 gather_fusion.2
  19.1 2.8 gather_fusion.1
  23.3 1.5 pad_maximum_fusion.1
  24.8 12.5 %all-to-all-start = ((bf16[16,32,2048]{2,1,0:T(8,128)(2,1)}), bf16[16,32,2048]{2,1,0:T(8,128)(2,1)S(1)}, u32[]{:S(2)}, u32[]{:S(2)}) async-start(bf16[16,32,2048]{2,1,0:T(8,128)(2,1)} %pad_maximum_fusion.1), calls=%async_computation | async-start | bytes 4194304 | tf_op jit(solution)/shard_map/all_to_all | solution.py:38
  38.2 2.8 gather_fusion.4
  41.1 2.8 gather_fusion.3
  46.8 38.3 %all-to-all-done = bf16[16,32,2048]{2,1,0:T(8,128)(2,1)S(1)} async-done(((bf16[16,32,2048]{2,1,0:T(8,128)(2,1)}), bf16[16,32,2048]{2,1,0:T(8,128)(2,1)S(1)}, u32[]{:S(2)}, u32[]{:S(2)}) %all-to-all-start) | async-done | bytes 2097184 | tf_op jit(solution)/shard_map/all_to_all | solution.py:38
  85.1 8.4 %all-to-all-start.2 = ((bf16[16,32,2048]{2,1,0:T(8,128)(2,1)}), bf16[16,32,2048]{2,1,0:T(8,128)(2,1)}, u32[]{:S(2)}, u32[]{:S(2)}) async-start(bf16[16,32,2048]{2,1,0:T(8,128)(2,1)} %pad_maximum_fusion.3), calls=%async_computation.2 | async-start | bytes 4194304 | tf_op jit(solution)/shard_map/all_to_all | solution.py:38
  93.8 19.7 %all-gather.2.cloned.1.call-done = bf16[1024,1152]{1,0:T(8,128)(2,1)} async-done(((bf16[32,1152]{1,0:T(8,128)(2,1)}), bf16[1024,1152]{1,0:T(8,128)(2,1)}) %all-gather.2.cloned.1.call-update) | async-done | bytes 2359312 | tf_op jit(solution)/shard_map/all_gather | solution.py:62
  113.4 1.9 fusion.13
  116.0 1.8 multiply_convert_fusion.5
  118.7 2.3 fusion.11
  120.9 20.9 %all-to-all-done.2 = bf16[16,32,2048]{2,1,0:T(8,128)(2,1)} async-done(((bf16[16,32,2048]{2,1,0:T(8,128)(2,1)}), bf16[16,32,2048]{2,1,0:T(8,128)(2,1)}, u32[]{:S(2)}, u32[]{:S(2)}) %all-to-all-start.2) | async-done | bytes 2097184 | tf_op jit(solution)/shard_map/all_to_all | solution.py:38
  141.8 2.2 fusion.7
  144.0 2.1 fusion.2
  146.2 3.0 multiply_convert_fusion.2
  149.2 2.5 convolution_add_fusion
  151.7 2.0 copy.26
  159.3 8.5 %all-to-all-start.1 = ((bf16[16,32,2048]{2,1,0:T(8,128)(2,1)}), bf16[16,32,2048]{2,1,0:T(8,128)(2,1)S(1)}, u32[]{:S(2)}, u32[]{:S(2)}) async-start(bf16[16,32,2048]{2,1,0:T(8,128)(2,1)} %bitcast.9), calls=%async_computation.1 | async-start | bytes 4194304 | tf_op jit(solution)/shard_map/all_to_all | solution.py:38
  167.8 2.6 convolution_convert_fusion
  170.5 2.0 convolution_convert_fusion.2
  172.5 1.5 pad_maximum_fusion.4
  174.0 41.8 %all-to-all-done.1 = bf16[16,32,2048]{2,1,0:T(8,128)(2,1)S(1)} async-done(((bf16[16,32,2048]{2,1,0:T(8,128)(2,1)}), bf16[16,32,2048]{2,1,0:T(8,128)(2,1)S(1)}, u32[]{:S(2)}, u32[]{:S(2)}) %all-to-all-start.1) | async-done | bytes 2097184 | tf_op jit(solution)/shard_map/all_to_all | solution.py:38
  215.9 8.2 %all-to-all-start.3 = ((bf16[16,32,2048]{2,1,0:T(8,128)(2,1)}), bf16[16,32,2048]{2,1,0:T(8,128)(2,1)}, u32[]{:S(2)}, u32[]{:S(2)}) async-start(bf16[16,32,2048]{2,1,0:T(8,128)(2,1)} %bitcast.13), calls=%async_computation.3 | async-start | bytes 4194304 | tf_op jit(solution)/shard_map/all_to_all | solution.py:38
  224.9 47.5 %all-to-all-done.3 = bf16[16,32,2048]{2,1,0:T(8,128)(2,1)} async-done(((bf16[16,32,2048]{2,1,0:T(8,128)(2,1)}), bf16[16,32,2048]{2,1,0:T(8,128)(2,1)}, u32[]{:S(2)}, u32[]{:S(2)}) %all-to-all-start.3) | async-done | bytes 2097184 | tf_op jit(solution)/shard_map/all_to_all | solution.py:38
  272.3 4.2 %pad_maximum_fusion = bf16[16,64,2048]{2,1,0:T(8,128)(2,1)} fusion(bf16[16,32,2048]{2,1,0:T(8,128)(2,1)} %all-to-all-done.3, bf16[16,32,2048]{2,1,0:T(8,128)(2,1)S(1)} %all-to-all-done.1), kind=kLoop, calls=%fused_computation.7 | loop fusion | flops 8388608 | bytes 8388608 | tf_op jit(solution)/shard_map/concatenate | solution.py:131
  276.5 5.1 %gather_fusion = bf16[256,2048]{1,0:T(8,128)(2,1)S(1)} fusion(bf16[1024,2048]{1,0:T(8,128)(2,1)} %bitcast.40, s32[1024]{0:T(1024)S(1)} %pad_clamp_fusion), kind=kCustom, calls=%fused_computation.4 | custom fusion | bytes 2098176 | tf_op jit(solution)/shard_map/jit(_take)/gather | solution.py:134
  283.0 1.9 reshape.146
  285.0 2.0 reshape.143
  288.0 3.0 reduce_sum.46
  291.0 2.1 multiply_reduce_fusion.1
  293.1 22.1 %reduce-scatter.5.cloned.1.call-done = f32[1,32,768]{2,1,0:T(8,128)} async-done(((f32[16,32,768]{2,1,0:T(8,128)}), f32[1,32,768]{2,1,0:T(8,128)}) %reduce-scatter.5.cloned.1.call-update) | async-done | bytes 98320 | tf_op jit(solution)/shard_map/reduce_scatter | solution.py:124
  (115 shorter events, 27.0 us)
Async XLA Ops:
  7.2 11.9 %copy-start = (bf16[128,1024]{1,0:T(8,128)(2,1)S(1)}, bf16[128,1024]{1,0:T(8,128)(2,1)}, u32[]{:S(2)}) copy-start(bf16[128,1024]{1,0:T(8,128)(2,1)} %param.11) | copy-start | bytes 786436
  7.2 9.3 %copy-start.16 = (f32[128,2]{0,1:T(2,128)S(1)}, f32[128,2]{0,1:T(2,128)}, u32[]{:S(2)}) copy-start(f32[128,2]{0,1:T(2,128)} %param.13) | copy-start | bytes 3076
  16.5 2.6 copy-start.1
  24.8 12.6 %copy-start.13 = (bf16[1,32,384]{2,1,0:T(8,128)(2,1)S(1)}, bf16[1,32,384]{2,1,0:T(8,128)(2,1)}, u32[]{:S(2)}) copy-start(bf16[1,32,384]{2,1,0:T(8,128)(2,1)} %param.17) | copy-start | bytes 73732
  24.8 12.6 %copy-start.14 = (bf16[1,32,384]{2,1,0:T(8,128)(2,1)S(1)}, bf16[1,32,384]{2,1,0:T(8,128)(2,1)}, u32[]{:S(2)}) copy-start(bf16[1,32,384]{2,1,0:T(8,128)(2,1)} %param.16) | copy-start | bytes 73732
  24.8 12.6 %copy-start.15 = (bf16[1,32,384]{2,1,0:T(8,128)(2,1)S(1)}, bf16[1,32,384]{2,1,0:T(8,128)(2,1)}, u32[]{:S(2)}) copy-start(bf16[1,32,384]{2,1,0:T(8,128)(2,1)} %param.15) | copy-start | bytes 73732
  24.8 60.3 %all-to-all-start = ((bf16[16,32,2048]{2,1,0:T(8,128)(2,1)}), bf16[16,32,2048]{2,1,0:T(8,128)(2,1)S(1)}, u32[]{:S(2)}, u32[]{:S(2)}) async-start(bf16[16,32,2048]{2,1,0:T(8,128)(2,1)} %pad_maximum_fusion.1), calls=%async_computation | async-start | bytes 4194304 | tf_op jit(solution)/shard_map/all_to_all | solution.py:38
  37.4 76.0 %all-gather.2.cloned.1.call-start = ((), (), s32[]{:S(2)}) async-start(), calls=%async_computation.6 | async-start | bytes 2433024 | tf_op jit(solution)/shard_map/all_gather | solution.py:62
  41.1 2.8 copy-start.4
  85.1 30.8 %copy-start.3 = (bf16[16,32,2048]{2,1,0:T(8,128)(2,1)}, bf16[16,32,2048]{2,1,0:T(8,128)(2,1)S(1)}, u32[]{:S(2)}) copy-start(bf16[16,32,2048]{2,1,0:T(8,128)(2,1)S(1)} %all-to-all-done) | copy-start | bytes 6291460
  85.1 56.7 %all-to-all-start.2 = ((bf16[16,32,2048]{2,1,0:T(8,128)(2,1)}), bf16[16,32,2048]{2,1,0:T(8,128)(2,1)}, u32[]{:S(2)}, u32[]{:S(2)}) async-start(bf16[16,32,2048]{2,1,0:T(8,128)(2,1)} %pad_maximum_fusion.3), calls=%async_computation.2 | async-start | bytes 4194304 | tf_op jit(solution)/shard_map/all_to_all | solution.py:38
  93.5 130.9 %reduce-scatter.3.cloned.1.call-start = ((), (), s32[]{:S(2)}) async-start(), calls=%async_computation.7 | async-start | bytes 4718592 | tf_op jit(solution)/shard_map/reduce_scatter | solution.py:123
  113.4 1.9 copy-start.17
  115.3 2.5 copy-start.22
  117.8 0.9 copy-start.11
  141.8 2.2 copy-start.18
  144.0 5.1 %copy-start.20 = (f32[512,384]{0,1:T(8,128)}, f32[512,384]{0,1:T(8,128)S(1)}, u32[]{:S(2)}) copy-start(f32[512,384]{0,1:T(8,128)S(1)} %fusion.7) | copy-start | bytes 2359300
  149.2 2.6 copy-start.5
  149.2 2.6 copy-start.7
  153.8 1.0 copy-start.10
  153.8 1.1 copy-start.12
  153.8 1.9 copy-start.19
  155.7 1.1 copy-start.23
  155.7 1.4 copy-start.25
  159.3 8.5 %copy-start.6 = (bf16[512,384]{0,1:T(8,128)(2,1)S(1)}, bf16[512,384]{0,1:T(8,128)(2,1)}, u32[]{:S(2)}) copy-start(bf16[512,384]{0,1:T(8,128)(2,1)} %copy-done.5) | copy-start | bytes 1179652
  159.3 8.5 %copy-start.8 = (bf16[512,384]{0,1:T(8,128)(2,1)S(1)}, bf16[512,384]{0,1:T(8,128)(2,1)}, u32[]{:S(2)}) copy-start(bf16[512,384]{0,1:T(8,128)(2,1)} %copy-done.7) | copy-start | bytes 1179652
  159.3 56.5 %all-to-all-start.1 = ((bf16[16,32,2048]{2,1,0:T(8,128)(2,1)}), bf16[16,32,2048]{2,1,0:T(8,128)(2,1)S(1)}, u32[]{:S(2)}, u32[]{:S(2)}) async-start(bf16[16,32,2048]{2,1,0:T(8,128)(2,1)} %bitcast.9), calls=%async_computation.1 | async-start | bytes 4194304 | tf_op jit(solution)/shard_map/all_to_all | solution.py:38
  167.8 2.7 copy-start.21
  167.8 2.7 copy-start.24
  215.9 56.5 %all-to-all-start.3 = ((bf16[16,32,2048]{2,1,0:T(8,128)(2,1)}), bf16[16,32,2048]{2,1,0:T(8,128)(2,1)}, u32[]{:S(2)}, u32[]{:S(2)}) async-start(bf16[16,32,2048]{2,1,0:T(8,128)(2,1)} %bitcast.13), calls=%async_computation.3 | async-start | bytes 4194304 | tf_op jit(solution)/shard_map/all_to_all | solution.py:38
  224.1 91.1 %reduce-scatter.5.cloned.1.call-start = ((), (), s32[]{:S(2)}) async-start(), calls=%async_computation.8 | async-start | bytes 1671168 | tf_op jit(solution)/shard_map/reduce_scatter | solution.py:124
  283.0 4.0 %copy-start.2 = (f32[256,1024]{1,0:T(8,128)S(1)}, f32[256,1024]{1,0:T(8,128)}, u32[]{:S(2)}) copy-start(f32[256,1024]{1,0:T(8,128)} %copy-done.1) | copy-start | bytes 3145732
  (1 other events, 0.7 us)
Sparse Core Ops, SparseCore 0:
  40.9 72.4 all-gather.1
  153.9 18.6 reduce-scatter.2
  228.0 87.1 reduce-scatter.4

commit v5 on v3

--- a/solution.py
+++ b/solution.py
@@ -65,32 +65,18 @@
     down_full = full_weights[:, 2 * hidden_total :]
     stacked = full_weights[:, : 2 * hidden_total]
     flat_ids, position, expert_loads = pick_slots(routing, expert_total)
-    pick_index = jnp.arange(pick_total, dtype=jnp.int32)
-    owners = pick_index // top_count
     upstream_wide = upstream.astype(jnp.float32)
     pick_cotangent = (
         (combine[:, :, None] * upstream_wide[:, None, :])
         .reshape(pick_total, feature_total)
         .astype(jnp.bfloat16)
     )
-    slot_index = jnp.where(flat_ids >= 0, flat_ids * capacity + position, expert_total * capacity)
-    token_source = (
-        jnp.full((expert_total * capacity,), tok_count, jnp.int32)
-        .at[slot_index]
-        .set(owners, mode="drop")
-    )
-    pick_source = (
-        jnp.full((expert_total * capacity,), pick_total, jnp.int32)
-        .at[slot_index]
-        .set(pick_index, mode="drop")
-    )
-    sending = jnp.concatenate(
-        [
-            jnp.take(tokens, token_source, axis=0, mode="fill", fill_value=0),
-            jnp.take(pick_cotangent, pick_source, axis=0, mode="fill", fill_value=0),
-        ],
-        axis=1,
-    )
+    slot_index = flat_ids * capacity + position
+    select = (
+        slot_index[None, :] == jnp.arange(expert_total * capacity, dtype=jnp.int32)[:, None]
+    ).astype(jnp.bfloat16)
+    payload = jnp.concatenate([jnp.repeat(tokens, top_count, axis=0), pick_cotangent], axis=1)
+    sending = jnp.dot(select, payload, preferred_element_type=jnp.float32).astype(jnp.bfloat16)
     arrived_both = trade_rows(
         sending.reshape(expert_total, capacity, 2 * feature_total)
     ).reshape(expert_total * capacity, 2 * feature_total)
@@ -117,16 +103,18 @@
     returned = trade_rows(back.reshape(expert_total, capacity, 2 * feature_total)).reshape(
         expert_total * capacity, 2 * feature_total
     )
-    pick_both = jnp.take(returned, slot_index, axis=0, mode="fill", fill_value=0)
+    pick_both = lax.dot_general(
+        select, returned, (((0,), (0,)), ((), ())), preferred_element_type=jnp.float32
+    )
     pick_rows = pick_both[:, :feature_total]
     pick_grads = pick_both[:, feature_total:]
     gate_grad = summed[:, :hidden_total][None]
     up_grad = summed[:, hidden_total:][None]
-    pick_wide = pick_rows.reshape(tok_count, top_count, feature_total).astype(jnp.float32)
+    pick_wide = pick_rows.reshape(tok_count, top_count, feature_total)
     layer_output = jnp.sum(combine[:, :, None] * pick_wide, axis=1).astype(jnp.bfloat16)
     combine_grad = jnp.sum(upstream_wide[:, None, :] * pick_wide, axis=2)
     token_grad = jnp.sum(
-        pick_grads.reshape(tok_count, top_count, feature_total).astype(jnp.float32), axis=1
+        pick_grads.reshape(tok_count, top_count, feature_total), axis=1
     ).astype(jnp.bfloat16)
     return (layer_output, token_grad, combine_grad, gate_grad, up_grad)
 

time: 301 us -> 283 us (0.940); the launches traced: 300 us -> 278 us
  local copies, waits for them, and re-layouts: 36.6 us -> 15.7 us
  other arithmetic: 17.3 us -> 9.2 us
  matrix products: 18.9 us -> 25.5 us
    gather x3 -> x0, local copies, waits for them, and re-layouts: 15.8 us -> none  [the longest x1 5.39 us: shards(): jnp.take(tokens, token_source, axis=0, mode='fill', fill_value=0)]
    dot_general x0 -> x2, matrix products: none -> 6.8 us  [the longest x1 3.48 us: shards(): lax.dot_general(select, returned, (((0,), (0,)), ((), ())), preferred_ele...]
  transfers between devices with their start and end apart: 5 -> 5, of which waited for: 3 -> 3; matrix products, arithmetic and copies ran while one was open for 10% -> 9% of each run, Pallas kernels for 0% -> 0%
where the time goes in v5:
time: 283 us; the launch traced here: 278 us
  waiting for transfers between devices  191 us (67%)
  matrix products  25.5 us (9%)
  starting transfers between devices  21.9 us (8%)
  local copies, waits for them, and re-layouts  15.7 us (6%)
  between operations  14 us (5%)
  other arithmetic  9.2 us (3%)
    all_to_all x2, waiting for transfers between devices, trade_rows(): lax.all_to_all(buffer, EXPERT_AXES, split_axis=0, concat_axis=0, tiled=True)  115 us
    all_gather x1, waiting for transfers between devices, shards(): full_weights = lax.all_gather(local_weights, DP_AXES, axis=0, tiled=True)  75.5 us
    all_to_all x2, starting transfers between devices, trade_rows(): lax.all_to_all(buffer, EXPERT_AXES, split_axis=0, concat_axis=0, tiled=True)  21.4 us
    concatenate x1, local copies, waits for them, and re-layouts, shards(): back = jnp.concatenate([results, input_grads], axis=1)  6.57 us
  transfers between devices with their start and end apart: 5, of which 3 were waited for; matrix products, arithmetic and copies ran while one was open for 9% of the time, Pallas kernels for 0%

profile of v5, /device:TPU:1, one launch (start us, length us, event | category | flops | bytes accessed | tf_op | source)
XLA Modules:
  0.0 277.5 jit_solution(10668888117497043271)
XLA Ops:
  7.2 0.8 copy.15
  8.3 0.6 reduce-window.6
  9.2 0.8 copy.14
  10.1 1.2 broadcast_in_dim.6
  11.6 0.3 mul.75
  11.9 0.7 mul.76
  12.7 3.3 %convolution_convert_fusion = bf16[1024,2048]{1,0:T(8,128)(2,1)} fusion(bf16[256,1024]{1,0:T(8,128)(2,1)S(1)} %multiply_convert_fusion.3, bf16[256,1024]{1,0:T(8,128)(2,1)S(1)} %reshape.79, s32[256]{0:T(256)S(1)} %multiply_add_fusion), kind=kOutput, calls=%fused_computation.1 | convolution fusion | flops 1078198272 | bytes 5243904 | tf_op jit(solution)/shard_map/dot_general | solution.py:79
  16.1 13.6 %all-to-all-start = ((bf16[16,64,2048]{2,1,0:T(8,128)(2,1)}), bf16[16,64,2048]{2,1,0:T(8,128)(2,1)}, u32[]{:S(2)}, u32[]{:S(2)}) async-start(bf16[16,64,2048]{2,1,0:T(8,128)(2,1)} %bitcast.34), calls=%async_computation | async-start | bytes 8388608 | tf_op jit(solution)/shard_map/all_to_all | solution.py:38
  29.8 0.6 pad_maximum_fusion.4
  30.6 75.5 %all-gather.2.cloned.1.call-done = bf16[1024,1152]{1,0:T(8,128)(2,1)} async-done(((bf16[32,1152]{1,0:T(8,128)(2,1)}), bf16[1024,1152]{1,0:T(8,128)(2,1)}) %all-gather.2.cloned.1.call-update) | async-done | bytes 2359312 | tf_op jit(solution)/shard_map/all_gather | solution.py:62
  106.2 19.7 %all-to-all-done = bf16[16,64,2048]{2,1,0:T(8,128)(2,1)} async-done(((bf16[16,64,2048]{2,1,0:T(8,128)(2,1)}), bf16[16,64,2048]{2,1,0:T(8,128)(2,1)}, u32[]{:S(2)}, u32[]{:S(2)}) %all-to-all-start) | async-done | bytes 4194336 | tf_op jit(solution)/shard_map/all_to_all | solution.py:38
  125.9 2.9 %fusion.4 = f32[1024,384]{0,1:T(8,128)S(1)} fusion(bf16[1024,2048]{1,0:T(8,128)(2,1)} %bitcast.2, bf16[1024,1152]{1,0:T(8,128)(2,1)} %all-gather.2.cloned.1.call-done), kind=kOutput, calls=%fused_computation.9 | convolution fusion | flops 805306368 | bytes 4456448 | tf_op jit(solution)/shard_map/dot_general | solution.py:15
  128.8 2.6 fusion
  131.5 4.4 %multiply_convert_fusion.1 = (bf16[1024,384]{0,1:T(8,128)(2,1)S(1)}, bf16[1024,384]{0,1:T(8,128)(2,1)S(1)}, f32[1024,384]{0,1:T(8,128)}) fusion(f32[1024,384]{0,1:T(8,128)S(1)} %fusion, f32[1024,384]{0,1:T(8,128)S(1)} %fusion.4, bf16[1024,1152]{1,0:T(8,128)(2,1)S(1)} %copy-done.4, bf16[1024,2048]{1,0:T(8,128)(2,1)} %bitcast.2), kind=kOutput, calls=%fused_computation.16 | convolution fusion | flops 810418176 | bytes 9175040 | tf_op jit(solution)/shard_map/dot_general | solution.py:14
  135.9 3.7 %fusion.2 = f32[1024,768]{1,0:T(8,128)S(1)} fusion(bf16[1024,2048]{1,0:T(8,128)(2,1)} %bitcast.2, bf16[1024,384]{0,1:T(8,128)(2,1)S(1)} %get-tuple-element.11, bf16[1024,384]{0,1:T(8,128)(2,1)S(1)} %get-tuple-element.10), kind=kOutput, calls=%fused_computation.7 | convolution fusion | flops 1613758464 | bytes 6815744 | tf_op jit(solution)/shard_map/dot_general | solution.py:87
  139.6 1.8 copy.25
  141.5 3.2 %convolution_convert_fusion.1 = bf16[1024,1024]{0,1:T(8,128)(2,1)S(1)} fusion(f32[1024,384]{0,1:T(8,128)S(1)} %fusion.4, bf16[1024,1152]{1,0:T(8,128)(2,1)} %all-gather.2.cloned.1.call-done, f32[1024,384]{0,1:T(8,128)} %get-tuple-element.17), kind=kOutput, calls=%fused_computation.5 | convolution fusion | flops 808714240 | bytes 6029312 | tf_op jit(solution)/shard_map/dot_general | solution.py:17
  144.7 1.8 convolution_convert_fusion.2
  146.5 2.4 pad_maximum_fusion
  148.9 6.6 %copy.19 = bf16[1024,2048]{1,0:T(8,128)(2,1)} copy(bf16[1024,2048]{0,1:T(8,128)(2,1)} %pad_maximum_fusion) | data formatting | bytes 8388608 | tf_op jit(solution)/shard_map/concatenate | solution.py:102
  155.5 7.8 %all-to-all-start.1 = ((bf16[16,64,2048]{2,1,0:T(8,128)(2,1)}), bf16[16,64,2048]{2,1,0:T(8,128)(2,1)}, u32[]{:S(2)}, u32[]{:S(2)}) async-start(bf16[16,64,2048]{2,1,0:T(8,128)(2,1)} %bitcast.35), calls=%async_computation.1 | async-start | bytes 8388608 | tf_op jit(solution)/shard_map/all_to_all | solution.py:38
  163.3 0.3 reduce-scatter.5.cloned.1.call-start
  163.6 0.4 reduce-scatter.5.cloned.1.call-update
  164.0 95.5 %all-to-all-done.1 = bf16[16,64,2048]{2,1,0:T(8,128)(2,1)} async-done(((bf16[16,64,2048]{2,1,0:T(8,128)(2,1)}), bf16[16,64,2048]{2,1,0:T(8,128)(2,1)}, u32[]{:S(2)}, u32[]{:S(2)}) %all-to-all-start.1) | async-done | bytes 4194336 | tf_op jit(solution)/shard_map/all_to_all | solution.py:38
  259.6 3.5 %fusion.13 = f32[256,2048]{1,0:T(8,128)S(1)} fusion(bf16[1024,2048]{1,0:T(8,128)(2,1)} %bitcast.7, s32[256]{0:T(256)S(1)} %multiply_add_fusion), kind=kOutput, calls=%fused_computation.27 | convolution fusion | flops 1074003968 | bytes 6292480 | tf_op jit(solution)/shard_map/dot_general | solution.py:106
  263.4 0.6 copy.21
  264.1 0.6 reshape.85
  264.7 0.6 reshape.84
  265.3 2.1 reduce_sum.40
  267.4 2.1 multiply_reduce_fusion.1
  269.5 0.9 multiply_bitcast_fusion
  270.4 0.6 slice_bitcast_fusion
  (35 shorter events, 1.8 us)
Async XLA Ops:
  7.2 4.4 %copy-start = (bf16[128,1024]{1,0:T(8,128)(2,1)S(1)}, bf16[128,1024]{1,0:T(8,128)(2,1)}, u32[]{:S(2)}) copy-start(bf16[128,1024]{1,0:T(8,128)(2,1)} %param.10) | copy-start | bytes 786436
  16.0 13.7 %copy-start.1 = (bf16[1,32,384]{2,1,0:T(8,128)(2,1)S(1)}, bf16[1,32,384]{2,1,0:T(8,128)(2,1)}, u32[]{:S(2)}) copy-start(bf16[1,32,384]{2,1,0:T(8,128)(2,1)} %param.13) | copy-start | bytes 73732
  16.0 13.7 %copy-start.2 = (bf16[1,32,384]{2,1,0:T(8,128)(2,1)S(1)}, bf16[1,32,384]{2,1,0:T(8,128)(2,1)}, u32[]{:S(2)}) copy-start(bf16[1,32,384]{2,1,0:T(8,128)(2,1)} %param.12) | copy-start | bytes 73732
  16.1 13.7 %copy-start.3 = (bf16[1,32,384]{2,1,0:T(8,128)(2,1)S(1)}, bf16[1,32,384]{2,1,0:T(8,128)(2,1)}, u32[]{:S(2)}) copy-start(bf16[1,32,384]{2,1,0:T(8,128)(2,1)} %param.11) | copy-start | bytes 73732
  16.1 109.8 %all-to-all-start = ((bf16[16,64,2048]{2,1,0:T(8,128)(2,1)}), bf16[16,64,2048]{2,1,0:T(8,128)(2,1)}, u32[]{:S(2)}, u32[]{:S(2)}) async-start(bf16[16,64,2048]{2,1,0:T(8,128)(2,1)} %bitcast.34), calls=%async_computation | async-start | bytes 8388608 | tf_op jit(solution)/shard_map/all_to_all | solution.py:38
  29.7 76.5 %all-gather.2.cloned.1.call-start = ((), (), s32[]{:S(2)}) async-start(), calls=%async_computation.4 | async-start | bytes 2433024 | tf_op jit(solution)/shard_map/all_gather | solution.py:62
  30.4 133.1 %reduce-scatter.3.cloned.1.call-start = ((), (), s32[]{:S(2)}) async-start(), calls=%async_computation.5 | async-start | bytes 4718592 | tf_op jit(solution)/shard_map/reduce_scatter | solution.py:94
  125.9 2.9 %copy-start.4 = (bf16[1024,1152]{1,0:T(8,128)(2,1)S(1)}, bf16[1024,1152]{1,0:T(8,128)(2,1)}, u32[]{:S(2)}) copy-start(bf16[1024,1152]{1,0:T(8,128)(2,1)} %all-gather.2.cloned.1.call-done) | copy-start | bytes 7077892
  135.9 3.8 %copy-start.6 = (bf16[1024,384]{0,1:T(8,128)(2,1)}, bf16[1024,384]{0,1:T(8,128)(2,1)S(1)}, u32[]{:S(2)}) copy-start(bf16[1024,384]{0,1:T(8,128)(2,1)S(1)} %get-tuple-element.11) | copy-start | bytes 2359300
  141.5 3.2 %copy-start.5 = (bf16[1024,1152]{1,0:T(8,128)(2,1)S(1)}, bf16[1024,1152]{1,0:T(8,128)(2,1)}, u32[]{:S(2)}) copy-start(bf16[1024,1152]{1,0:T(8,128)(2,1)} %all-gather.2.cloned.1.call-done) | copy-start | bytes 7077892
  141.5 3.2 %copy-start.7 = (bf16[1024,384]{0,1:T(8,128)(2,1)S(1)}, bf16[1024,384]{0,1:T(8,128)(2,1)}, u32[]{:S(2)}) copy-start(bf16[1024,384]{0,1:T(8,128)(2,1)} %copy-done.6) | copy-start | bytes 2359300
  155.5 104.0 %all-to-all-start.1 = ((bf16[16,64,2048]{2,1,0:T(8,128)(2,1)}), bf16[16,64,2048]{2,1,0:T(8,128)(2,1)}, u32[]{:S(2)}, u32[]{:S(2)}) async-start(bf16[16,64,2048]{2,1,0:T(8,128)(2,1)} %bitcast.35), calls=%async_computation.1 | async-start | bytes 8388608 | tf_op jit(solution)/shard_map/all_to_all | solution.py:38
  163.3 106.2 %reduce-scatter.5.cloned.1.call-start = ((), (), s32[]{:S(2)}) async-start(), calls=%async_computation.6 | async-start | bytes 1671168 | tf_op jit(solution)/shard_map/reduce_scatter | solution.py:95
Sparse Core Ops, SparseCore 0:
  33.2 72.8 all-gather.1
  141.6 19.8 reduce-scatter.2
  167.2 85.3 reduce-scatter.4

commit v6 on v5

--- a/solution.py
+++ b/solution.py
@@ -1,6 +1,7 @@
 import jax
 import jax.numpy as jnp
 from jax import lax
+from jax.experimental.layout import Layout, with_layout_constraint
 from jax.sharding import Mesh
 from jax.sharding import PartitionSpec as P
 
@@ -99,7 +100,11 @@
         tiled=True,
     )
     summed = summed.reshape(slice_rows, 2 * hidden_total) / group_total
-    back = jnp.concatenate([results, input_grads], axis=1)
+    row_major = Layout(major_to_minor=(0, 1))
+    back = jnp.concatenate(
+        [with_layout_constraint(results, row_major), with_layout_constraint(input_grads, row_major)],
+        axis=1,
+    )
     returned = trade_rows(back.reshape(expert_total, capacity, 2 * feature_total)).reshape(
         expert_total * capacity, 2 * feature_total
     )

time: 283 us -> 273 us (0.965); the launches traced: 278 us -> 272 us
  local copies, waits for them, and re-layouts: 15.7 us -> 9.17 us
    concatenate x1 -> x0, local copies, waits for them, and re-layouts: 6.57 us -> none  [shards(): back = jnp.concatenate([results, input_grads], axis=1)]
    reduce_scatter x1, waiting for transfers between devices: 0.02 us -> 4.34 us  [shards(): lax.psum_scatter(by_core, 'c', scatter_dimension=0, tiled=True)]
    all_to_all x2, waiting for transfers between devices: 115 us -> 112 us  [trade_rows(): lax.all_to_all(buffer, EXPERT_AXES, split_axis=0, concat_axis=0, tiled=True)]
  transfers between devices with their start and end apart: 5 -> 5, of which waited for: 3 -> 4; matrix products, arithmetic and copies ran while one was open for 9% -> 7% of each run, Pallas kernels for 0% -> 0%
where the time goes in v6:
time: 273 us; the launch traced here: 272 us
  waiting for transfers between devices  191 us (70%)
  matrix products  26.4 us (10%)
  starting transfers between devices  21.9 us (8%)
  between operations  14 us (5%)
  other arithmetic  9.19 us (3%)
  local copies, waits for them, and re-layouts  9.17 us (3%)
    all_to_all x2, waiting for transfers between devices, trade_rows(): lax.all_to_all(buffer, EXPERT_AXES, split_axis=0, concat_axis=0, tiled=True)  112 us
    all_gather x1, waiting for transfers between devices, shards(): full_weights = lax.all_gather(local_weights, DP_AXES, axis=0, tiled=True)  75.5 us
    all_to_all x2, starting transfers between devices, trade_rows(): lax.all_to_all(buffer, EXPERT_AXES, split_axis=0, concat_axis=0, tiled=True)  21.4 us
  transfers between devices with their start and end apart: 5, of which 4 were waited for; matrix products, arithmetic and copies ran while one was open for 7% of the time, Pallas kernels for 0%

profile of v6, /device:TPU:1, one launch (start us, length us, event | category | flops | bytes accessed | tf_op | source)
XLA Modules:
  0.0 272.1 jit_solution(4716121978781664775)
XLA Ops:
  7.2 0.8 copy.15
  8.3 0.6 reduce-window.6
  9.2 0.8 copy.14
  10.1 1.2 broadcast_in_dim.6
  11.6 0.3 mul.75
  11.9 0.7 mul.76
  12.7 3.2 %convolution_convert_fusion = bf16[1024,2048]{1,0:T(8,128)(2,1)} fusion(bf16[256,1024]{1,0:T(8,128)(2,1)S(1)} %multiply_convert_fusion.3, bf16[256,1024]{1,0:T(8,128)(2,1)S(1)} %reshape.79, s32[256]{0:T(256)S(1)} %multiply_add_fusion), kind=kOutput, calls=%fused_computation.1 | convolution fusion | flops 1078198272 | bytes 5243904 | tf_op jit(solution)/shard_map/dot_general | solution.py:80
  16.0 13.6 %all-to-all-start = ((bf16[16,64,2048]{2,1,0:T(8,128)(2,1)}), bf16[16,64,2048]{2,1,0:T(8,128)(2,1)}, u32[]{:S(2)}, u32[]{:S(2)}) async-start(bf16[16,64,2048]{2,1,0:T(8,128)(2,1)} %bitcast.34), calls=%async_computation | async-start | bytes 8388608 | tf_op jit(solution)/shard_map/all_to_all | solution.py:39
  29.7 0.6 pad_maximum_fusion.4
  30.6 75.5 %all-gather.2.cloned.1.call-done = bf16[1024,1152]{1,0:T(8,128)(2,1)} async-done(((bf16[32,1152]{1,0:T(8,128)(2,1)}), bf16[1024,1152]{1,0:T(8,128)(2,1)}) %all-gather.2.cloned.1.call-update) | async-done | bytes 2359312 | tf_op jit(solution)/shard_map/all_gather | solution.py:63
  106.1 19.7 %all-to-all-done = bf16[16,64,2048]{2,1,0:T(8,128)(2,1)} async-done(((bf16[16,64,2048]{2,1,0:T(8,128)(2,1)}), bf16[16,64,2048]{2,1,0:T(8,128)(2,1)}, u32[]{:S(2)}, u32[]{:S(2)}) %all-to-all-start) | async-done | bytes 4194336 | tf_op jit(solution)/shard_map/all_to_all | solution.py:39
  125.8 2.9 %fusion.4 = f32[1024,384]{0,1:T(8,128)S(1)} fusion(bf16[1024,2048]{1,0:T(8,128)(2,1)} %bitcast.2, bf16[1024,1152]{1,0:T(8,128)(2,1)} %all-gather.2.cloned.1.call-done), kind=kOutput, calls=%fused_computation.9 | convolution fusion | flops 805306368 | bytes 4456448 | tf_op jit(solution)/shard_map/dot_general | solution.py:16
  128.8 3.2 %fusion = f32[1024,384]{0,1:T(8,128)S(1)} fusion(bf16[1024,2048]{1,0:T(8,128)(2,1)} %bitcast.2, bf16[1024,1152]{1,0:T(8,128)(2,1)S(1)} %copy-done.4), kind=kOutput, calls=%fused_computation.3 | convolution fusion | flops 805306368 | bytes 4456448 | tf_op jit(solution)/shard_map/dot_general | solution.py:25
  132.0 4.3 %multiply_convert_fusion.1 = (bf16[1024,384]{0,1:T(8,128)(2,1)S(1)}, bf16[1024,384]{0,1:T(8,128)(2,1)S(1)}, f32[1024,384]{0,1:T(8,128)}) fusion(f32[1024,384]{0,1:T(8,128)S(1)} %fusion, f32[1024,384]{0,1:T(8,128)S(1)} %fusion.4, bf16[1024,1152]{1,0:T(8,128)(2,1)S(1)} %copy-done.4, bf16[1024,2048]{1,0:T(8,128)(2,1)} %bitcast.2), kind=kOutput, calls=%fused_computation.16 | convolution fusion | flops 810418176 | bytes 9175040 | tf_op jit(solution)/shard_map/dot_general | solution.py:15
  136.3 4.0 %fusion.2 = f32[1024,768]{1,0:T(8,128)S(1)} fusion(bf16[1024,2048]{1,0:T(8,128)(2,1)} %bitcast.2, bf16[1024,384]{0,1:T(8,128)(2,1)S(1)} %get-tuple-element.11, bf16[1024,384]{0,1:T(8,128)(2,1)S(1)} %get-tuple-element.10), kind=kOutput, calls=%fused_computation.7 | convolution fusion | flops 1613758464 | bytes 6815744 | tf_op jit(solution)/shard_map/dot_general | solution.py:88
  140.4 1.8 copy.24
  142.2 3.3 %convolution_convert_fusion.1 = bf16[1024,1024]{1,0:T(8,128)(2,1)S(1)} fusion(f32[1024,384]{0,1:T(8,128)} %copy-done.5, bf16[1024,1152]{1,0:T(8,128)(2,1)S(1)} %copy-done.4, f32[1024,384]{0,1:T(8,128)} %get-tuple-element.17), kind=kOutput, calls=%fused_computation.5 | convolution fusion | flops 808714240 | bytes 6029312 | tf_op jit(solution)/shard_map/dot_general | solution.py:18
  145.6 1.8 convolution_convert_fusion.2
  147.4 2.4 pad_maximum_fusion
  149.9 7.7 %all-to-all-start.1 = ((bf16[16,64,2048]{2,1,0:T(8,128)(2,1)}), bf16[16,64,2048]{2,1,0:T(8,128)(2,1)}, u32[]{:S(2)}, u32[]{:S(2)}) async-start(bf16[16,64,2048]{2,1,0:T(8,128)(2,1)} %bitcast.35), calls=%async_computation.1 | async-start | bytes 8388608 | tf_op jit(solution)/shard_map/all_to_all | solution.py:39
  157.6 0.3 reduce-scatter.5.cloned.1.call-start
  157.9 4.3 %reduce-scatter.3.cloned.1.call-done = f32[1,16,32,768]{3,2,1,0:T(8,128)} async-done(((f32[2,16,32,768]{3,2,1,0:T(8,128)}), f32[1,16,32,768]{3,2,1,0:T(8,128)}) %reduce-scatter.3.cloned.1.call-update) | async-done | bytes 1572880 | tf_op jit(solution)/shard_map/reduce_scatter | solution.py:95
  162.3 91.8 %all-to-all-done.1 = bf16[16,64,2048]{2,1,0:T(8,128)(2,1)} async-done(((bf16[16,64,2048]{2,1,0:T(8,128)(2,1)}), bf16[16,64,2048]{2,1,0:T(8,128)(2,1)}, u32[]{:S(2)}, u32[]{:S(2)}) %all-to-all-start.1) | async-done | bytes 4194336 | tf_op jit(solution)/shard_map/all_to_all | solution.py:39
  254.1 3.5 %fusion.13 = f32[256,2048]{1,0:T(8,128)S(1)} fusion(bf16[1024,2048]{1,0:T(8,128)(2,1)} %bitcast.7, s32[256]{0:T(256)S(1)} %multiply_add_fusion), kind=kOutput, calls=%fused_computation.27 | convolution fusion | flops 1074003968 | bytes 6292480 | tf_op jit(solution)/shard_map/dot_general | solution.py:111
  257.6 0.2 multiply_reduce_fusion
  258.0 0.6 copy.20
  258.6 0.6 reshape.85
  259.2 0.6 reshape.84
  259.9 2.1 reduce_sum.40
  261.9 2.1 multiply_reduce_fusion.1
  264.0 0.9 multiply_bitcast_fusion
  264.9 0.6 slice_bitcast_fusion
  (38 shorter events, 1.6 us)
Async XLA Ops:
  7.2 4.4 %copy-start = (bf16[128,1024]{1,0:T(8,128)(2,1)S(1)}, bf16[128,1024]{1,0:T(8,128)(2,1)}, u32[]{:S(2)}) copy-start(bf16[128,1024]{1,0:T(8,128)(2,1)} %param.10) | copy-start | bytes 786436
  16.0 13.7 %copy-start.1 = (bf16[1,32,384]{2,1,0:T(8,128)(2,1)S(1)}, bf16[1,32,384]{2,1,0:T(8,128)(2,1)}, u32[]{:S(2)}) copy-start(bf16[1,32,384]{2,1,0:T(8,128)(2,1)} %param.13) | copy-start | bytes 73732
  16.0 13.7 %copy-start.2 = (bf16[1,32,384]{2,1,0:T(8,128)(2,1)S(1)}, bf16[1,32,384]{2,1,0:T(8,128)(2,1)}, u32[]{:S(2)}) copy-start(bf16[1,32,384]{2,1,0:T(8,128)(2,1)} %param.12) | copy-start | bytes 73732
  16.0 13.7 %copy-start.3 = (bf16[1,32,384]{2,1,0:T(8,128)(2,1)S(1)}, bf16[1,32,384]{2,1,0:T(8,128)(2,1)}, u32[]{:S(2)}) copy-start(bf16[1,32,384]{2,1,0:T(8,128)(2,1)} %param.11) | copy-start | bytes 73732
  16.0 109.8 %all-to-all-start = ((bf16[16,64,2048]{2,1,0:T(8,128)(2,1)}), bf16[16,64,2048]{2,1,0:T(8,128)(2,1)}, u32[]{:S(2)}, u32[]{:S(2)}) async-start(bf16[16,64,2048]{2,1,0:T(8,128)(2,1)} %bitcast.34), calls=%async_computation | async-start | bytes 8388608 | tf_op jit(solution)/shard_map/all_to_all | solution.py:39
  29.6 76.5 %all-gather.2.cloned.1.call-start = ((), (), s32[]{:S(2)}) async-start(), calls=%async_computation.4 | async-start | bytes 2433024 | tf_op jit(solution)/shard_map/all_gather | solution.py:63
  30.3 131.9 %reduce-scatter.3.cloned.1.call-start = ((), (), s32[]{:S(2)}) async-start(), calls=%async_computation.5 | async-start | bytes 4718592 | tf_op jit(solution)/shard_map/reduce_scatter | solution.py:95
  125.8 2.9 %copy-start.4 = (bf16[1024,1152]{1,0:T(8,128)(2,1)S(1)}, bf16[1024,1152]{1,0:T(8,128)(2,1)}, u32[]{:S(2)}) copy-start(bf16[1024,1152]{1,0:T(8,128)(2,1)} %all-gather.2.cloned.1.call-done) | copy-start | bytes 7077892
  128.7 3.2 %copy-start.5 = (f32[1024,384]{0,1:T(8,128)}, f32[1024,384]{0,1:T(8,128)S(1)}, u32[]{:S(2)}) copy-start(f32[1024,384]{0,1:T(8,128)S(1)} %fusion.4) | copy-start | bytes 4718596
  136.3 4.0 %copy-start.6 = (bf16[1024,384]{0,1:T(8,128)(2,1)}, bf16[1024,384]{0,1:T(8,128)(2,1)S(1)}, u32[]{:S(2)}) copy-start(bf16[1024,384]{0,1:T(8,128)(2,1)S(1)} %get-tuple-element.10) | copy-start | bytes 2359300
  136.3 4.0 %copy-start.8 = (bf16[1024,384]{0,1:T(8,128)(2,1)}, bf16[1024,384]{0,1:T(8,128)(2,1)S(1)}, u32[]{:S(2)}) copy-start(bf16[1024,384]{0,1:T(8,128)(2,1)S(1)} %get-tuple-element.11) | copy-start | bytes 2359300
  142.2 3.4 %copy-start.7 = (bf16[1024,384]{0,1:T(8,128)(2,1)S(1)}, bf16[1024,384]{0,1:T(8,128)(2,1)}, u32[]{:S(2)}) copy-start(bf16[1024,384]{0,1:T(8,128)(2,1)} %copy-done.6) | copy-start | bytes 2359300
  142.2 3.4 %copy-start.9 = (bf16[1024,384]{0,1:T(8,128)(2,1)S(1)}, bf16[1024,384]{0,1:T(8,128)(2,1)}, u32[]{:S(2)}) copy-start(bf16[1024,384]{0,1:T(8,128)(2,1)} %copy-done.8) | copy-start | bytes 2359300
  149.9 104.2 %all-to-all-start.1 = ((bf16[16,64,2048]{2,1,0:T(8,128)(2,1)}), bf16[16,64,2048]{2,1,0:T(8,128)(2,1)}, u32[]{:S(2)}, u32[]{:S(2)}) async-start(bf16[16,64,2048]{2,1,0:T(8,128)(2,1)} %bitcast.35), calls=%async_computation.1 | async-start | bytes 8388608 | tf_op jit(solution)/shard_map/all_to_all | solution.py:39
  157.6 106.4 %reduce-scatter.5.cloned.1.call-start = ((), (), s32[]{:S(2)}) async-start(), calls=%async_computation.6 | async-start | bytes 1671168 | tf_op jit(solution)/shard_map/reduce_scatter | solution.py:96
Sparse Core Ops, SparseCore 0:
  33.1 72.8 all-gather.1
  142.3 19.8 reduce-scatter.2
  165.3 85.2 reduce-scatter.4

commit v7 on v6

--- a/solution.py
+++ b/solution.py
@@ -11,9 +11,11 @@
 TOKEN_AXES = DP_AXES + EXPERT_AXES
 
 
-def expert_forward(input_rows, gate_full, up_full, down_full):
-    gate_pre = jnp.dot(input_rows, gate_full, preferred_element_type=jnp.float32)
-    up_pre = jnp.dot(input_rows, up_full, preferred_element_type=jnp.float32)
+def expert_forward(input_rows, stacked, down_full):
+    hidden_total = stacked.shape[1] // 2
+    both_pre = jnp.dot(input_rows, stacked, preferred_element_type=jnp.float32)
+    gate_pre = both_pre[:, :hidden_total]
+    up_pre = both_pre[:, hidden_total:]
     hidden = (jax.nn.silu(gate_pre) * up_pre).astype(jnp.bfloat16)
     results = lax.dot_general(
         hidden, down_full, (((1,), (1,)), ((), ())), preferred_element_type=jnp.float32
@@ -83,22 +85,18 @@
     ).reshape(expert_total * capacity, 2 * feature_total)
     arrived = arrived_both[:, :feature_total]
     cot_arrived = arrived_both[:, feature_total:]
-    results, gate_pre, up_pre = expert_forward(arrived, gate_full, up_full, down_full)
+    results, gate_pre, up_pre = expert_forward(arrived, stacked, down_full)
     input_grads, deltas = expert_backward(cot_arrived, gate_pre, up_pre, stacked, down_full)
     piece = lax.dot_general(
         arrived, deltas, (((0,), (0,)), ((), ())), preferred_element_type=jnp.float32
     )
     slice_rows = gate_weight.shape[1]
-    by_core = jnp.swapaxes(
-        piece.reshape(group_total // core_total, core_total, slice_rows, 2 * hidden_total), 0, 1
-    )
-    core_summed = lax.psum_scatter(by_core, "c", scatter_dimension=0, tiled=True)
-    summed = lax.psum_scatter(
-        core_summed.reshape(group_total // core_total, slice_rows, 2 * hidden_total),
-        CHIP_AXES,
-        scatter_dimension=0,
-        tiled=True,
-    )
+    blocks = piece.reshape(group_total // core_total, core_total, slice_rows, 2 * hidden_total)
+    core = lax.axis_index("c")
+    own_blocks = lax.dynamic_index_in_dim(blocks, core, axis=1, keepdims=False)
+    other_blocks = lax.dynamic_index_in_dim(blocks, 1 - core, axis=1, keepdims=False)
+    core_summed = own_blocks + lax.ppermute(other_blocks, "c", perm=[(0, 1), (1, 0)])
+    summed = lax.psum_scatter(core_summed, CHIP_AXES, scatter_dimension=0, tiled=True)
     summed = summed.reshape(slice_rows, 2 * hidden_total) / group_total
     row_major = Layout(major_to_minor=(0, 1))
     back = jnp.concatenate(
@@ -108,19 +106,25 @@
     returned = trade_rows(back.reshape(expert_total, capacity, 2 * feature_total)).reshape(
         expert_total * capacity, 2 * feature_total
     )
-    pick_both = lax.dot_general(
-        select, returned, (((0,), (0,)), ((), ())), preferred_element_type=jnp.float32
+    pick_rows = lax.dot_general(
+        select,
+        returned[:, :feature_total],
+        (((0,), (0,)), ((), ())),
+        preferred_element_type=jnp.float32,
     )
-    pick_rows = pick_both[:, :feature_total]
-    pick_grads = pick_both[:, feature_total:]
+    token_select = jnp.any(
+        slot_index.reshape(tok_count, top_count)[:, :, None]
+        == jnp.arange(expert_total * capacity, dtype=jnp.int32)[None, None, :],
+        axis=1,
+    ).astype(jnp.bfloat16)
+    token_grad = jnp.dot(
+        token_select, returned[:, feature_total:], preferred_element_type=jnp.float32
+    ).astype(jnp.bfloat16)
     gate_grad = summed[:, :hidden_total][None]
     up_grad = summed[:, hidden_total:][None]
     pick_wide = pick_rows.reshape(tok_count, top_count, feature_total)
     layer_output = jnp.sum(combine[:, :, None] * pick_wide, axis=1).astype(jnp.bfloat16)
     combine_grad = jnp.sum(upstream_wide[:, None, :] * pick_wide, axis=2)
-    token_grad = jnp.sum(
-        pick_grads.reshape(tok_count, top_count, feature_total), axis=1
-    ).astype(jnp.bfloat16)
     return (layer_output, token_grad, combine_grad, gate_grad, up_grad)
 
 

time: 273 us -> 276 us (1.011)
  the two profiles are of different devices: /device:TPU:1 before, /device:TPU:64 now
where the time goes in v7:
time: 276 us
  waiting for transfers between devices  196 us (71%)
  starting transfers between devices  23.6 us (9%)
  matrix products  22.1 us (8%)
  between operations  14.2 us (5%)
  local copies, waits for them, and re-layouts  9.93 us (4%)
  other arithmetic  9.85 us (4%)
    reduce_scatter x1, waiting for transfers between devices, shards(): lax.psum_scatter(core_summed, CHIP_AXES, scatter_dimension=0, tiled=True)  97.9 us
    all_gather x1, waiting for transfers between devices, shards(): full_weights = lax.all_gather(local_weights, DP_AXES, axis=0, tiled=True)  82.3 us
    all_to_all x2, starting transfers between devices, trade_rows(): lax.all_to_all(buffer, EXPERT_AXES, split_axis=0, concat_axis=0, tiled=True)  21.4 us
    all_to_all x2, waiting for transfers between devices, trade_rows(): lax.all_to_all(buffer, EXPERT_AXES, split_axis=0, concat_axis=0, tiled=True)  12.1 us
  transfers between devices with their start and end apart: 5, of which 4 were waited for; matrix products, arithmetic and copies ran while one was open for 4% of the time, Pallas kernels for 0%

profile of v7, /device:TPU:64, one launch (start us, length us, event | category | flops | bytes accessed | tf_op | source)
XLA Modules:
  0.0 275.7 jit_solution(13049830553330244048)
XLA Ops:
  7.2 0.8 copy.32
  8.3 0.8 copy.31
  9.2 0.6 reduce-window.6
  10.1 1.2 broadcast_in_dim.6
  11.6 0.3 mul.81
  11.9 0.7 mul.82
  12.7 3.2 %convolution_convert_fusion = bf16[1024,2048]{1,0:T(8,128)(2,1)} fusion(bf16[256,1024]{1,0:T(8,128)(2,1)S(1)} %multiply_convert_fusion.3, bf16[256,1024]{1,0:T(8,128)(2,1)S(1)} %reshape.79, s32[256]{0:T(256)S(1)} %multiply_add_fusion.1), kind=kOutput, calls=%fused_computation.1 | convolution fusion | flops 1078198272 | bytes 5243904 | tf_op jit(solution)/shard_map/dot_general | solution.py:82
  15.9 12.6 %all-to-all-start = ((bf16[16,64,2048]{2,1,0:T(8,128)(2,1)}), bf16[16,64,2048]{2,1,0:T(8,128)(2,1)}, u32[]{:S(2)}, u32[]{:S(2)}) async-start(bf16[16,64,2048]{2,1,0:T(8,128)(2,1)} %bitcast.34), calls=%async_computation | async-start | bytes 8388608 | tf_op jit(solution)/shard_map/all_to_all | solution.py:41
  28.6 0.6 pad_maximum_fusion.4
  29.2 82.3 %all-gather.2.cloned.1.call-done = bf16[1024,1152]{1,0:T(8,128)(2,1)} async-done(((bf16[32,1152]{1,0:T(8,128)(2,1)}), bf16[1024,1152]{1,0:T(8,128)(2,1)}) %all-gather.2.cloned.1.call-update) | async-done | bytes 2359312 | tf_op jit(solution)/shard_map/all_gather | solution.py:65
  111.5 12.1 %all-to-all-done = bf16[16,64,2048]{2,1,0:T(8,128)(2,1)} async-done(((bf16[16,64,2048]{2,1,0:T(8,128)(2,1)}), bf16[16,64,2048]{2,1,0:T(8,128)(2,1)}, u32[]{:S(2)}, u32[]{:S(2)}) %all-to-all-start) | async-done | bytes 4194336 | tf_op jit(solution)/shard_map/all_to_all | solution.py:41
  123.7 4.1 %fusion.8 = f32[1024,768]{0,1:T(8,128)S(1)} fusion(bf16[1024,2048]{1,0:T(8,128)(2,1)} %bitcast.2, bf16[1024,1152]{1,0:T(8,128)(2,1)} %all-gather.2.cloned.1.call-done), kind=kOutput, calls=%fused_computation.12 | convolution fusion | flops 1610612736 | bytes 6815744 | tf_op jit(solution)/shard_map/dot_general | solution.py:16
  127.8 3.1 %multiply_convert_fusion.1 = (bf16[1024,384]{0,1:T(8,128)(2,1)S(1)}, bf16[1024,384]{0,1:T(8,128)(2,1)S(1)}) fusion(f32[1024,768]{0,1:T(8,128)S(1)} %fusion.8, bf16[1024,1152]{1,0:T(8,128)(2,1)S(1)} %copy-done.6, bf16[1024,2048]{1,0:T(8,128)(2,1)} %bitcast.2), kind=kOutput, calls=%fused_computation.18 | convolution fusion | flops 810418176 | bytes 7602176 | tf_op jit(solution)/shard_map/dot_general | solution.py:27
  130.9 1.3 convolution_convert_fusion.1
  132.2 1.9 convolution_convert_fusion.2
  134.1 2.4 pad_maximum_fusion
  136.5 8.9 %all-to-all-start.1 = ((bf16[16,64,2048]{2,1,0:T(8,128)(2,1)}), bf16[16,64,2048]{2,1,0:T(8,128)(2,1)}, u32[]{:S(2)}, u32[]{:S(2)}) async-start(bf16[16,64,2048]{2,1,0:T(8,128)(2,1)} %bitcast.35), calls=%async_computation.1 | async-start | bytes 8388608 | tf_op jit(solution)/shard_map/all_to_all | solution.py:41
  145.3 0.2 reduce-scatter.2.cloned.1.call-start
  145.6 3.4 %fusion.6 = f32[1024,768]{1,0:T(8,128)S(1)} fusion(bf16[1024,2048]{1,0:T(8,128)(2,1)} %bitcast.2, bf16[1024,384]{0,1:T(8,128)(2,1)S(1)} %get-tuple-element.21, bf16[1024,384]{0,1:T(8,128)(2,1)S(1)} %get-tuple-element.20), kind=kOutput, calls=%fused_computation.10 | convolution fusion | flops 1613758464 | bytes 6815744 | tf_op jit(solution)/shard_map/dot_general | solution.py:90
  149.0 1.7 copy-done
  150.8 1.3 dynamic-slice_bitcast_fusion
  152.1 1.9 collective-permute-start
  154.0 3.6 %collective-permute-done = f32[16,32,768]{2,1,0:T(8,128)S(1)} collective-permute-done((f32[16,32,768]{2,1,0:T(8,128)}, f32[16,32,768]{2,1,0:T(8,128)S(1)}, u32[]{:S(2)}, u32[]{:S(2)}) %collective-permute-start) | collective-permute-done | bytes 1572896 | tf_op jit(solution)/shard_map/ppermute | solution.py:98
  157.6 2.8 %bitcast_add_fusion = f32[16,32,768]{2,1,0:T(8,128)} fusion(f32[16,32,768]{2,1,0:T(8,128)S(1)} %collective-permute-done, f32[16,2,32,768]{3,2,1,0:T(8,128)} %bitcast.37, s32[]{:T(128)S(6)} %select_n.7), kind=kLoop, calls=%fused_computation.15 | loop fusion | flops 393216 | bytes 4718596 | tf_op jit(solution)/shard_map/add | solution.py:98
  160.8 97.9 %reduce-scatter.2.cloned.1.call-done = f32[1,32,768]{2,1,0:T(8,128)} async-done(((f32[16,32,768]{2,1,0:T(8,128)}), f32[1,32,768]{2,1,0:T(8,128)}) %reduce-scatter.2.cloned.1.call-update) | async-done | bytes 98320 | tf_op jit(solution)/shard_map/reduce_scatter | solution.py:99
  258.7 0.9 multiply_bitcast_fusion
  259.6 0.6 slice_bitcast_fusion
  260.2 2.4 multiply_reduce_fusion
  262.7 2.7 fusion.13
  265.5 0.6 copy.37
  266.2 0.6 reshape.84
  266.8 2.1 multiply_reduce_fusion.1
  (33 shorter events, 1.7 us)
Async XLA Ops:
  7.2 4.4 %copy-start.1 = (bf16[128,1024]{1,0:T(8,128)(2,1)S(1)}, bf16[128,1024]{1,0:T(8,128)(2,1)}, u32[]{:S(2)}) copy-start(bf16[128,1024]{1,0:T(8,128)(2,1)} %param.10) | copy-start | bytes 786436
  15.9 12.6 %copy-start.2 = (bf16[1,32,384]{2,1,0:T(8,128)(2,1)S(1)}, bf16[1,32,384]{2,1,0:T(8,128)(2,1)}, u32[]{:S(2)}) copy-start(bf16[1,32,384]{2,1,0:T(8,128)(2,1)} %param.13) | copy-start | bytes 73732
  15.9 12.6 %copy-start.3 = (bf16[1,32,384]{2,1,0:T(8,128)(2,1)S(1)}, bf16[1,32,384]{2,1,0:T(8,128)(2,1)}, u32[]{:S(2)}) copy-start(bf16[1,32,384]{2,1,0:T(8,128)(2,1)} %param.12) | copy-start | bytes 73732
  15.9 12.6 %copy-start.4 = (bf16[1,32,384]{2,1,0:T(8,128)(2,1)S(1)}, bf16[1,32,384]{2,1,0:T(8,128)(2,1)}, u32[]{:S(2)}) copy-start(bf16[1,32,384]{2,1,0:T(8,128)(2,1)} %param.11) | copy-start | bytes 73732
  15.9 107.8 %all-to-all-start = ((bf16[16,64,2048]{2,1,0:T(8,128)(2,1)}), bf16[16,64,2048]{2,1,0:T(8,128)(2,1)}, u32[]{:S(2)}, u32[]{:S(2)}) async-start(bf16[16,64,2048]{2,1,0:T(8,128)(2,1)} %bitcast.34), calls=%async_computation | async-start | bytes 8388608 | tf_op jit(solution)/shard_map/all_to_all | solution.py:41
  28.5 83.1 %all-gather.2.cloned.1.call-start = ((), (), s32[]{:S(2)}) async-start(), calls=%async_computation.3 | async-start | bytes 2433024 | tf_op jit(solution)/shard_map/all_gather | solution.py:65
  123.7 4.1 %copy-start.6 = (bf16[1024,1152]{1,0:T(8,128)(2,1)S(1)}, bf16[1024,1152]{1,0:T(8,128)(2,1)}, u32[]{:S(2)}) copy-start(bf16[1024,1152]{1,0:T(8,128)(2,1)} %all-gather.2.cloned.1.call-done) | copy-start | bytes 7077892
  136.5 123.8 %all-to-all-start.1 = ((bf16[16,64,2048]{2,1,0:T(8,128)(2,1)}), bf16[16,64,2048]{2,1,0:T(8,128)(2,1)}, u32[]{:S(2)}, u32[]{:S(2)}) async-start(bf16[16,64,2048]{2,1,0:T(8,128)(2,1)} %bitcast.35), calls=%async_computation.1 | async-start | bytes 8388608 | tf_op jit(solution)/shard_map/all_to_all | solution.py:41
  145.3 113.3 %reduce-scatter.2.cloned.1.call-start = ((), (), s32[]{:S(2)}) async-start(), calls=%async_computation.4 | async-start | bytes 1671168 | tf_op jit(solution)/shard_map/reduce_scatter | solution.py:99
  149.0 1.8 copy-start
  152.1 5.5 %collective-permute-start = (f32[16,32,768]{2,1,0:T(8,128)}, f32[16,32,768]{2,1,0:T(8,128)S(1)}, u32[]{:S(2)}, u32[]{:S(2)}) collective-permute-start(f32[16,32,768]{2,1,0:T(8,128)} %dynamic-slice_bitcast_fusion), channel_id=1, source_target_pairs={{0,16},{16,0},{1,17},{17,1},{2,18},{18,2},{3,19},{19,3},{4,20},{20... | collective-permute-start | bytes 4718600 | tf_op jit(solution)/shard_map/ppermute | solution.py:98
  154.0 6.6 %copy-start.5 = (s32[128,2]{0,1:T(2,128)S(1)}, s32[128,2]{0,1:T(2,128)}, u32[]{:S(2)}) copy-start(s32[128,2]{0,1:T(2,128)} %param.8) | copy-start | bytes 3076
Sparse Core Ops, SparseCore 0:
  32.1 79.4 all-gather.1
  160.5 98.1 reduce-scatter.1

commit v8 on v7

--- a/solution.py
+++ b/solution.py
@@ -90,6 +90,7 @@
     piece = lax.dot_general(
         arrived, deltas, (((0,), (0,)), ((), ())), preferred_element_type=jnp.float32
     )
+    piece, results, input_grads = lax.optimization_barrier((piece, results, input_grads))
     slice_rows = gate_weight.shape[1]
     blocks = piece.reshape(group_total // core_total, core_total, slice_rows, 2 * hidden_total)
     core = lax.axis_index("c")
@@ -120,11 +121,12 @@
     token_grad = jnp.dot(
         token_select, returned[:, feature_total:], preferred_element_type=jnp.float32
     ).astype(jnp.bfloat16)
-    gate_grad = summed[:, :hidden_total][None]
-    up_grad = summed[:, hidden_total:][None]
     pick_wide = pick_rows.reshape(tok_count, top_count, feature_total)
     layer_output = jnp.sum(combine[:, :, None] * pick_wide, axis=1).astype(jnp.bfloat16)
     combine_grad = jnp.sum(upstream_wide[:, None, :] * pick_wide, axis=2)
+    after_tokens = summed + 0.0 * layer_output[0, 0].astype(jnp.float32)
+    gate_grad = after_tokens[:, :hidden_total][None]
+    up_grad = after_tokens[:, hidden_total:][None]
     return (layer_output, token_grad, combine_grad, gate_grad, up_grad)
 
 

time: 276 us -> 271 us (0.982)
  the two profiles are of different devices: /device:TPU:64 before, /device:TPU:1 now
where the time goes in v8:
time: 271 us; the launch traced here: 266 us
  waiting for transfers between devices  183 us (68%)
  starting transfers between devices  24.7 us (9%)
  matrix products  24 us (9%)
  between operations  14.9 us (5%)
  local copies, waits for them, and re-layouts  10.2 us (4%)
  other arithmetic  9.18 us (3%)
    all_to_all x2, waiting for transfers between devices, trade_rows(): lax.all_to_all(buffer, EXPERT_AXES, split_axis=0, concat_axis=0, tiled=True)  104 us
    all_gather x1, waiting for transfers between devices, shards(): full_weights = lax.all_gather(local_weights, DP_AXES, axis=0, tiled=True)  75.1 us
    all_to_all x2, starting transfers between devices, trade_rows(): lax.all_to_all(buffer, EXPERT_AXES, split_axis=0, concat_axis=0, tiled=True)  21.2 us
  transfers between devices with their start and end apart: 5, of which 4 were waited for; matrix products, arithmetic and copies ran while one was open for 6% of the time, Pallas kernels for 0%

profile of v8, /device:TPU:1, one launch (start us, length us, event | category | flops | bytes accessed | tf_op | source)
XLA Modules:
  0.0 265.5 jit_solution(1737882563788633067)
XLA Ops:
  7.2 0.8 copy.32
  8.3 0.8 copy.31
  9.2 0.6 reduce-window.6
  10.1 1.2 broadcast_in_dim.6
  11.6 0.3 mul.87
  11.9 0.7 mul.88
  12.7 3.2 %convolution_convert_fusion = bf16[1024,2048]{1,0:T(8,128)(2,1)} fusion(bf16[256,1024]{1,0:T(8,128)(2,1)S(1)} %multiply_convert_fusion.3, bf16[256,1024]{1,0:T(8,128)(2,1)S(1)} %reshape.84, s32[256]{0:T(256)S(1)} %multiply_add_fusion.1), kind=kOutput, calls=%fused_computation.1 | convolution fusion | flops 1078198272 | bytes 5243904 | tf_op jit(solution)/shard_map/dot_general | solution.py:82
  16.0 13.6 %all-to-all-start = ((bf16[16,64,2048]{2,1,0:T(8,128)(2,1)}), bf16[16,64,2048]{2,1,0:T(8,128)(2,1)}, u32[]{:S(2)}, u32[]{:S(2)}) async-start(bf16[16,64,2048]{2,1,0:T(8,128)(2,1)} %bitcast.35), calls=%async_computation | async-start | bytes 8388608 | tf_op jit(solution)/shard_map/all_to_all | solution.py:41
  29.6 0.2 all-gather.2.cloned.1.call-start
  29.9 0.6 pad_maximum_fusion.4
  30.5 75.1 %all-gather.2.cloned.1.call-done = bf16[1024,1152]{1,0:T(8,128)(2,1)} async-done(((bf16[32,1152]{1,0:T(8,128)(2,1)}), bf16[1024,1152]{1,0:T(8,128)(2,1)}) %all-gather.2.cloned.1.call-update) | async-done | bytes 2359312 | tf_op jit(solution)/shard_map/all_gather | solution.py:65
  105.7 20.1 %all-to-all-done = bf16[16,64,2048]{2,1,0:T(8,128)(2,1)} async-done(((bf16[16,64,2048]{2,1,0:T(8,128)(2,1)}), bf16[16,64,2048]{2,1,0:T(8,128)(2,1)}, u32[]{:S(2)}, u32[]{:S(2)}) %all-to-all-start) | async-done | bytes 4194336 | tf_op jit(solution)/shard_map/all_to_all | solution.py:41
  125.8 4.1 %fusion.8 = f32[1024,768]{0,1:T(8,128)S(1)} fusion(bf16[1024,2048]{1,0:T(8,128)(2,1)} %bitcast.2, bf16[1024,1152]{1,0:T(8,128)(2,1)} %all-gather.2.cloned.1.call-done), kind=kOutput, calls=%fused_computation.12 | convolution fusion | flops 1610612736 | bytes 6815744 | tf_op jit(solution)/shard_map/dot_general | solution.py:16
  129.9 3.1 %multiply_convert_fusion.2 = (bf16[1024,384]{0,1:T(8,128)(2,1)S(1)}, bf16[1024,384]{0,1:T(8,128)(2,1)S(1)}) fusion(f32[1024,768]{0,1:T(8,128)S(1)} %fusion.8, bf16[1024,1152]{1,0:T(8,128)(2,1)S(1)} %copy-done.6, bf16[1024,2048]{1,0:T(8,128)(2,1)} %bitcast.2), kind=kOutput, calls=%fused_computation.19 | convolution fusion | flops 810418176 | bytes 7602176 | tf_op jit(solution)/shard_map/dot_general | solution.py:27
  133.0 5.2 %fusion.6 = f32[1024,768]{1,0:T(8,128)} fusion(bf16[1024,2048]{1,0:T(8,128)(2,1)} %bitcast.2, bf16[1024,384]{0,1:T(8,128)(2,1)S(1)} %get-tuple-element.27, bf16[1024,384]{0,1:T(8,128)(2,1)S(1)} %get-tuple-element.26), kind=kOutput, calls=%fused_computation.10 | convolution fusion | flops 1613758464 | bytes 6815744 | tf_op jit(solution)/shard_map/dot_general | solution.py:90
  138.2 1.3 convolution_convert_fusion.1
  139.6 1.8 convolution_convert_fusion.2
  141.4 2.4 pad_maximum_fusion
  143.8 7.6 %all-to-all-start.1 = ((bf16[16,64,2048]{2,1,0:T(8,128)(2,1)}), bf16[16,64,2048]{2,1,0:T(8,128)(2,1)}, u32[]{:S(2)}, u32[]{:S(2)}) async-start(bf16[16,64,2048]{2,1,0:T(8,128)(2,1)} %bitcast.36), calls=%async_computation.1 | async-start | bytes 8388608 | tf_op jit(solution)/shard_map/all_to_all | solution.py:41
  151.5 2.8 %dynamic-slice_bitcast_fusion = f32[16,32,768]{2,1,0:T(8,128)} fusion(f32[16,2,32,768]{3,2,1,0:T(8,128)} %bitcast.37, s32[]{:T(128)S(6)} %select_n.8), kind=kLoop, calls=%fused_computation.16 | loop fusion | bytes 3145732 | tf_op jit(solution)/shard_map/jit(dynamic_index_in_dim)/squeeze | solution.py:98
  154.3 3.2 %collective-permute-start = (f32[16,32,768]{2,1,0:T(8,128)}, f32[16,32,768]{2,1,0:T(8,128)S(1)}, u32[]{:S(2)}, u32[]{:S(2)}) collective-permute-start(f32[16,32,768]{2,1,0:T(8,128)} %dynamic-slice_bitcast_fusion), channel_id=1, source_target_pairs={{0,16},{16,0},{1,17},{17,1},{2,18},{18,2},{3,19},{19,3},{4,20},{20... | collective-permute-start | bytes 4718600 | tf_op jit(solution)/shard_map/ppermute | solution.py:99
  157.5 3.0 %collective-permute-done = f32[16,32,768]{2,1,0:T(8,128)S(1)} collective-permute-done((f32[16,32,768]{2,1,0:T(8,128)}, f32[16,32,768]{2,1,0:T(8,128)S(1)}, u32[]{:S(2)}, u32[]{:S(2)}) %collective-permute-start) | collective-permute-done | bytes 1572896 | tf_op jit(solution)/shard_map/ppermute | solution.py:99
  160.5 2.8 %bitcast_add_fusion = f32[16,32,768]{2,1,0:T(8,128)} fusion(f32[16,32,768]{2,1,0:T(8,128)S(1)} %collective-permute-done, f32[16,2,32,768]{3,2,1,0:T(8,128)} %bitcast.38, s32[]{:T(128)S(6)} %select_n.7), kind=kLoop, calls=%fused_computation.15 | loop fusion | flops 393216 | bytes 4718596 | tf_op jit(solution)/shard_map/add | solution.py:99
  163.7 84.2 %all-to-all-done.1 = bf16[16,64,2048]{2,1,0:T(8,128)(2,1)} async-done(((bf16[16,64,2048]{2,1,0:T(8,128)(2,1)}), bf16[16,64,2048]{2,1,0:T(8,128)(2,1)}, u32[]{:S(2)}, u32[]{:S(2)}) %all-to-all-start.1) | async-done | bytes 4194336 | tf_op jit(solution)/shard_map/all_to_all | solution.py:41
  247.9 2.4 multiply_reduce_fusion
  250.5 0.6 copy.37
  251.2 0.6 reshape.89
  251.8 1.4 multiply_reduce_fusion.1
  253.2 0.6 slice.61
  254.4 2.7 %fusion.13 = bf16[128,1024]{1,0:T(8,128)(2,1)} fusion(pred[128,1024]{1,0:T(8,128)(4,1)S(1)} %fusion.19, bf16[1024,2048]{1,0:T(8,128)(2,1)} %bitcast.7), kind=kOutput, calls=%fused_computation.24 | convolution fusion | flops 268566528 | bytes 2490368 | tf_op jit(solution)/shard_map/dot_general | solution.py:121
  257.1 0.9 add_bitcast_fusion
  258.0 0.6 slice_bitcast_fusion
  (34 shorter events, 1.7 us)
Async XLA Ops:
  7.2 4.4 %copy-start = (bf16[128,1024]{1,0:T(8,128)(2,1)S(1)}, bf16[128,1024]{1,0:T(8,128)(2,1)}, u32[]{:S(2)}) copy-start(bf16[128,1024]{1,0:T(8,128)(2,1)} %param.10) | copy-start | bytes 786436
  16.0 13.9 %copy-start.2 = (bf16[1,32,384]{2,1,0:T(8,128)(2,1)S(1)}, bf16[1,32,384]{2,1,0:T(8,128)(2,1)}, u32[]{:S(2)}) copy-start(bf16[1,32,384]{2,1,0:T(8,128)(2,1)} %param.13) | copy-start | bytes 73732
  16.0 13.9 %copy-start.3 = (bf16[1,32,384]{2,1,0:T(8,128)(2,1)S(1)}, bf16[1,32,384]{2,1,0:T(8,128)(2,1)}, u32[]{:S(2)}) copy-start(bf16[1,32,384]{2,1,0:T(8,128)(2,1)} %param.12) | copy-start | bytes 73732
  16.0 13.9 %copy-start.4 = (bf16[1,32,384]{2,1,0:T(8,128)(2,1)S(1)}, bf16[1,32,384]{2,1,0:T(8,128)(2,1)}, u32[]{:S(2)}) copy-start(bf16[1,32,384]{2,1,0:T(8,128)(2,1)} %param.11) | copy-start | bytes 73732
  16.0 109.8 %all-to-all-start = ((bf16[16,64,2048]{2,1,0:T(8,128)(2,1)}), bf16[16,64,2048]{2,1,0:T(8,128)(2,1)}, u32[]{:S(2)}, u32[]{:S(2)}) async-start(bf16[16,64,2048]{2,1,0:T(8,128)(2,1)} %bitcast.35), calls=%async_computation | async-start | bytes 8388608 | tf_op jit(solution)/shard_map/all_to_all | solution.py:41
  29.6 76.1 %all-gather.2.cloned.1.call-start = ((), (), s32[]{:S(2)}) async-start(), calls=%async_computation.3 | async-start | bytes 2433024 | tf_op jit(solution)/shard_map/all_gather | solution.py:65
  125.8 4.1 %copy-start.6 = (bf16[1024,1152]{1,0:T(8,128)(2,1)S(1)}, bf16[1024,1152]{1,0:T(8,128)(2,1)}, u32[]{:S(2)}) copy-start(bf16[1024,1152]{1,0:T(8,128)(2,1)} %all-gather.2.cloned.1.call-done) | copy-start | bytes 7077892
  143.8 104.1 %all-to-all-start.1 = ((bf16[16,64,2048]{2,1,0:T(8,128)(2,1)}), bf16[16,64,2048]{2,1,0:T(8,128)(2,1)}, u32[]{:S(2)}, u32[]{:S(2)}) async-start(bf16[16,64,2048]{2,1,0:T(8,128)(2,1)} %bitcast.36), calls=%async_computation.1 | async-start | bytes 8388608 | tf_op jit(solution)/shard_map/all_to_all | solution.py:41
  151.5 105.7 %reduce-scatter.2.cloned.1.call-start = ((), (), s32[]{:S(2)}) async-start(), calls=%async_computation.4 | async-start | bytes 1671168 | tf_op jit(solution)/shard_map/reduce_scatter | solution.py:100
  154.3 6.2 %collective-permute-start = (f32[16,32,768]{2,1,0:T(8,128)}, f32[16,32,768]{2,1,0:T(8,128)S(1)}, u32[]{:S(2)}, u32[]{:S(2)}) collective-permute-start(f32[16,32,768]{2,1,0:T(8,128)} %dynamic-slice_bitcast_fusion), channel_id=1, source_target_pairs={{0,16},{16,0},{1,17},{17,1},{2,18},{18,2},{3,19},{19,3},{4,20},{20... | collective-permute-start | bytes 4718600 | tf_op jit(solution)/shard_map/ppermute | solution.py:99
  157.5 6.0 %copy-start.5 = (s32[128,2]{0,1:T(2,128)S(1)}, s32[128,2]{0,1:T(2,128)}, u32[]{:S(2)}) copy-start(s32[128,2]{0,1:T(2,128)} %param.8) | copy-start | bytes 3076
  253.2 5.5 %copy-start.1 = (bf16[128,1024]{1,0:T(8,128)(2,1)}, bf16[128,1024]{1,0:T(8,128)(2,1)S(1)}, u32[]{:S(2)}) copy-start(bf16[128,1024]{1,0:T(8,128)(2,1)S(1)} %multiply_reduce_fusion.1) | copy-start | bytes 786436
Sparse Core Ops, SparseCore 0:
  33.2 72.4 all-gather.1
  163.4 84.8 reduce-scatter.1

commit v9 on v8

--- a/solution.py
+++ b/solution.py
@@ -90,13 +90,13 @@
     piece = lax.dot_general(
         arrived, deltas, (((0,), (0,)), ((), ())), preferred_element_type=jnp.float32
     )
-    piece, results, input_grads = lax.optimization_barrier((piece, results, input_grads))
     slice_rows = gate_weight.shape[1]
     blocks = piece.reshape(group_total // core_total, core_total, slice_rows, 2 * hidden_total)
     core = lax.axis_index("c")
     own_blocks = lax.dynamic_index_in_dim(blocks, core, axis=1, keepdims=False)
     other_blocks = lax.dynamic_index_in_dim(blocks, 1 - core, axis=1, keepdims=False)
     core_summed = own_blocks + lax.ppermute(other_blocks, "c", perm=[(0, 1), (1, 0)])
+    core_summed, results, input_grads = lax.optimization_barrier((core_summed, results, input_grads))
     summed = lax.psum_scatter(core_summed, CHIP_AXES, scatter_dimension=0, tiled=True)
     summed = summed.reshape(slice_rows, 2 * hidden_total) / group_total
     row_major = Layout(major_to_minor=(0, 1))

time: 271 us -> 285 us (1.052)
  waiting for transfers between devices: 183 us -> 192 us
  matrix products: 24 us -> 28.7 us
    all_to_all x2, waiting for transfers between devices: 104 us -> 116 us  [trade_rows(): lax.all_to_all(buffer, EXPERT_AXES, split_axis=0, concat_axis=0, tiled=True)]
    ppermute x1, waiting for transfers between devices: 2.99 us -> 0.01 us  [shards(): lax.ppermute(other_blocks, 'c', perm=[(0, 1), (1, 0)])]
  transfers between devices with their start and end apart: 5 -> 5, of which waited for: 4 -> 3; matrix products, arithmetic and copies ran while one was open for 6% -> 6% of each run, Pallas kernels for 0% -> 0%
where the time goes in v9:
time: 285 us; the launch traced here: 282 us
  waiting for transfers between devices  192 us (67%)
  matrix products  28.7 us (10%)
  starting transfers between devices  24.4 us (9%)
  between operations  15 us (5%)
  other arithmetic  10.8 us (4%)
  local copies, waits for them, and re-layouts  10.4 us (4%)
    all_to_all x2, waiting for transfers between devices, trade_rows(): lax.all_to_all(buffer, EXPERT_AXES, split_axis=0, concat_axis=0, tiled=True)  116 us
    all_gather x1, waiting for transfers between devices, shards(): full_weights = lax.all_gather(local_weights, DP_AXES, axis=0, tiled=True)  75.7 us
    all_to_all x2, starting transfers between devices, trade_rows(): lax.all_to_all(buffer, EXPERT_AXES, split_axis=0, concat_axis=0, tiled=True)  20.8 us
  transfers between devices with their start and end apart: 5, of which 3 were waited for; matrix products, arithmetic and copies ran while one was open for 6% of the time, Pallas kernels for 0%

profile of v9, /device:TPU:1, one launch (start us, length us, event | category | flops | bytes accessed | tf_op | source)
XLA Modules:
  0.0 281.7 jit_solution(13583971754128386537)
XLA Ops:
  7.2 0.8 copy.32
  8.3 0.8 copy.31
  9.2 0.6 reduce-window.6
  10.1 1.2 broadcast_in_dim.6
  11.6 0.3 mul.87
  11.9 0.7 mul.88
  12.7 3.4 %convolution_convert_fusion = bf16[1024,2048]{1,0:T(8,128)(2,1)} fusion(bf16[256,1024]{1,0:T(8,128)(2,1)S(1)} %multiply_convert_fusion.3, bf16[256,1024]{1,0:T(8,128)(2,1)S(1)} %reshape.84, s32[256]{0:T(256)S(1)} %multiply_add_fusion.1), kind=kOutput, calls=%fused_computation.1 | convolution fusion | flops 1078198272 | bytes 5243904 | tf_op jit(solution)/shard_map/dot_general | solution.py:82
  16.1 13.6 %all-to-all-start = ((bf16[16,64,2048]{2,1,0:T(8,128)(2,1)}), bf16[16,64,2048]{2,1,0:T(8,128)(2,1)}, u32[]{:S(2)}, u32[]{:S(2)}) async-start(bf16[16,64,2048]{2,1,0:T(8,128)(2,1)} %bitcast.35), calls=%async_computation | async-start | bytes 8388608 | tf_op jit(solution)/shard_map/all_to_all | solution.py:41
  29.8 0.6 pad_maximum_fusion.4
  30.5 75.7 %all-gather.2.cloned.1.call-done = bf16[1024,1152]{1,0:T(8,128)(2,1)} async-done(((bf16[32,1152]{1,0:T(8,128)(2,1)}), bf16[1024,1152]{1,0:T(8,128)(2,1)}) %all-gather.2.cloned.1.call-update) | async-done | bytes 2359312 | tf_op jit(solution)/shard_map/all_gather | solution.py:65
  106.2 19.7 %all-to-all-done = bf16[16,64,2048]{2,1,0:T(8,128)(2,1)} async-done(((bf16[16,64,2048]{2,1,0:T(8,128)(2,1)}), bf16[16,64,2048]{2,1,0:T(8,128)(2,1)}, u32[]{:S(2)}, u32[]{:S(2)}) %all-to-all-start) | async-done | bytes 4194336 | tf_op jit(solution)/shard_map/all_to_all | solution.py:41
  125.9 3.9 %fusion.8 = f32[1024,768]{0,1:T(8,128)S(1)} fusion(bf16[1024,2048]{1,0:T(8,128)(2,1)} %bitcast.2, bf16[1024,1152]{1,0:T(8,128)(2,1)} %all-gather.2.cloned.1.call-done), kind=kOutput, calls=%fused_computation.12 | convolution fusion | flops 1610612736 | bytes 6815744 | tf_op jit(solution)/shard_map/dot_general | solution.py:16
  129.9 4.4 %multiply_convert_fusion.2 = (bf16[1024,384]{0,1:T(8,128)(2,1)S(1)}, bf16[1024,384]{0,1:T(8,128)(2,1)S(1)}) fusion(f32[1024,768]{0,1:T(8,128)S(1)} %fusion.8, bf16[1024,1152]{1,0:T(8,128)(2,1)} %all-gather.2.cloned.1.call-done, bf16[1024,2048]{1,0:T(8,128)(2,1)} %bitcast.2), kind=kOutput, calls=%fused_computation.19 | convolution fusion | flops 810418176 | bytes 7602176 | tf_op jit(solution)/shard_map/dot_general | solution.py:27
  134.3 4.0 %fusion.6 = f32[1024,768]{1,0:T(8,128)S(1)} fusion(bf16[1024,2048]{1,0:T(8,128)(2,1)} %bitcast.2, bf16[1024,384]{0,1:T(8,128)(2,1)S(1)} %get-tuple-element.27, bf16[1024,384]{0,1:T(8,128)(2,1)S(1)} %get-tuple-element.26), kind=kOutput, calls=%fused_computation.10 | convolution fusion | flops 1613758464 | bytes 6815744 | tf_op jit(solution)/shard_map/dot_general | solution.py:90
  138.4 1.7 copy-done
  140.0 1.3 dynamic-slice_bitcast_fusion
  141.3 3.5 %collective-permute-start = (f32[16,32,768]{2,1,0:T(8,128)}, f32[16,32,768]{2,1,0:T(8,128)}, u32[]{:S(2)}, u32[]{:S(2)}) collective-permute-start(f32[16,32,768]{2,1,0:T(8,128)} %dynamic-slice_bitcast_fusion), channel_id=1, source_target_pairs={{0,16},{16,0},{1,17},{17,1},{2,18},{18,2},{3,19},{19,3},{4,20},{20... | collective-permute-start | bytes 4718600 | tf_op jit(solution)/shard_map/ppermute | solution.py:98
  144.9 3.9 %convolution_convert_fusion.2 = bf16[1024,1024]{1,0:T(8,128)(2,1)S(1)} fusion(bf16[1024,1152]{1,0:T(8,128)(2,1)} %all-gather.2.cloned.1.call-done, bf16[1024,384]{0,1:T(8,128)(2,1)} %copy-done.11, bf16[1024,384]{0,1:T(8,128)(2,1)} %copy-done.10), kind=kOutput, calls=%fused_computation.9 | convolution fusion | flops 1614807040 | bytes 5242880 | tf_op jit(solution)/shard_map/dot_general | solution.py:34
  148.8 3.9 %convolution_convert_fusion.1 = bf16[1024,1024]{1,0:T(8,128)(2,1)} fusion(f32[1024,768]{0,1:T(8,128)S(1)} %copy-done.9, bf16[1024,1152]{1,0:T(8,128)(2,1)} %all-gather.2.cloned.1.call-done), kind=kOutput, calls=%fused_computation.8 | convolution fusion | flops 808714240 | bytes 6029312 | tf_op jit(solution)/shard_map/dot_general | solution.py:20
  152.7 2.9 %bitcast_add_fusion = f32[16,32,768]{2,1,0:T(8,128)} fusion(f32[16,32,768]{2,1,0:T(8,128)} %collective-permute-done, f32[16,2,32,768]{3,2,1,0:T(8,128)S(1)} %bitcast.38, s32[]{:T(128)S(6)} %select_n.7), kind=kLoop, calls=%fused_computation.15 | loop fusion | flops 393216 | bytes 4718596 | tf_op jit(solution)/shard_map/add | solution.py:98
  155.6 4.0 %pad_maximum_fusion = bf16[1024,2048]{1,0:T(8,128)(2,1)} fusion(bf16[1024,1024]{1,0:T(8,128)(2,1)S(1)} %convolution_convert_fusion.2, bf16[1024,1024]{1,0:T(8,128)(2,1)} %convolution_convert_fusion.1), kind=kLoop, calls=%fused_computation | loop fusion | flops 8388608 | bytes 8388608 | tf_op jit(solution)/shard_map/concatenate | solution.py:103
  159.6 7.2 %all-to-all-start.1 = ((bf16[16,64,2048]{2,1,0:T(8,128)(2,1)}), bf16[16,64,2048]{2,1,0:T(8,128)(2,1)}, u32[]{:S(2)}, u32[]{:S(2)}) async-start(bf16[16,64,2048]{2,1,0:T(8,128)(2,1)} %bitcast.36), calls=%async_computation.1 | async-start | bytes 8388608 | tf_op jit(solution)/shard_map/all_to_all | solution.py:41
  166.8 0.7 reduce-scatter.2.cloned.1.call-update
  167.9 96.2 %all-to-all-done.1 = bf16[16,64,2048]{2,1,0:T(8,128)(2,1)} async-done(((bf16[16,64,2048]{2,1,0:T(8,128)(2,1)}), bf16[16,64,2048]{2,1,0:T(8,128)(2,1)}, u32[]{:S(2)}, u32[]{:S(2)}) %all-to-all-start.1) | async-done | bytes 4194336 | tf_op jit(solution)/shard_map/all_to_all | solution.py:41
  264.1 2.4 multiply_reduce_fusion
  266.7 0.6 copy.37
  267.4 0.6 reshape.90
  268.0 1.4 multiply_reduce_fusion.1
  269.4 0.6 slice.61
  270.6 2.7 fusion.13
  273.3 0.9 add_bitcast_fusion
  274.2 0.6 slice_bitcast_fusion
  (44 shorter events, 1.7 us)
Async XLA Ops:
  7.2 4.4 %copy-start.2 = (bf16[128,1024]{1,0:T(8,128)(2,1)S(1)}, bf16[128,1024]{1,0:T(8,128)(2,1)}, u32[]{:S(2)}) copy-start(bf16[128,1024]{1,0:T(8,128)(2,1)} %param.10) | copy-start | bytes 786436
  16.1 13.7 %copy-start.4 = (bf16[1,32,384]{2,1,0:T(8,128)(2,1)S(1)}, bf16[1,32,384]{2,1,0:T(8,128)(2,1)}, u32[]{:S(2)}) copy-start(bf16[1,32,384]{2,1,0:T(8,128)(2,1)} %param.13) | copy-start | bytes 73732
  16.1 13.7 %copy-start.5 = (bf16[1,32,384]{2,1,0:T(8,128)(2,1)S(1)}, bf16[1,32,384]{2,1,0:T(8,128)(2,1)}, u32[]{:S(2)}) copy-start(bf16[1,32,384]{2,1,0:T(8,128)(2,1)} %param.12) | copy-start | bytes 73732
  16.1 13.7 %copy-start.6 = (bf16[1,32,384]{2,1,0:T(8,128)(2,1)S(1)}, bf16[1,32,384]{2,1,0:T(8,128)(2,1)}, u32[]{:S(2)}) copy-start(bf16[1,32,384]{2,1,0:T(8,128)(2,1)} %param.11) | copy-start | bytes 73732
  16.1 109.8 %all-to-all-start = ((bf16[16,64,2048]{2,1,0:T(8,128)(2,1)}), bf16[16,64,2048]{2,1,0:T(8,128)(2,1)}, u32[]{:S(2)}, u32[]{:S(2)}) async-start(bf16[16,64,2048]{2,1,0:T(8,128)(2,1)} %bitcast.35), calls=%async_computation | async-start | bytes 8388608 | tf_op jit(solution)/shard_map/all_to_all | solution.py:41
  29.7 76.5 %all-gather.2.cloned.1.call-start = ((), (), s32[]{:S(2)}) async-start(), calls=%async_computation.3 | async-start | bytes 2433024 | tf_op jit(solution)/shard_map/all_gather | solution.py:65
  129.8 4.4 %copy-start.8 = (f32[1024,768]{0,1:T(8,128)}, f32[1024,768]{0,1:T(8,128)S(1)}, u32[]{:S(2)}) copy-start(f32[1024,768]{0,1:T(8,128)S(1)} %fusion.8) | copy-start | bytes 9437188
  134.3 4.1 %copy-start.10 = (bf16[1024,384]{0,1:T(8,128)(2,1)}, bf16[1024,384]{0,1:T(8,128)(2,1)S(1)}, u32[]{:S(2)}) copy-start(bf16[1024,384]{0,1:T(8,128)(2,1)S(1)} %get-tuple-element.26) | copy-start | bytes 2359300
  134.3 4.1 %copy-start.11 = (bf16[1024,384]{0,1:T(8,128)(2,1)}, bf16[1024,384]{0,1:T(8,128)(2,1)S(1)}, u32[]{:S(2)}) copy-start(bf16[1024,384]{0,1:T(8,128)(2,1)S(1)} %get-tuple-element.27) | copy-start | bytes 2359300
  138.4 1.7 copy-start
  141.3 11.4 %collective-permute-start = (f32[16,32,768]{2,1,0:T(8,128)}, f32[16,32,768]{2,1,0:T(8,128)}, u32[]{:S(2)}, u32[]{:S(2)}) collective-permute-start(f32[16,32,768]{2,1,0:T(8,128)} %dynamic-slice_bitcast_fusion), channel_id=1, source_target_pairs={{0,16},{16,0},{1,17},{17,1},{2,18},{18,2},{3,19},{19,3},{4,20},{20... | collective-permute-start | bytes 4718600 | tf_op jit(solution)/shard_map/ppermute | solution.py:98
  144.8 3.9 %copy-start.9 = (f32[1024,768]{0,1:T(8,128)S(1)}, f32[1024,768]{0,1:T(8,128)}, u32[]{:S(2)}) copy-start(f32[1024,768]{0,1:T(8,128)} %copy-done.8) | copy-start | bytes 9437188
  148.7 4.0 %copy-start.1 = (f32[1024,768]{1,0:T(8,128)S(1)}, f32[1024,768]{1,0:T(8,128)}, u32[]{:S(2)}) copy-start(f32[1024,768]{1,0:T(8,128)} %copy-done) | copy-start | bytes 9437188
  159.6 8.2 %copy-start.7 = (s32[128,2]{0,1:T(2,128)S(1)}, s32[128,2]{0,1:T(2,128)}, u32[]{:S(2)}) copy-start(s32[128,2]{0,1:T(2,128)} %param.8) | copy-start | bytes 3076
  159.6 104.6 %all-to-all-start.1 = ((bf16[16,64,2048]{2,1,0:T(8,128)(2,1)}), bf16[16,64,2048]{2,1,0:T(8,128)(2,1)}, u32[]{:S(2)}, u32[]{:S(2)}) async-start(bf16[16,64,2048]{2,1,0:T(8,128)(2,1)} %bitcast.36), calls=%async_computation.1 | async-start | bytes 8388608 | tf_op jit(solution)/shard_map/all_to_all | solution.py:41
  166.8 106.6 %reduce-scatter.2.cloned.1.call-start = ((), (), s32[]{:S(2)}) async-start(), calls=%async_computation.4 | async-start | bytes 1671168 | tf_op jit(solution)/shard_map/reduce_scatter | solution.py:100
  269.4 5.5 %copy-start.3 = (bf16[128,1024]{1,0:T(8,128)(2,1)}, bf16[128,1024]{1,0:T(8,128)(2,1)S(1)}, u32[]{:S(2)}) copy-start(bf16[128,1024]{1,0:T(8,128)(2,1)S(1)} %multiply_reduce_fusion.1) | copy-start | bytes 786436
Sparse Core Ops, SparseCore 0:
  33.3 72.8 all-gather.1
  170.5 87.7 reduce-scatter.1

commit v10 on v9

--- a/solution.py
+++ b/solution.py
@@ -96,7 +96,6 @@
     own_blocks = lax.dynamic_index_in_dim(blocks, core, axis=1, keepdims=False)
     other_blocks = lax.dynamic_index_in_dim(blocks, 1 - core, axis=1, keepdims=False)
     core_summed = own_blocks + lax.ppermute(other_blocks, "c", perm=[(0, 1), (1, 0)])
-    core_summed, results, input_grads = lax.optimization_barrier((core_summed, results, input_grads))
     summed = lax.psum_scatter(core_summed, CHIP_AXES, scatter_dimension=0, tiled=True)
     summed = summed.reshape(slice_rows, 2 * hidden_total) / group_total
     row_major = Layout(major_to_minor=(0, 1))

time: 285 us -> 267 us (0.937)
  the two profiles are of different devices: /device:TPU:1 before, /device:TPU:64 now
where the time goes in v10:
time: 267 us
  waiting for transfers between devices  186 us (70%)
  starting transfers between devices  23.5 us (9%)
  matrix products  22.2 us (8%)
  between operations  14.9 us (6%)
  local copies, waits for them, and re-layouts  10.5 us (4%)
  other arithmetic  9.18 us (3%)
    all_to_all x2, waiting for transfers between devices, trade_rows(): lax.all_to_all(buffer, EXPERT_AXES, split_axis=0, concat_axis=0, tiled=True)  92.1 us
    all_gather x1, waiting for transfers between devices, shards(): full_weights = lax.all_gather(local_weights, DP_AXES, axis=0, tiled=True)  82.3 us
    all_to_all x2, starting transfers between devices, trade_rows(): lax.all_to_all(buffer, EXPERT_AXES, split_axis=0, concat_axis=0, tiled=True)  21.4 us
    reduce_scatter x1, waiting for transfers between devices, shards(): lax.psum_scatter(core_summed, CHIP_AXES, scatter_dimension=0, tiled=True)  8.39 us
  transfers between devices with their start and end apart: 5, of which 5 were waited for; matrix products, arithmetic and copies ran while one was open for 6% of the time, Pallas kernels for 0%

profile of v10, /device:TPU:64, one launch (start us, length us, event | category | flops | bytes accessed | tf_op | source)
XLA Modules:
  0.0 266.7 jit_solution(5991748895216023546)
XLA Ops:
  7.2 0.8 copy.32
  8.3 0.8 copy.31
  9.2 0.6 reduce-window.6
  10.1 1.2 broadcast_in_dim.6
  11.9 0.7 mul.88
  12.7 3.2 %convolution_convert_fusion = bf16[1024,2048]{1,0:T(8,128)(2,1)} fusion(bf16[256,1024]{1,0:T(8,128)(2,1)S(1)} %multiply_convert_fusion.3, bf16[256,1024]{1,0:T(8,128)(2,1)S(1)} %reshape.84, s32[256]{0:T(256)S(1)} %multiply_add_fusion.1), kind=kOutput, calls=%fused_computation.1 | convolution fusion | flops 1078198272 | bytes 5243904 | tf_op jit(solution)/shard_map/dot_general | solution.py:82
  15.9 12.6 %all-to-all-start = ((bf16[16,64,2048]{2,1,0:T(8,128)(2,1)}), bf16[16,64,2048]{2,1,0:T(8,128)(2,1)}, u32[]{:S(2)}, u32[]{:S(2)}) async-start(bf16[16,64,2048]{2,1,0:T(8,128)(2,1)} %bitcast.35), calls=%async_computation | async-start | bytes 8388608 | tf_op jit(solution)/shard_map/all_to_all | solution.py:41
  28.6 0.6 pad_maximum_fusion.4
  29.2 82.3 %all-gather.2.cloned.1.call-done = bf16[1024,1152]{1,0:T(8,128)(2,1)} async-done(((bf16[32,1152]{1,0:T(8,128)(2,1)}), bf16[1024,1152]{1,0:T(8,128)(2,1)}) %all-gather.2.cloned.1.call-update) | async-done | bytes 2359312 | tf_op jit(solution)/shard_map/all_gather | solution.py:65
  111.6 12.1 %all-to-all-done = bf16[16,64,2048]{2,1,0:T(8,128)(2,1)} async-done(((bf16[16,64,2048]{2,1,0:T(8,128)(2,1)}), bf16[16,64,2048]{2,1,0:T(8,128)(2,1)}, u32[]{:S(2)}, u32[]{:S(2)}) %all-to-all-start) | async-done | bytes 4194336 | tf_op jit(solution)/shard_map/all_to_all | solution.py:41
  123.7 4.1 %fusion.8 = f32[1024,768]{0,1:T(8,128)S(1)} fusion(bf16[1024,2048]{1,0:T(8,128)(2,1)} %bitcast.2, bf16[1024,1152]{1,0:T(8,128)(2,1)} %all-gather.2.cloned.1.call-done), kind=kOutput, calls=%fused_computation.12 | convolution fusion | flops 1610612736 | bytes 6815744 | tf_op jit(solution)/shard_map/dot_general | solution.py:16
  127.8 3.1 %multiply_convert_fusion.1 = (bf16[1024,384]{0,1:T(8,128)(2,1)S(1)}, bf16[1024,384]{0,1:T(8,128)(2,1)S(1)}) fusion(f32[1024,768]{0,1:T(8,128)S(1)} %fusion.8, bf16[1024,1152]{1,0:T(8,128)(2,1)S(1)} %copy-done.7, bf16[1024,2048]{1,0:T(8,128)(2,1)} %bitcast.2), kind=kOutput, calls=%fused_computation.18 | convolution fusion | flops 810418176 | bytes 7602176 | tf_op jit(solution)/shard_map/dot_general | solution.py:27
  130.9 1.3 convolution_convert_fusion.1
  132.2 1.9 convolution_convert_fusion.2
  134.1 2.4 pad_maximum_fusion
  136.5 8.8 %all-to-all-start.1 = ((bf16[16,64,2048]{2,1,0:T(8,128)(2,1)}), bf16[16,64,2048]{2,1,0:T(8,128)(2,1)}, u32[]{:S(2)}, u32[]{:S(2)}) async-start(bf16[16,64,2048]{2,1,0:T(8,128)(2,1)} %bitcast.36), calls=%async_computation.1 | async-start | bytes 8388608 | tf_op jit(solution)/shard_map/all_to_all | solution.py:41
  145.5 3.5 %fusion.6 = f32[1024,768]{1,0:T(8,128)S(1)} fusion(bf16[1024,2048]{1,0:T(8,128)(2,1)} %bitcast.2, bf16[1024,384]{0,1:T(8,128)(2,1)S(1)} %get-tuple-element.21, bf16[1024,384]{0,1:T(8,128)(2,1)S(1)} %get-tuple-element.20), kind=kOutput, calls=%fused_computation.10 | convolution fusion | flops 1613758464 | bytes 6815744 | tf_op jit(solution)/shard_map/dot_general | solution.py:90
  149.0 1.7 copy-done
  150.8 1.3 dynamic-slice_bitcast_fusion
  152.1 1.9 collective-permute-start
  154.0 3.6 %collective-permute-done = f32[16,32,768]{2,1,0:T(8,128)S(1)} collective-permute-done((f32[16,32,768]{2,1,0:T(8,128)}, f32[16,32,768]{2,1,0:T(8,128)S(1)}, u32[]{:S(2)}, u32[]{:S(2)}) %collective-permute-start) | collective-permute-done | bytes 1572896 | tf_op jit(solution)/shard_map/ppermute | solution.py:98
  157.6 2.8 %bitcast_add_fusion = f32[16,32,768]{2,1,0:T(8,128)} fusion(f32[16,32,768]{2,1,0:T(8,128)S(1)} %collective-permute-done, f32[16,2,32,768]{3,2,1,0:T(8,128)} %bitcast.38, s32[]{:T(128)S(6)} %select_n.7), kind=kLoop, calls=%fused_computation.15 | loop fusion | flops 393216 | bytes 4718596 | tf_op jit(solution)/shard_map/add | solution.py:98
  160.8 80.0 %all-to-all-done.1 = bf16[16,64,2048]{2,1,0:T(8,128)(2,1)} async-done(((bf16[16,64,2048]{2,1,0:T(8,128)(2,1)}), bf16[16,64,2048]{2,1,0:T(8,128)(2,1)}, u32[]{:S(2)}, u32[]{:S(2)}) %all-to-all-start.1) | async-done | bytes 4194336 | tf_op jit(solution)/shard_map/all_to_all | solution.py:41
  240.8 2.4 multiply_reduce_fusion
  243.4 0.6 copy.37
  244.0 0.6 reshape.89
  244.6 1.4 multiply_reduce_fusion.1
  246.0 0.6 slice.61
  247.2 2.8 %fusion.13 = bf16[128,1024]{1,0:T(8,128)(2,1)} fusion(pred[128,1024]{1,0:T(8,128)(4,1)S(1)} %fusion.19, bf16[1024,2048]{1,0:T(8,128)(2,1)} %bitcast.7), kind=kOutput, calls=%fused_computation.24 | convolution fusion | flops 268566528 | bytes 2490368 | tf_op jit(solution)/shard_map/dot_general | solution.py:120
  250.0 8.4 %reduce-scatter.2.cloned.1.call-done = f32[1,32,768]{2,1,0:T(8,128)} async-done(((f32[16,32,768]{2,1,0:T(8,128)}), f32[1,32,768]{2,1,0:T(8,128)}) %reduce-scatter.2.cloned.1.call-update) | async-done | bytes 98320 | tf_op jit(solution)/shard_map/reduce_scatter | solution.py:99
  258.4 0.9 add_bitcast_fusion
  259.3 0.6 slice_bitcast_fusion
  (36 shorter events, 2.2 us)
Async XLA Ops:
  7.2 4.4 %copy-start.1 = (bf16[128,1024]{1,0:T(8,128)(2,1)S(1)}, bf16[128,1024]{1,0:T(8,128)(2,1)}, u32[]{:S(2)}) copy-start(bf16[128,1024]{1,0:T(8,128)(2,1)} %param.10) | copy-start | bytes 786436
  15.9 12.6 %copy-start.3 = (bf16[1,32,384]{2,1,0:T(8,128)(2,1)S(1)}, bf16[1,32,384]{2,1,0:T(8,128)(2,1)}, u32[]{:S(2)}) copy-start(bf16[1,32,384]{2,1,0:T(8,128)(2,1)} %param.13) | copy-start | bytes 73732
  15.9 12.6 %copy-start.4 = (bf16[1,32,384]{2,1,0:T(8,128)(2,1)S(1)}, bf16[1,32,384]{2,1,0:T(8,128)(2,1)}, u32[]{:S(2)}) copy-start(bf16[1,32,384]{2,1,0:T(8,128)(2,1)} %param.12) | copy-start | bytes 73732
  15.9 12.6 %copy-start.5 = (bf16[1,32,384]{2,1,0:T(8,128)(2,1)S(1)}, bf16[1,32,384]{2,1,0:T(8,128)(2,1)}, u32[]{:S(2)}) copy-start(bf16[1,32,384]{2,1,0:T(8,128)(2,1)} %param.11) | copy-start | bytes 73732
  15.9 107.8 %all-to-all-start = ((bf16[16,64,2048]{2,1,0:T(8,128)(2,1)}), bf16[16,64,2048]{2,1,0:T(8,128)(2,1)}, u32[]{:S(2)}, u32[]{:S(2)}) async-start(bf16[16,64,2048]{2,1,0:T(8,128)(2,1)} %bitcast.35), calls=%async_computation | async-start | bytes 8388608 | tf_op jit(solution)/shard_map/all_to_all | solution.py:41
  28.5 83.1 %all-gather.2.cloned.1.call-start = ((), (), s32[]{:S(2)}) async-start(), calls=%async_computation.3 | async-start | bytes 2433024 | tf_op jit(solution)/shard_map/all_gather | solution.py:65
  123.7 4.1 %copy-start.7 = (bf16[1024,1152]{1,0:T(8,128)(2,1)S(1)}, bf16[1024,1152]{1,0:T(8,128)(2,1)}, u32[]{:S(2)}) copy-start(bf16[1024,1152]{1,0:T(8,128)(2,1)} %all-gather.2.cloned.1.call-done) | copy-start | bytes 7077892
  136.5 104.3 %all-to-all-start.1 = ((bf16[16,64,2048]{2,1,0:T(8,128)(2,1)}), bf16[16,64,2048]{2,1,0:T(8,128)(2,1)}, u32[]{:S(2)}, u32[]{:S(2)}) async-start(bf16[16,64,2048]{2,1,0:T(8,128)(2,1)} %bitcast.36), calls=%async_computation.1 | async-start | bytes 8388608 | tf_op jit(solution)/shard_map/all_to_all | solution.py:41
  145.3 113.1 %reduce-scatter.2.cloned.1.call-start = ((), (), s32[]{:S(2)}) async-start(), calls=%async_computation.4 | async-start | bytes 1671168 | tf_op jit(solution)/shard_map/reduce_scatter | solution.py:99
  149.0 1.8 copy-start
  152.1 5.5 %collective-permute-start = (f32[16,32,768]{2,1,0:T(8,128)}, f32[16,32,768]{2,1,0:T(8,128)S(1)}, u32[]{:S(2)}, u32[]{:S(2)}) collective-permute-start(f32[16,32,768]{2,1,0:T(8,128)} %dynamic-slice_bitcast_fusion), channel_id=1, source_target_pairs={{0,16},{16,0},{1,17},{17,1},{2,18},{18,2},{3,19},{19,3},{4,20},{20... | collective-permute-start | bytes 4718600 | tf_op jit(solution)/shard_map/ppermute | solution.py:98
  154.0 6.6 %copy-start.6 = (s32[128,2]{0,1:T(2,128)S(1)}, s32[128,2]{0,1:T(2,128)}, u32[]{:S(2)}) copy-start(s32[128,2]{0,1:T(2,128)} %param.8) | copy-start | bytes 3076
  246.0 13.9 %copy-start.2 = (bf16[128,1024]{1,0:T(8,128)(2,1)}, bf16[128,1024]{1,0:T(8,128)(2,1)S(1)}, u32[]{:S(2)}) copy-start(bf16[128,1024]{1,0:T(8,128)(2,1)S(1)} %multiply_reduce_fusion.1) | copy-start | bytes 786436
Sparse Core Ops, SparseCore 0:
  32.1 79.4 all-gather.1
  160.5 97.8 reduce-scatter.1

commit v11 on v10

--- a/solution.py
+++ b/solution.py
@@ -35,6 +35,37 @@
         deltas, stacked, (((1,), (1,)), ((), ())), preferred_element_type=jnp.float32
     )
     return (input_grads.astype(jnp.bfloat16), deltas)
+
+
+def swap_partner(values, axis):
+    return lax.ppermute(values, axis, perm=[(0, 1), (1, 0)])
+
+
+def ring_gather(values, axis, size):
+    me = lax.axis_index(axis)
+    held = [values]
+    moving = values
+    for _ in range(size - 1):
+        moving = lax.ppermute(moving, axis, perm=[(i, (i + 1) % size) for i in range(size)])
+        held.append(moving)
+    stacked = jnp.stack(held)
+    order = (me - jnp.arange(size, dtype=jnp.int32)) % size
+    return jnp.take(stacked, order, axis=0)
+
+
+def ring_reduce_scatter(blocks, axis, size):
+    me = lax.axis_index(axis)
+    carry = lax.dynamic_index_in_dim(blocks, (me - 1) % size, axis=0, keepdims=False)
+    for hop in range(size - 1):
+        arrived = lax.ppermute(carry, axis, perm=[(i, (i + 1) % size) for i in range(size)])
+        own = lax.dynamic_index_in_dim(blocks, (me - hop - 2) % size, axis=0, keepdims=False)
+        carry = arrived + own
+    return carry
+
+
+def ordered_pair(own, other, axis):
+    first = lax.axis_index(axis) == 0
+    return jnp.stack([jnp.where(first, own, other), jnp.where(first, other, own)])
 
 
 def trade_rows(buffer):
@@ -62,7 +93,11 @@
     core_total = lax.axis_size("c")
     capacity = max(tok_count // 2, top_count * tok_count // expert_total + tok_count // 4)
     local_weights = jnp.concatenate([gate_weight[0], up_weight[0], down_weight[0]], axis=1)
-    full_weights = lax.all_gather(local_weights, DP_AXES, axis=0, tiled=True)
+    y_size = lax.axis_size("y")
+    along_y = ring_gather(local_weights, "y", y_size)
+    along_xl = ordered_pair(along_y, swap_partner(along_y, "xl"), "xl")
+    along_c = ordered_pair(along_xl, swap_partner(along_xl, "c"), "c")
+    full_weights = jnp.transpose(along_c, (2, 1, 0, 3, 4)).reshape(-1, local_weights.shape[1])
     gate_full = full_weights[:, :hidden_total]
     up_full = full_weights[:, hidden_total : 2 * hidden_total]
     down_full = full_weights[:, 2 * hidden_total :]
@@ -96,7 +131,12 @@
     own_blocks = lax.dynamic_index_in_dim(blocks, core, axis=1, keepdims=False)
     other_blocks = lax.dynamic_index_in_dim(blocks, 1 - core, axis=1, keepdims=False)
     core_summed = own_blocks + lax.ppermute(other_blocks, "c", perm=[(0, 1), (1, 0)])
-    summed = lax.psum_scatter(core_summed, CHIP_AXES, scatter_dimension=0, tiled=True)
+    by_xl = core_summed.reshape(y_size, lax.axis_size("xl"), slice_rows, 2 * hidden_total)
+    xl = lax.axis_index("xl")
+    keep_xl = lax.dynamic_index_in_dim(by_xl, xl, axis=1, keepdims=False)
+    send_xl = lax.dynamic_index_in_dim(by_xl, 1 - xl, axis=1, keepdims=False)
+    xl_summed = keep_xl + swap_partner(send_xl, "xl")
+    summed = ring_reduce_scatter(xl_summed, "y", y_size)
     summed = summed.reshape(slice_rows, 2 * hidden_total) / group_total
     row_major = Layout(major_to_minor=(0, 1))
     back = jnp.concatenate(

time: 267 us -> 248 us (0.929)
  the two profiles are of different devices: /device:TPU:64 before, /device:TPU:1 now
where the time goes in v11:
time: 248 us; the launch traced here: 245 us
  waiting for transfers between devices  138 us (56%)
  starting transfers between devices  62.9 us (25%)
  matrix products  21.6 us (9%)
  other arithmetic  10.2 us (4%)
  local copies, waits for them, and re-layouts  10.1 us (4%)
    ppermute x3, waiting for transfers between devices, swap_partner(): return lax.ppermute(values, axis, perm=[(0, 1), (1, 0)])  50 us
    ppermute x7, waiting for transfers between devices, ring_gather(): lax.ppermute(moving, axis, perm=[(i, (i + 1) % size) for i in range(size)])  32.5 us
    ppermute x7, waiting for transfers between devices, ring_reduce_scatter(): lax.ppermute(carry, axis, perm=[(i, (i + 1) % size) for i in range(size)])  29.8 us
    all_to_all x2, waiting for transfers between devices, trade_rows(): lax.all_to_all(buffer, EXPERT_AXES, split_axis=0, concat_axis=0, tiled=True)  22.9 us
    all_to_all x2, starting transfers between devices, trade_rows(): lax.all_to_all(buffer, EXPERT_AXES, split_axis=0, concat_axis=0, tiled=True)  21.4 us
    ppermute x7, starting transfers between devices, ring_reduce_scatter(): lax.ppermute(carry, axis, perm=[(i, (i + 1) % size) for i in range(size)])  14.9 us
    ppermute x7, starting transfers between devices, ring_gather(): lax.ppermute(moving, axis, perm=[(i, (i + 1) % size) for i in range(size)])  14.7 us
    ppermute x3, starting transfers between devices, swap_partner(): return lax.ppermute(values, axis, perm=[(0, 1), (1, 0)])  8.98 us
  transfers between devices with their start and end apart: 20, of which 19 were waited for; matrix products, arithmetic and copies ran while one was open for 8% of the time, Pallas kernels for 0%

profile of v11, /device:TPU:1, one launch (start us, length us, event | category | flops | bytes accessed | tf_op | source)
XLA Modules:
  0.0 245.3 jit_solution(5278576235076449395)
XLA Ops:
  6.2 3.2 %convolution_convert_fusion = bf16[1024,2048]{1,0:T(8,128)(2,1)} fusion(bf16[256,1024]{1,0:T(8,128)(2,1)S(1)} %multiply_convert_fusion.3, bf16[256,1024]{1,0:T(8,128)(2,1)S(1)} %reshape.139, s32[256]{0:T(256)S(1)} %multiply_add_fusion.1), kind=kOutput, calls=%fused_computation.2 | convolution fusion | flops 1078198272 | bytes 5243904 | tf_op jit(solution)/shard_map/dot_general | solution.py:117
  9.4 13.6 %all-to-all-start = ((bf16[16,64,2048]{2,1,0:T(8,128)(2,1)}), bf16[16,64,2048]{2,1,0:T(8,128)(2,1)}, u32[]{:S(2)}, u32[]{:S(2)}) async-start(bf16[16,64,2048]{2,1,0:T(8,128)(2,1)} %bitcast.91), calls=%async_computation | async-start | bytes 8388608 | tf_op jit(solution)/shard_map/all_to_all | solution.py:72
  23.1 3.2 %collective-permute-start = (bf16[32,1152]{1,0:T(8,128)(2,1)S(1)}, bf16[32,1152]{1,0:T(8,128)(2,1)S(1)}, u32[]{:S(2)}, u32[]{:S(2)}) collective-permute-start(bf16[32,1152]{1,0:T(8,128)(2,1)S(1)} %pad_maximum_fusion.6), channel_id=1, source_target_pairs={{0,64},{64,128},{128,192},{192,256},{256,320},{320,384},{384,448},... | collective-permute-start | bytes 221192 | tf_op jit(solution)/shard_map/ppermute | solution.py:49
  26.4 3.9 %collective-permute-done = bf16[32,1152]{1,0:T(8,128)(2,1)S(1)} collective-permute-done((bf16[32,1152]{1,0:T(8,128)(2,1)S(1)}, bf16[32,1152]{1,0:T(8,128)(2,1)S(1)}, u32[]{:S(2)}, u32[]{:S(2)}) %collective-permute-start) | collective-permute-done | bytes 73760 | tf_op jit(solution)/shard_map/ppermute | solution.py:49
  32.3 4.8 %collective-permute-done.1 = bf16[32,1152]{1,0:T(8,128)(2,1)S(1)} collective-permute-done((bf16[32,1152]{1,0:T(8,128)(2,1)S(1)}, bf16[32,1152]{1,0:T(8,128)(2,1)S(1)}, u32[]{:S(2)}, u32[]{:S(2)}) %collective-permute-start.1) | collective-permute-done | bytes 73760 | tf_op jit(solution)/shard_map/ppermute | solution.py:49
  39.0 4.8 %collective-permute-done.2 = bf16[32,1152]{1,0:T(8,128)(2,1)S(1)} collective-permute-done((bf16[32,1152]{1,0:T(8,128)(2,1)S(1)}, bf16[32,1152]{1,0:T(8,128)(2,1)S(1)}, u32[]{:S(2)}, u32[]{:S(2)}) %collective-permute-start.2) | collective-permute-done | bytes 73760 | tf_op jit(solution)/shard_map/ppermute | solution.py:49
  45.7 4.8 %collective-permute-done.3 = bf16[32,1152]{1,0:T(8,128)(2,1)S(1)} collective-permute-done((bf16[32,1152]{1,0:T(8,128)(2,1)S(1)}, bf16[32,1152]{1,0:T(8,128)(2,1)S(1)}, u32[]{:S(2)}, u32[]{:S(2)}) %collective-permute-start.3) | collective-permute-done | bytes 73760 | tf_op jit(solution)/shard_map/ppermute | solution.py:49
  52.4 4.8 %collective-permute-done.4 = bf16[32,1152]{1,0:T(8,128)(2,1)S(1)} collective-permute-done((bf16[32,1152]{1,0:T(8,128)(2,1)S(1)}, bf16[32,1152]{1,0:T(8,128)(2,1)S(1)}, u32[]{:S(2)}, u32[]{:S(2)}) %collective-permute-start.4) | collective-permute-done | bytes 73760 | tf_op jit(solution)/shard_map/ppermute | solution.py:49
  59.0 4.8 %collective-permute-done.5 = bf16[32,1152]{1,0:T(8,128)(2,1)S(1)} collective-permute-done((bf16[32,1152]{1,0:T(8,128)(2,1)S(1)}, bf16[32,1152]{1,0:T(8,128)(2,1)S(1)}, u32[]{:S(2)}, u32[]{:S(2)}) %collective-permute-start.5) | collective-permute-done | bytes 73760 | tf_op jit(solution)/shard_map/ppermute | solution.py:49
  65.7 4.8 %collective-permute-done.6 = bf16[32,1152]{1,0:T(8,128)(2,1)S(1)} collective-permute-done((bf16[32,1152]{1,0:T(8,128)(2,1)S(1)}, bf16[32,1152]{1,0:T(8,128)(2,1)S(1)}, u32[]{:S(2)}, u32[]{:S(2)}) %collective-permute-start.6) | collective-permute-done | bytes 73760 | tf_op jit(solution)/shard_map/ppermute | solution.py:49
  73.4 25.1 %collective-permute-done.7 = bf16[8,32,1152]{2,1,0:T(8,128)(2,1)S(1)} collective-permute-done((bf16[8,32,1152]{2,1,0:T(8,128)(2,1)S(1)}, bf16[8,32,1152]{2,1,0:T(8,128)(2,1)S(1)}, u32[]{:S(2)}, u32[]{:S(2)}) %collective-permute-start.7) | collective-permute-done | bytes 589856 | tf_op jit(solution)/shard_map/ppermute | solution.py:41
  99.8 4.7 %collective-permute-start.8 = (bf16[2,8,32,1152]{3,2,0,1:T(8,128)(2,1)}, bf16[2,8,32,1152]{3,2,0,1:T(8,128)(2,1)S(1)}, u32[]{:S(2)}, u32[]{:S(2)}) collective-permute-start(bf16[2,8,32,1152]{3,2,0,1:T(8,128)(2,1)} %pad_maximum_fusion.3), channel_id=1, source_target_pairs={{0,16},{16,0},{1,17},{17,1},{2,18},{18,2},{3,19},{19,3},{4,20},{20... | collective-permute-start | bytes 3538952 | tf_op jit(solution)/shard_map/ppermute | solution.py:41
  104.5 2.5 %collective-permute-done.8 = bf16[2,8,32,1152]{3,2,0,1:T(8,128)(2,1)S(1)} collective-permute-done((bf16[2,8,32,1152]{3,2,0,1:T(8,128)(2,1)}, bf16[2,8,32,1152]{3,2,0,1:T(8,128)(2,1)S(1)}, u32[]{:S(2)}, u32[]{:S(2)}) %collective-permute-start.8) | collective-permute-done | bytes 1179680 | tf_op jit(solution)/shard_map/ppermute | solution.py:41
  107.5 11.7 %all-to-all-done = bf16[16,64,2048]{2,1,0:T(8,128)(2,1)} async-done(((bf16[16,64,2048]{2,1,0:T(8,128)(2,1)}), bf16[16,64,2048]{2,1,0:T(8,128)(2,1)}, u32[]{:S(2)}, u32[]{:S(2)}) %all-to-all-start) | async-done | bytes 4194336 | tf_op jit(solution)/shard_map/all_to_all | solution.py:72
  119.3 3.5 %fusion.8 = f32[1024,768]{0,1:T(8,128)S(1)} fusion(bf16[1024,2048]{1,0:T(8,128)(2,1)} %bitcast.2, bf16[1024,1152]{1,0:T(8,128)(2,1)S(1)} %bitcast.97), kind=kOutput, calls=%fused_computation.14 | convolution fusion | flops 1610612736 | bytes 6815744 | tf_op jit(solution)/shard_map/dot_general | solution.py:16
  122.7 3.1 %multiply_convert_fusion.1 = (bf16[1024,384]{0,1:T(8,128)(2,1)S(1)}, bf16[1024,384]{0,1:T(8,128)(2,1)S(1)}) fusion(f32[1024,768]{0,1:T(8,128)S(1)} %fusion.8, bf16[1024,1152]{1,0:T(8,128)(2,1)S(1)} %bitcast.98, bf16[1024,2048]{1,0:T(8,128)(2,1)} %bitcast.2), kind=kOutput, calls=%fused_computation.20 | convolution fusion | flops 810418176 | bytes 7602176 | tf_op jit(solution)/shard_map/dot_general | solution.py:27
  129.1 2.4 pad_maximum_fusion
  131.5 7.7 %all-to-all-start.1 = ((bf16[16,64,2048]{2,1,0:T(8,128)(2,1)}), bf16[16,64,2048]{2,1,0:T(8,128)(2,1)}, u32[]{:S(2)}, u32[]{:S(2)}) async-start(bf16[16,64,2048]{2,1,0:T(8,128)(2,1)} %bitcast.92), calls=%async_computation.1 | async-start | bytes 8388608 | tf_op jit(solution)/shard_map/all_to_all | solution.py:72
  139.3 3.4 %fusion.6 = f32[1024,768]{1,0:T(8,128)S(1)} fusion(bf16[1024,2048]{1,0:T(8,128)(2,1)} %bitcast.2, bf16[1024,384]{0,1:T(8,128)(2,1)S(1)} %copy-done.10, bf16[1024,384]{0,1:T(8,128)(2,1)S(1)} %copy-done.8), kind=kOutput, calls=%fused_computation.12 | convolution fusion | flops 1613758464 | bytes 6815744 | tf_op jit(solution)/shard_map/dot_general | solution.py:125
  144.6 3.0 %collective-permute-start.9 = (f32[16,32,768]{2,1,0:T(8,128)S(1)}, f32[16,32,768]{2,1,0:T(8,128)}, u32[]{:S(2)}, u32[]{:S(2)}) collective-permute-start(f32[16,32,768]{2,1,0:T(8,128)S(1)} %dynamic-slice_bitcast_fusion), channel_id=1, source_target_pairs={{0,16},{16,0},{1,17},{17,1},{2,18},{18,2},{3,19},{19,3},{4,20},{20... | collective-permute-start | bytes 4718600 | tf_op jit(solution)/shard_map/ppermute | solution.py:133
  147.6 3.1 %collective-permute-done.9 = f32[16,32,768]{2,1,0:T(8,128)} collective-permute-done((f32[16,32,768]{2,1,0:T(8,128)S(1)}, f32[16,32,768]{2,1,0:T(8,128)}, u32[]{:S(2)}, u32[]{:S(2)}) %collective-permute-start.9) | collective-permute-done | bytes 1572896 | tf_op jit(solution)/shard_map/ppermute | solution.py:133
  155.1 22.5 %collective-permute-done.10 = f32[8,32,768]{2,1,0:T(8,128)} collective-permute-done((f32[8,32,768]{2,1,0:T(8,128)S(1)}, f32[8,32,768]{2,1,0:T(8,128)}, u32[]{:S(2)}, u32[]{:S(2)}) %collective-permute-start.10) | collective-permute-done | bytes 786464 | tf_op jit(solution)/shard_map/ppermute | solution.py:41
  178.9 3.2 %collective-permute-start.11 = (f32[32,768]{1,0:T(8,128)S(1)}, f32[32,768]{1,0:T(8,128)S(1)}, u32[]{:S(2)}, u32[]{:S(2)}) collective-permute-start(f32[32,768]{1,0:T(8,128)S(1)} %dynamic-slice_bitcast_fusion.2), channel_id=1, source_target_pairs={{0,64},{64,128},{128,192},{192,256},{256,320},{320,384},{384,448},... | collective-permute-start | bytes 294920 | tf_op jit(solution)/shard_map/ppermute | solution.py:60
  182.1 5.0 %collective-permute-done.11 = f32[32,768]{1,0:T(8,128)S(1)} collective-permute-done((f32[32,768]{1,0:T(8,128)S(1)}, f32[32,768]{1,0:T(8,128)S(1)}, u32[]{:S(2)}, u32[]{:S(2)}) %collective-permute-start.11) | collective-permute-done | bytes 98336 | tf_op jit(solution)/shard_map/ppermute | solution.py:60
  189.0 5.0 %collective-permute-done.12 = f32[32,768]{1,0:T(8,128)S(1)} collective-permute-done((f32[32,768]{1,0:T(8,128)S(1)}, f32[32,768]{1,0:T(8,128)S(1)}, u32[]{:S(2)}, u32[]{:S(2)}) %collective-permute-start.12) | collective-permute-done | bytes 98336 | tf_op jit(solution)/shard_map/ppermute | solution.py:60
  196.0 5.0 %collective-permute-done.13 = f32[32,768]{1,0:T(8,128)S(1)} collective-permute-done((f32[32,768]{1,0:T(8,128)S(1)}, f32[32,768]{1,0:T(8,128)S(1)}, u32[]{:S(2)}, u32[]{:S(2)}) %collective-permute-start.13) | collective-permute-done | bytes 98336 | tf_op jit(solution)/shard_map/ppermute | solution.py:60
  203.2 4.8 %collective-permute-done.14 = f32[32,768]{1,0:T(8,128)S(1)} collective-permute-done((f32[32,768]{1,0:T(8,128)S(1)}, f32[32,768]{1,0:T(8,128)S(1)}, u32[]{:S(2)}, u32[]{:S(2)}) %collective-permute-start.14) | collective-permute-done | bytes 98336 | tf_op jit(solution)/shard_map/ppermute | solution.py:60
  210.0 5.0 %collective-permute-done.15 = f32[32,768]{1,0:T(8,128)S(1)} collective-permute-done((f32[32,768]{1,0:T(8,128)S(1)}, f32[32,768]{1,0:T(8,128)S(1)}, u32[]{:S(2)}, u32[]{:S(2)}) %collective-permute-start.15) | collective-permute-done | bytes 98336 | tf_op jit(solution)/shard_map/ppermute | solution.py:60
  217.1 5.0 %collective-permute-done.16 = f32[32,768]{1,0:T(8,128)S(1)} collective-permute-done((f32[32,768]{1,0:T(8,128)S(1)}, f32[32,768]{1,0:T(8,128)S(1)}, u32[]{:S(2)}, u32[]{:S(2)}) %collective-permute-start.16) | collective-permute-done | bytes 98336 | tf_op jit(solution)/shard_map/ppermute | solution.py:60
  224.3 11.1 %all-to-all-done.1 = bf16[16,64,2048]{2,1,0:T(8,128)(2,1)} async-done(((bf16[16,64,2048]{2,1,0:T(8,128)(2,1)}), bf16[16,64,2048]{2,1,0:T(8,128)(2,1)}, u32[]{:S(2)}, u32[]{:S(2)}) %all-to-all-start.1) | async-done | bytes 4194336 | tf_op jit(solution)/shard_map/all_to_all | solution.py:72
  235.5 2.4 multiply_reduce_fusion
  237.9 2.7 %fusion.13 = bf16[128,1024]{1,0:T(8,128)(2,1)} fusion(pred[128,1024]{1,0:T(8,128)(4,1)S(1)} %fusion.19, bf16[1024,2048]{1,0:T(8,128)(2,1)} %bitcast.25), kind=kOutput, calls=%fused_computation.26 | convolution fusion | flops 268566528 | bytes 2490368 | tf_op jit(solution)/shard_map/dot_general | solution.py:160
  (96 shorter events, 48.6 us)
Async XLA Ops:
  0.6 4.4 %copy-start.1 = (bf16[128,1024]{1,0:T(8,128)(2,1)S(1)}, bf16[128,1024]{1,0:T(8,128)(2,1)}, u32[]{:S(2)}) copy-start(bf16[128,1024]{1,0:T(8,128)(2,1)} %param.10) | copy-start | bytes 786436
  9.4 13.6 %copy-start.3 = (bf16[1,32,384]{2,1,0:T(8,128)(2,1)S(1)}, bf16[1,32,384]{2,1,0:T(8,128)(2,1)}, u32[]{:S(2)}) copy-start(bf16[1,32,384]{2,1,0:T(8,128)(2,1)} %param.13) | copy-start | bytes 73732
  9.4 13.6 %copy-start.4 = (bf16[1,32,384]{2,1,0:T(8,128)(2,1)S(1)}, bf16[1,32,384]{2,1,0:T(8,128)(2,1)}, u32[]{:S(2)}) copy-start(bf16[1,32,384]{2,1,0:T(8,128)(2,1)} %param.12) | copy-start | bytes 73732
  9.4 13.6 %copy-start.5 = (bf16[1,32,384]{2,1,0:T(8,128)(2,1)S(1)}, bf16[1,32,384]{2,1,0:T(8,128)(2,1)}, u32[]{:S(2)}) copy-start(bf16[1,32,384]{2,1,0:T(8,128)(2,1)} %param.11) | copy-start | bytes 73732
  9.4 109.8 %all-to-all-start = ((bf16[16,64,2048]{2,1,0:T(8,128)(2,1)}), bf16[16,64,2048]{2,1,0:T(8,128)(2,1)}, u32[]{:S(2)}, u32[]{:S(2)}) async-start(bf16[16,64,2048]{2,1,0:T(8,128)(2,1)} %bitcast.91), calls=%async_computation | async-start | bytes 8388608 | tf_op jit(solution)/shard_map/all_to_all | solution.py:72
  23.1 7.2 %collective-permute-start = (bf16[32,1152]{1,0:T(8,128)(2,1)S(1)}, bf16[32,1152]{1,0:T(8,128)(2,1)S(1)}, u32[]{:S(2)}, u32[]{:S(2)}) collective-permute-start(bf16[32,1152]{1,0:T(8,128)(2,1)S(1)} %pad_maximum_fusion.6), channel_id=1, source_target_pairs={{0,64},{64,128},{128,192},{192,256},{256,320},{320,384},{384,448},... | collective-permute-start | bytes 221192 | tf_op jit(solution)/shard_map/ppermute | solution.py:49
  30.3 6.7 %collective-permute-start.1 = (bf16[32,1152]{1,0:T(8,128)(2,1)S(1)}, bf16[32,1152]{1,0:T(8,128)(2,1)S(1)}, u32[]{:S(2)}, u32[]{:S(2)}) collective-permute-start(bf16[32,1152]{1,0:T(8,128)(2,1)S(1)} %collective-permute-done), channel_id=1, source_target_pairs={{0,64},{64,128},{128,192},{192,256},{256,320},{320,384},{384,448},... | collective-permute-start | bytes 221192 | tf_op jit(solution)/shard_map/ppermute | solution.py:49
  37.0 6.7 %collective-permute-start.2 = (bf16[32,1152]{1,0:T(8,128)(2,1)S(1)}, bf16[32,1152]{1,0:T(8,128)(2,1)S(1)}, u32[]{:S(2)}, u32[]{:S(2)}) collective-permute-start(bf16[32,1152]{1,0:T(8,128)(2,1)S(1)} %collective-permute-done.1), channel_id=1, source_target_pairs={{0,64},{64,128},{128,192},{192,256},{256,320},{320,384},{384,448},... | collective-permute-start | bytes 221192 | tf_op jit(solution)/shard_map/ppermute | solution.py:49
  43.7 6.7 %collective-permute-start.3 = (bf16[32,1152]{1,0:T(8,128)(2,1)S(1)}, bf16[32,1152]{1,0:T(8,128)(2,1)S(1)}, u32[]{:S(2)}, u32[]{:S(2)}) collective-permute-start(bf16[32,1152]{1,0:T(8,128)(2,1)S(1)} %collective-permute-done.2), channel_id=1, source_target_pairs={{0,64},{64,128},{128,192},{192,256},{256,320},{320,384},{384,448},... | collective-permute-start | bytes 221192 | tf_op jit(solution)/shard_map/ppermute | solution.py:49
  50.4 6.7 %collective-permute-start.4 = (bf16[32,1152]{1,0:T(8,128)(2,1)S(1)}, bf16[32,1152]{1,0:T(8,128)(2,1)S(1)}, u32[]{:S(2)}, u32[]{:S(2)}) collective-permute-start(bf16[32,1152]{1,0:T(8,128)(2,1)S(1)} %collective-permute-done.3), channel_id=1, source_target_pairs={{0,64},{64,128},{128,192},{192,256},{256,320},{320,384},{384,448},... | collective-permute-start | bytes 221192 | tf_op jit(solution)/shard_map/ppermute | solution.py:49
  57.1 6.7 %collective-permute-start.5 = (bf16[32,1152]{1,0:T(8,128)(2,1)S(1)}, bf16[32,1152]{1,0:T(8,128)(2,1)S(1)}, u32[]{:S(2)}, u32[]{:S(2)}) collective-permute-start(bf16[32,1152]{1,0:T(8,128)(2,1)S(1)} %collective-permute-done.4), channel_id=1, source_target_pairs={{0,64},{64,128},{128,192},{192,256},{256,320},{320,384},{384,448},... | collective-permute-start | bytes 221192 | tf_op jit(solution)/shard_map/ppermute | solution.py:49
  63.8 6.7 %collective-permute-start.6 = (bf16[32,1152]{1,0:T(8,128)(2,1)S(1)}, bf16[32,1152]{1,0:T(8,128)(2,1)S(1)}, u32[]{:S(2)}, u32[]{:S(2)}) collective-permute-start(bf16[32,1152]{1,0:T(8,128)(2,1)S(1)} %collective-permute-done.5), channel_id=1, source_target_pairs={{0,64},{64,128},{128,192},{192,256},{256,320},{320,384},{384,448},... | collective-permute-start | bytes 221192 | tf_op jit(solution)/shard_map/ppermute | solution.py:49
  71.3 27.2 %collective-permute-start.7 = (bf16[8,32,1152]{2,1,0:T(8,128)(2,1)S(1)}, bf16[8,32,1152]{2,1,0:T(8,128)(2,1)S(1)}, u32[]{:S(2)}, u32[]{:S(2)}) collective-permute-start(bf16[8,32,1152]{2,1,0:T(8,128)(2,1)S(1)} %broadcast_select_fusion), channel_id=1, source_target_pairs={{0,32},{32,0},{1,33},{33,1},{2,34},{34,2},{3,35},{35,3},{4,36},{36... | collective-permute-start | bytes 1769480 | tf_op jit(solution)/shard_map/ppermute | solution.py:41
  99.8 7.2 %collective-permute-start.8 = (bf16[2,8,32,1152]{3,2,0,1:T(8,128)(2,1)}, bf16[2,8,32,1152]{3,2,0,1:T(8,128)(2,1)S(1)}, u32[]{:S(2)}, u32[]{:S(2)}) collective-permute-start(bf16[2,8,32,1152]{3,2,0,1:T(8,128)(2,1)} %pad_maximum_fusion.3), channel_id=1, source_target_pairs={{0,16},{16,0},{1,17},{17,1},{2,18},{18,2},{3,19},{19,3},{4,20},{20... | collective-permute-start | bytes 3538952 | tf_op jit(solution)/shard_map/ppermute | solution.py:41
  125.8 1.4 copy-start.7
  125.8 1.4 copy-start.9
  131.5 7.8 %copy-start.8 = (bf16[1024,384]{0,1:T(8,128)(2,1)S(1)}, bf16[1024,384]{0,1:T(8,128)(2,1)}, u32[]{:S(2)}) copy-start(bf16[1024,384]{0,1:T(8,128)(2,1)} %copy-done.7) | copy-start | bytes 2359300
  131.5 7.8 %copy-start.10 = (bf16[1024,384]{0,1:T(8,128)(2,1)S(1)}, bf16[1024,384]{0,1:T(8,128)(2,1)}, u32[]{:S(2)}) copy-start(bf16[1024,384]{0,1:T(8,128)(2,1)} %copy-done.9) | copy-start | bytes 2359300
  131.5 103.9 %all-to-all-start.1 = ((bf16[16,64,2048]{2,1,0:T(8,128)(2,1)}), bf16[16,64,2048]{2,1,0:T(8,128)(2,1)}, u32[]{:S(2)}, u32[]{:S(2)}) async-start(bf16[16,64,2048]{2,1,0:T(8,128)(2,1)} %bitcast.92), calls=%async_computation.1 | async-start | bytes 8388608 | tf_op jit(solution)/shard_map/all_to_all | solution.py:72
  142.7 1.7 copy-start
  144.6 6.2 %collective-permute-start.9 = (f32[16,32,768]{2,1,0:T(8,128)S(1)}, f32[16,32,768]{2,1,0:T(8,128)}, u32[]{:S(2)}, u32[]{:S(2)}) collective-permute-start(f32[16,32,768]{2,1,0:T(8,128)S(1)} %dynamic-slice_bitcast_fusion), channel_id=1, source_target_pairs={{0,16},{16,0},{1,17},{17,1},{2,18},{18,2},{3,19},{19,3},{4,20},{20... | collective-permute-start | bytes 4718600 | tf_op jit(solution)/shard_map/ppermute | solution.py:133
  152.9 57.1 %copy-start.6 = (s32[128,2]{0,1:T(2,128)S(1)}, s32[128,2]{0,1:T(2,128)}, u32[]{:S(2)}) copy-start(s32[128,2]{0,1:T(2,128)} %param.8) | copy-start | bytes 3076
  152.9 24.7 %collective-permute-start.10 = (f32[8,32,768]{2,1,0:T(8,128)S(1)}, f32[8,32,768]{2,1,0:T(8,128)}, u32[]{:S(2)}, u32[]{:S(2)}) collective-permute-start(f32[8,32,768]{2,1,0:T(8,128)S(1)} %dynamic-slice_bitcast_fusion.1), channel_id=1, source_target_pairs={{0,32},{32,0},{1,33},{33,1},{2,34},{34,2},{3,35},{35,3},{4,36},{36... | collective-permute-start | bytes 2359304 | tf_op jit(solution)/shard_map/ppermute | solution.py:41
  178.9 8.2 %collective-permute-start.11 = (f32[32,768]{1,0:T(8,128)S(1)}, f32[32,768]{1,0:T(8,128)S(1)}, u32[]{:S(2)}, u32[]{:S(2)}) collective-permute-start(f32[32,768]{1,0:T(8,128)S(1)} %dynamic-slice_bitcast_fusion.2), channel_id=1, source_target_pairs={{0,64},{64,128},{128,192},{192,256},{256,320},{320,384},{384,448},... | collective-permute-start | bytes 294920 | tf_op jit(solution)/shard_map/ppermute | solution.py:60
  187.1 7.0 %collective-permute-start.12 = (f32[32,768]{1,0:T(8,128)S(1)}, f32[32,768]{1,0:T(8,128)S(1)}, u32[]{:S(2)}, u32[]{:S(2)}) collective-permute-start(f32[32,768]{1,0:T(8,128)S(1)} %bitcast_add_fusion.8), channel_id=1, source_target_pairs={{0,64},{64,128},{128,192},{192,256},{256,320},{320,384},{384,448},... | collective-permute-start | bytes 294920 | tf_op jit(solution)/shard_map/ppermute | solution.py:60
  194.1 7.0 %collective-permute-start.13 = (f32[32,768]{1,0:T(8,128)S(1)}, f32[32,768]{1,0:T(8,128)S(1)}, u32[]{:S(2)}, u32[]{:S(2)}) collective-permute-start(f32[32,768]{1,0:T(8,128)S(1)} %bitcast_add_fusion.7), channel_id=1, source_target_pairs={{0,64},{64,128},{128,192},{192,256},{256,320},{320,384},{384,448},... | collective-permute-start | bytes 294920 | tf_op jit(solution)/shard_map/ppermute | solution.py:60
  201.0 7.0 %collective-permute-start.14 = (f32[32,768]{1,0:T(8,128)S(1)}, f32[32,768]{1,0:T(8,128)S(1)}, u32[]{:S(2)}, u32[]{:S(2)}) collective-permute-start(f32[32,768]{1,0:T(8,128)S(1)} %bitcast_add_fusion.6), channel_id=1, source_target_pairs={{0,64},{64,128},{128,192},{192,256},{256,320},{320,384},{384,448},... | collective-permute-start | bytes 294920 | tf_op jit(solution)/shard_map/ppermute | solution.py:60
  208.0 7.0 %collective-permute-start.15 = (f32[32,768]{1,0:T(8,128)S(1)}, f32[32,768]{1,0:T(8,128)S(1)}, u32[]{:S(2)}, u32[]{:S(2)}) collective-permute-start(f32[32,768]{1,0:T(8,128)S(1)} %bitcast_add_fusion.5), channel_id=1, source_target_pairs={{0,64},{64,128},{128,192},{192,256},{256,320},{320,384},{384,448},... | collective-permute-start | bytes 294920 | tf_op jit(solution)/shard_map/ppermute | solution.py:60
  215.0 7.1 %collective-permute-start.16 = (f32[32,768]{1,0:T(8,128)S(1)}, f32[32,768]{1,0:T(8,128)S(1)}, u32[]{:S(2)}, u32[]{:S(2)}) collective-permute-start(f32[32,768]{1,0:T(8,128)S(1)} %bitcast_add_fusion.4), channel_id=1, source_target_pairs={{0,64},{64,128},{128,192},{192,256},{256,320},{320,384},{384,448},... | collective-permute-start | bytes 294920 | tf_op jit(solution)/shard_map/ppermute | solution.py:60
  222.2 22.4 %collective-permute-start.17 = (f32[32,768]{1,0:T(8,128)S(1)}, f32[32,768]{1,0:T(8,128)S(1)}, u32[]{:S(2)}, u32[]{:S(2)}) collective-permute-start(f32[32,768]{1,0:T(8,128)S(1)} %bitcast_add_fusion.3), channel_id=1, source_target_pairs={{0,64},{64,128},{128,192},{192,256},{256,320},{320,384},{384,448},... | collective-permute-start | bytes 294920 | tf_op jit(solution)/shard_map/ppermute | solution.py:60
  242.6 2.6 %copy-start.2 = (bf16[128,1024]{1,0:T(8,128)(2,1)}, bf16[128,1024]{1,0:T(8,128)(2,1)S(1)}, u32[]{:S(2)}) copy-start(bf16[128,1024]{1,0:T(8,128)(2,1)S(1)} %multiply_reduce_fusion.1) | copy-start | bytes 786436

commit v12 on v11

--- a/solution.py
+++ b/solution.py
@@ -8,6 +8,7 @@
 DP_AXES = ("y", "xl", "c")
 CHIP_AXES = ("y", "xl")
 EXPERT_AXES = ("xh", "z")
+TRADE_AXES = ("z", "xh")
 TOKEN_AXES = DP_AXES + EXPERT_AXES
 
 
@@ -69,7 +70,7 @@
 
 
 def trade_rows(buffer):
-    return lax.all_to_all(buffer, EXPERT_AXES, split_axis=0, concat_axis=0, tiled=True)
+    return lax.all_to_all(buffer, TRADE_AXES, split_axis=0, concat_axis=0, tiled=True)
 
 
 def pick_slots(routing, expert_total):
@@ -109,7 +110,9 @@
         .reshape(pick_total, feature_total)
         .astype(jnp.bfloat16)
     )
-    slot_index = flat_ids * capacity + position
+    z_total = lax.axis_size("z")
+    chunk_of = (flat_ids % z_total) * (expert_total // z_total) + flat_ids // z_total
+    slot_index = chunk_of * capacity + position
     select = (
         slot_index[None, :] == jnp.arange(expert_total * capacity, dtype=jnp.int32)[:, None]
     ).astype(jnp.bfloat16)

time: 248 us -> 256 us (1.032)
  starting transfers between devices: 62.9 us -> 77.7 us
  waiting for transfers between devices: 138 us -> 134 us
    ppermute x3, starting transfers between devices: 8.98 us -> 25.7 us  [swap_partner(): return lax.ppermute(values, axis, perm=[(0, 1), (1, 0)])]
    all_to_all x2, waiting for transfers between devices: 22.9 us -> 18.6 us  [trade_rows(): lax.all_to_all(buffer, TRADE_AXES, split_axis=0, concat_axis=0, tiled=True)]
  transfers between devices with their start and end apart: 20 -> 20, of which waited for: 19 -> 18; matrix products, arithmetic and copies ran while one was open for 8% -> 7% of each run, Pallas kernels for 0% -> 0%
where the time goes in v12:
time: 256 us; the launch traced here: 255 us
  waiting for transfers between devices  134 us (52%)
  starting transfers between devices  77.7 us (30%)
  matrix products  21.6 us (8%)
  other arithmetic  10.3 us (4%)
  local copies, waits for them, and re-layouts  10.1 us (4%)
    ppermute x3, waiting for transfers between devices, swap_partner(): return lax.ppermute(values, axis, perm=[(0, 1), (1, 0)])  49.7 us
    ppermute x7, waiting for transfers between devices, ring_gather(): lax.ppermute(moving, axis, perm=[(i, (i + 1) % size) for i in range(size)])  32.5 us
    ppermute x7, waiting for transfers between devices, ring_reduce_scatter(): lax.ppermute(carry, axis, perm=[(i, (i + 1) % size) for i in range(size)])  29.7 us
    ppermute x3, starting transfers between devices, swap_partner(): return lax.ppermute(values, axis, perm=[(0, 1), (1, 0)])  25.7 us
    all_to_all x2, starting transfers between devices, trade_rows(): lax.all_to_all(buffer, TRADE_AXES, split_axis=0, concat_axis=0, tiled=True)  21.1 us
    all_to_all x2, waiting for transfers between devices, trade_rows(): lax.all_to_all(buffer, TRADE_AXES, split_axis=0, concat_axis=0, tiled=True)  18.6 us
    ppermute x7, starting transfers between devices, ring_gather(): lax.ppermute(moving, axis, perm=[(i, (i + 1) % size) for i in range(size)])  14.7 us
    ppermute x7, starting transfers between devices, ring_reduce_scatter(): lax.ppermute(carry, axis, perm=[(i, (i + 1) % size) for i in range(size)])  13.7 us
  transfers between devices with their start and end apart: 20, of which 18 were waited for; matrix products, arithmetic and copies ran while one was open for 7% of the time, Pallas kernels for 0%

profile of v12, /device:TPU:1, one launch (start us, length us, event | category | flops | bytes accessed | tf_op | source)
XLA Modules:
  0.0 255.3 jit_solution(16381834748690276951)
XLA Ops:
  6.2 3.2 %convolution_convert_fusion = bf16[1024,2048]{1,0:T(8,128)(2,1)} fusion(bf16[256,1024]{1,0:T(8,128)(2,1)S(1)} %multiply_convert_fusion.3, bf16[256,1024]{1,0:T(8,128)(2,1)S(1)} %reshape.213, s32[256]{0:T(256)S(1)} %multiply_add_fusion.1), kind=kOutput, calls=%fused_computation.2 | convolution fusion | flops 1078198272 | bytes 5243904 | tf_op jit(solution)/shard_map/dot_general | solution.py:120
  9.4 13.6 %all-to-all-start = ((bf16[16,64,2048]{2,1,0:T(8,128)(2,1)}), bf16[16,64,2048]{2,1,0:T(8,128)(2,1)}, u32[]{:S(2)}, u32[]{:S(2)}) async-start(bf16[16,64,2048]{2,1,0:T(8,128)(2,1)} %bitcast.91), calls=%async_computation | async-start | bytes 8388608 | tf_op jit(solution)/shard_map/all_to_all | solution.py:73
  23.1 3.2 %collective-permute-start = (bf16[32,1152]{1,0:T(8,128)(2,1)S(1)}, bf16[32,1152]{1,0:T(8,128)(2,1)S(1)}, u32[]{:S(2)}, u32[]{:S(2)}) collective-permute-start(bf16[32,1152]{1,0:T(8,128)(2,1)S(1)} %pad_maximum_fusion.6), channel_id=1, source_target_pairs={{0,64},{64,128},{128,192},{192,256},{256,320},{320,384},{384,448},... | collective-permute-start | bytes 221192 | tf_op jit(solution)/shard_map/ppermute | solution.py:50
  26.4 4.0 %collective-permute-done = bf16[32,1152]{1,0:T(8,128)(2,1)S(1)} collective-permute-done((bf16[32,1152]{1,0:T(8,128)(2,1)S(1)}, bf16[32,1152]{1,0:T(8,128)(2,1)S(1)}, u32[]{:S(2)}, u32[]{:S(2)}) %collective-permute-start) | collective-permute-done | bytes 73760 | tf_op jit(solution)/shard_map/ppermute | solution.py:50
  32.3 4.8 %collective-permute-done.1 = bf16[32,1152]{1,0:T(8,128)(2,1)S(1)} collective-permute-done((bf16[32,1152]{1,0:T(8,128)(2,1)S(1)}, bf16[32,1152]{1,0:T(8,128)(2,1)S(1)}, u32[]{:S(2)}, u32[]{:S(2)}) %collective-permute-start.1) | collective-permute-done | bytes 73760 | tf_op jit(solution)/shard_map/ppermute | solution.py:50
  39.0 4.8 %collective-permute-done.2 = bf16[32,1152]{1,0:T(8,128)(2,1)S(1)} collective-permute-done((bf16[32,1152]{1,0:T(8,128)(2,1)S(1)}, bf16[32,1152]{1,0:T(8,128)(2,1)S(1)}, u32[]{:S(2)}, u32[]{:S(2)}) %collective-permute-start.2) | collective-permute-done | bytes 73760 | tf_op jit(solution)/shard_map/ppermute | solution.py:50
  45.7 4.8 %collective-permute-done.3 = bf16[32,1152]{1,0:T(8,128)(2,1)S(1)} collective-permute-done((bf16[32,1152]{1,0:T(8,128)(2,1)S(1)}, bf16[32,1152]{1,0:T(8,128)(2,1)S(1)}, u32[]{:S(2)}, u32[]{:S(2)}) %collective-permute-start.3) | collective-permute-done | bytes 73760 | tf_op jit(solution)/shard_map/ppermute | solution.py:50
  52.4 4.8 %collective-permute-done.4 = bf16[32,1152]{1,0:T(8,128)(2,1)S(1)} collective-permute-done((bf16[32,1152]{1,0:T(8,128)(2,1)S(1)}, bf16[32,1152]{1,0:T(8,128)(2,1)S(1)}, u32[]{:S(2)}, u32[]{:S(2)}) %collective-permute-start.4) | collective-permute-done | bytes 73760 | tf_op jit(solution)/shard_map/ppermute | solution.py:50
  59.1 4.8 %collective-permute-done.5 = bf16[32,1152]{1,0:T(8,128)(2,1)S(1)} collective-permute-done((bf16[32,1152]{1,0:T(8,128)(2,1)S(1)}, bf16[32,1152]{1,0:T(8,128)(2,1)S(1)}, u32[]{:S(2)}, u32[]{:S(2)}) %collective-permute-start.5) | collective-permute-done | bytes 73760 | tf_op jit(solution)/shard_map/ppermute | solution.py:50
  65.8 4.8 %collective-permute-done.6 = bf16[32,1152]{1,0:T(8,128)(2,1)S(1)} collective-permute-done((bf16[32,1152]{1,0:T(8,128)(2,1)S(1)}, bf16[32,1152]{1,0:T(8,128)(2,1)S(1)}, u32[]{:S(2)}, u32[]{:S(2)}) %collective-permute-start.6) | collective-permute-done | bytes 73760 | tf_op jit(solution)/shard_map/ppermute | solution.py:50
  71.3 2.2 collective-permute-start.7
  73.5 27.6 %collective-permute-done.7 = bf16[8,32,1152]{2,1,0:T(8,128)(2,1)S(1)} collective-permute-done((bf16[8,32,1152]{2,1,0:T(8,128)(2,1)S(1)}, bf16[8,32,1152]{2,1,0:T(8,128)(2,1)S(1)}, u32[]{:S(2)}, u32[]{:S(2)}) %collective-permute-start.7) | collective-permute-done | bytes 589856 | tf_op jit(solution)/shard_map/ppermute | solution.py:42
  102.5 21.5 %collective-permute-start.8 = (bf16[2,8,32,1152]{3,2,0,1:T(8,128)(2,1)}, bf16[2,8,32,1152]{3,2,0,1:T(8,128)(2,1)S(1)}, u32[]{:S(2)}, u32[]{:S(2)}) collective-permute-start(bf16[2,8,32,1152]{3,2,0,1:T(8,128)(2,1)} %pad_maximum_fusion.3), channel_id=1, source_target_pairs={{0,16},{16,0},{1,17},{17,1},{2,18},{18,2},{3,19},{19,3},{4,20},{20... | collective-permute-start | bytes 3538952 | tf_op jit(solution)/shard_map/ppermute | solution.py:42
  124.1 2.5 collective-permute-done.8
  127.0 3.5 %fusion.8 = f32[1024,768]{0,1:T(8,128)S(1)} fusion(bf16[1024,2048]{1,0:T(8,128)(2,1)} %bitcast.2, bf16[1024,1152]{1,0:T(8,128)(2,1)S(1)} %bitcast.97), kind=kOutput, calls=%fused_computation.14 | convolution fusion | flops 1610612736 | bytes 6815744 | tf_op jit(solution)/shard_map/dot_general | solution.py:17
  130.5 3.1 %multiply_convert_fusion.1 = (bf16[1024,384]{0,1:T(8,128)(2,1)S(1)}, bf16[1024,384]{0,1:T(8,128)(2,1)S(1)}) fusion(f32[1024,768]{0,1:T(8,128)S(1)} %fusion.8, bf16[1024,1152]{1,0:T(8,128)(2,1)S(1)} %bitcast.98, bf16[1024,2048]{1,0:T(8,128)(2,1)} %bitcast.2), kind=kOutput, calls=%fused_computation.20 | convolution fusion | flops 810418176 | bytes 7602176 | tf_op jit(solution)/shard_map/dot_general | solution.py:28
  136.9 2.4 pad_maximum_fusion
  139.3 7.5 %all-to-all-start.1 = ((bf16[16,64,2048]{2,1,0:T(8,128)(2,1)}), bf16[16,64,2048]{2,1,0:T(8,128)(2,1)}, u32[]{:S(2)}, u32[]{:S(2)}) async-start(bf16[16,64,2048]{2,1,0:T(8,128)(2,1)} %bitcast.92), calls=%async_computation.1 | async-start | bytes 8388608 | tf_op jit(solution)/shard_map/all_to_all | solution.py:73
  146.8 3.4 %fusion.6 = f32[1024,768]{1,0:T(8,128)S(1)} fusion(bf16[1024,2048]{1,0:T(8,128)(2,1)} %bitcast.2, bf16[1024,384]{0,1:T(8,128)(2,1)S(1)} %copy-done.10, bf16[1024,384]{0,1:T(8,128)(2,1)S(1)} %copy-done.8), kind=kOutput, calls=%fused_computation.12 | convolution fusion | flops 1613758464 | bytes 6815744 | tf_op jit(solution)/shard_map/dot_general | solution.py:128
  152.1 2.6 %collective-permute-start.9 = (f32[16,32,768]{2,1,0:T(8,128)S(1)}, f32[16,32,768]{2,1,0:T(8,128)}, u32[]{:S(2)}, u32[]{:S(2)}) collective-permute-start(f32[16,32,768]{2,1,0:T(8,128)S(1)} %dynamic-slice_bitcast_fusion), channel_id=1, source_target_pairs={{0,16},{16,0},{1,17},{17,1},{2,18},{18,2},{3,19},{19,3},{4,20},{20... | collective-permute-start | bytes 4718600 | tf_op jit(solution)/shard_map/ppermute | solution.py:136
  154.6 3.1 %collective-permute-done.9 = f32[16,32,768]{2,1,0:T(8,128)} collective-permute-done((f32[16,32,768]{2,1,0:T(8,128)S(1)}, f32[16,32,768]{2,1,0:T(8,128)}, u32[]{:S(2)}, u32[]{:S(2)}) %collective-permute-start.9) | collective-permute-done | bytes 1572896 | tf_op jit(solution)/shard_map/ppermute | solution.py:136
  161.9 19.6 %collective-permute-done.10 = f32[8,32,768]{2,1,0:T(8,128)} collective-permute-done((f32[8,32,768]{2,1,0:T(8,128)S(1)}, f32[8,32,768]{2,1,0:T(8,128)}, u32[]{:S(2)}, u32[]{:S(2)}) %collective-permute-start.10) | collective-permute-done | bytes 786464 | tf_op jit(solution)/shard_map/ppermute | solution.py:42
  184.8 5.0 %collective-permute-done.11 = f32[32,768]{1,0:T(8,128)S(1)} collective-permute-done((f32[32,768]{1,0:T(8,128)S(1)}, f32[32,768]{1,0:T(8,128)S(1)}, u32[]{:S(2)}, u32[]{:S(2)}) %collective-permute-start.11) | collective-permute-done | bytes 98336 | tf_op jit(solution)/shard_map/ppermute | solution.py:61
  191.7 5.0 %collective-permute-done.12 = f32[32,768]{1,0:T(8,128)S(1)} collective-permute-done((f32[32,768]{1,0:T(8,128)S(1)}, f32[32,768]{1,0:T(8,128)S(1)}, u32[]{:S(2)}, u32[]{:S(2)}) %collective-permute-start.12) | collective-permute-done | bytes 98336 | tf_op jit(solution)/shard_map/ppermute | solution.py:61
  198.7 5.0 %collective-permute-done.13 = f32[32,768]{1,0:T(8,128)S(1)} collective-permute-done((f32[32,768]{1,0:T(8,128)S(1)}, f32[32,768]{1,0:T(8,128)S(1)}, u32[]{:S(2)}, u32[]{:S(2)}) %collective-permute-start.13) | collective-permute-done | bytes 98336 | tf_op jit(solution)/shard_map/ppermute | solution.py:61
  205.9 4.8 %collective-permute-done.14 = f32[32,768]{1,0:T(8,128)S(1)} collective-permute-done((f32[32,768]{1,0:T(8,128)S(1)}, f32[32,768]{1,0:T(8,128)S(1)}, u32[]{:S(2)}, u32[]{:S(2)}) %collective-permute-start.14) | collective-permute-done | bytes 98336 | tf_op jit(solution)/shard_map/ppermute | solution.py:61
  212.8 5.0 %collective-permute-done.15 = f32[32,768]{1,0:T(8,128)S(1)} collective-permute-done((f32[32,768]{1,0:T(8,128)S(1)}, f32[32,768]{1,0:T(8,128)S(1)}, u32[]{:S(2)}, u32[]{:S(2)}) %collective-permute-start.15) | collective-permute-done | bytes 98336 | tf_op jit(solution)/shard_map/ppermute | solution.py:61
  219.9 4.9 %collective-permute-done.16 = f32[32,768]{1,0:T(8,128)S(1)} collective-permute-done((f32[32,768]{1,0:T(8,128)S(1)}, f32[32,768]{1,0:T(8,128)S(1)}, u32[]{:S(2)}, u32[]{:S(2)}) %collective-permute-start.16) | collective-permute-done | bytes 98336 | tf_op jit(solution)/shard_map/ppermute | solution.py:61
  224.7 2.1 collective-permute-start.17
  226.9 18.6 %all-to-all-done.1 = bf16[16,64,2048]{2,1,0:T(8,128)(2,1)} async-done(((bf16[16,64,2048]{2,1,0:T(8,128)(2,1)}), bf16[16,64,2048]{2,1,0:T(8,128)(2,1)}, u32[]{:S(2)}, u32[]{:S(2)}) %all-to-all-start.1) | async-done | bytes 4194336 | tf_op jit(solution)/shard_map/all_to_all | solution.py:73
  245.5 2.4 multiply_reduce_fusion
  247.9 2.7 %fusion.13 = bf16[128,1024]{1,0:T(8,128)(2,1)} fusion(pred[128,1024]{1,0:T(8,128)(4,1)S(1)} %fusion.19, bf16[1024,2048]{1,0:T(8,128)(2,1)} %bitcast.25), kind=kOutput, calls=%fused_computation.26 | convolution fusion | flops 268566528 | bytes 2490368 | tf_op jit(solution)/shard_map/dot_general | solution.py:163
  (96 shorter events, 46.0 us)
Async XLA Ops:
  0.6 4.4 %copy-start.1 = (bf16[128,1024]{1,0:T(8,128)(2,1)S(1)}, bf16[128,1024]{1,0:T(8,128)(2,1)}, u32[]{:S(2)}) copy-start(bf16[128,1024]{1,0:T(8,128)(2,1)} %param.10) | copy-start | bytes 786436
  9.4 13.6 %copy-start.3 = (bf16[1,32,384]{2,1,0:T(8,128)(2,1)S(1)}, bf16[1,32,384]{2,1,0:T(8,128)(2,1)}, u32[]{:S(2)}) copy-start(bf16[1,32,384]{2,1,0:T(8,128)(2,1)} %param.13) | copy-start | bytes 73732
  9.4 13.6 %copy-start.4 = (bf16[1,32,384]{2,1,0:T(8,128)(2,1)S(1)}, bf16[1,32,384]{2,1,0:T(8,128)(2,1)}, u32[]{:S(2)}) copy-start(bf16[1,32,384]{2,1,0:T(8,128)(2,1)} %param.12) | copy-start | bytes 73732
  9.4 13.7 %copy-start.5 = (bf16[1,32,384]{2,1,0:T(8,128)(2,1)S(1)}, bf16[1,32,384]{2,1,0:T(8,128)(2,1)}, u32[]{:S(2)}) copy-start(bf16[1,32,384]{2,1,0:T(8,128)(2,1)} %param.11) | copy-start | bytes 73732
  9.4 117.6 %all-to-all-start = ((bf16[16,64,2048]{2,1,0:T(8,128)(2,1)}), bf16[16,64,2048]{2,1,0:T(8,128)(2,1)}, u32[]{:S(2)}, u32[]{:S(2)}) async-start(bf16[16,64,2048]{2,1,0:T(8,128)(2,1)} %bitcast.91), calls=%async_computation | async-start | bytes 8388608 | tf_op jit(solution)/shard_map/all_to_all | solution.py:73
  23.1 7.2 %collective-permute-start = (bf16[32,1152]{1,0:T(8,128)(2,1)S(1)}, bf16[32,1152]{1,0:T(8,128)(2,1)S(1)}, u32[]{:S(2)}, u32[]{:S(2)}) collective-permute-start(bf16[32,1152]{1,0:T(8,128)(2,1)S(1)} %pad_maximum_fusion.6), channel_id=1, source_target_pairs={{0,64},{64,128},{128,192},{192,256},{256,320},{320,384},{384,448},... | collective-permute-start | bytes 221192 | tf_op jit(solution)/shard_map/ppermute | solution.py:50
  30.3 6.7 %collective-permute-start.1 = (bf16[32,1152]{1,0:T(8,128)(2,1)S(1)}, bf16[32,1152]{1,0:T(8,128)(2,1)S(1)}, u32[]{:S(2)}, u32[]{:S(2)}) collective-permute-start(bf16[32,1152]{1,0:T(8,128)(2,1)S(1)} %collective-permute-done), channel_id=1, source_target_pairs={{0,64},{64,128},{128,192},{192,256},{256,320},{320,384},{384,448},... | collective-permute-start | bytes 221192 | tf_op jit(solution)/shard_map/ppermute | solution.py:50
  37.0 6.7 %collective-permute-start.2 = (bf16[32,1152]{1,0:T(8,128)(2,1)S(1)}, bf16[32,1152]{1,0:T(8,128)(2,1)S(1)}, u32[]{:S(2)}, u32[]{:S(2)}) collective-permute-start(bf16[32,1152]{1,0:T(8,128)(2,1)S(1)} %collective-permute-done.1), channel_id=1, source_target_pairs={{0,64},{64,128},{128,192},{192,256},{256,320},{320,384},{384,448},... | collective-permute-start | bytes 221192 | tf_op jit(solution)/shard_map/ppermute | solution.py:50
  43.7 6.7 %collective-permute-start.3 = (bf16[32,1152]{1,0:T(8,128)(2,1)S(1)}, bf16[32,1152]{1,0:T(8,128)(2,1)S(1)}, u32[]{:S(2)}, u32[]{:S(2)}) collective-permute-start(bf16[32,1152]{1,0:T(8,128)(2,1)S(1)} %collective-permute-done.2), channel_id=1, source_target_pairs={{0,64},{64,128},{128,192},{192,256},{256,320},{320,384},{384,448},... | collective-permute-start | bytes 221192 | tf_op jit(solution)/shard_map/ppermute | solution.py:50
  50.4 6.7 %collective-permute-start.4 = (bf16[32,1152]{1,0:T(8,128)(2,1)S(1)}, bf16[32,1152]{1,0:T(8,128)(2,1)S(1)}, u32[]{:S(2)}, u32[]{:S(2)}) collective-permute-start(bf16[32,1152]{1,0:T(8,128)(2,1)S(1)} %collective-permute-done.3), channel_id=1, source_target_pairs={{0,64},{64,128},{128,192},{192,256},{256,320},{320,384},{384,448},... | collective-permute-start | bytes 221192 | tf_op jit(solution)/shard_map/ppermute | solution.py:50
  57.1 6.7 %collective-permute-start.5 = (bf16[32,1152]{1,0:T(8,128)(2,1)S(1)}, bf16[32,1152]{1,0:T(8,128)(2,1)S(1)}, u32[]{:S(2)}, u32[]{:S(2)}) collective-permute-start(bf16[32,1152]{1,0:T(8,128)(2,1)S(1)} %collective-permute-done.4), channel_id=1, source_target_pairs={{0,64},{64,128},{128,192},{192,256},{256,320},{320,384},{384,448},... | collective-permute-start | bytes 221192 | tf_op jit(solution)/shard_map/ppermute | solution.py:50
  63.8 6.7 %collective-permute-start.6 = (bf16[32,1152]{1,0:T(8,128)(2,1)S(1)}, bf16[32,1152]{1,0:T(8,128)(2,1)S(1)}, u32[]{:S(2)}, u32[]{:S(2)}) collective-permute-start(bf16[32,1152]{1,0:T(8,128)(2,1)S(1)} %collective-permute-done.5), channel_id=1, source_target_pairs={{0,64},{64,128},{128,192},{192,256},{256,320},{320,384},{384,448},... | collective-permute-start | bytes 221192 | tf_op jit(solution)/shard_map/ppermute | solution.py:50
  71.3 29.8 %collective-permute-start.7 = (bf16[8,32,1152]{2,1,0:T(8,128)(2,1)S(1)}, bf16[8,32,1152]{2,1,0:T(8,128)(2,1)S(1)}, u32[]{:S(2)}, u32[]{:S(2)}) collective-permute-start(bf16[8,32,1152]{2,1,0:T(8,128)(2,1)S(1)} %broadcast_select_fusion), channel_id=1, source_target_pairs={{0,32},{32,0},{1,33},{33,1},{2,34},{34,2},{3,35},{35,3},{4,36},{36... | collective-permute-start | bytes 1769480 | tf_op jit(solution)/shard_map/ppermute | solution.py:42
  102.5 24.0 %collective-permute-start.8 = (bf16[2,8,32,1152]{3,2,0,1:T(8,128)(2,1)}, bf16[2,8,32,1152]{3,2,0,1:T(8,128)(2,1)S(1)}, u32[]{:S(2)}, u32[]{:S(2)}) collective-permute-start(bf16[2,8,32,1152]{3,2,0,1:T(8,128)(2,1)} %pad_maximum_fusion.3), channel_id=1, source_target_pairs={{0,16},{16,0},{1,17},{17,1},{2,18},{18,2},{3,19},{19,3},{4,20},{20... | collective-permute-start | bytes 3538952 | tf_op jit(solution)/shard_map/ppermute | solution.py:42
  133.6 1.4 copy-start.7
  133.6 1.4 copy-start.9
  139.3 7.5 %copy-start.8 = (bf16[1024,384]{0,1:T(8,128)(2,1)S(1)}, bf16[1024,384]{0,1:T(8,128)(2,1)}, u32[]{:S(2)}) copy-start(bf16[1024,384]{0,1:T(8,128)(2,1)} %copy-done.7) | copy-start | bytes 2359300
  139.3 7.5 %copy-start.10 = (bf16[1024,384]{0,1:T(8,128)(2,1)S(1)}, bf16[1024,384]{0,1:T(8,128)(2,1)}, u32[]{:S(2)}) copy-start(bf16[1024,384]{0,1:T(8,128)(2,1)} %copy-done.9) | copy-start | bytes 2359300
  139.3 106.2 %all-to-all-start.1 = ((bf16[16,64,2048]{2,1,0:T(8,128)(2,1)}), bf16[16,64,2048]{2,1,0:T(8,128)(2,1)}, u32[]{:S(2)}, u32[]{:S(2)}) async-start(bf16[16,64,2048]{2,1,0:T(8,128)(2,1)} %bitcast.92), calls=%async_computation.1 | async-start | bytes 8388608 | tf_op jit(solution)/shard_map/all_to_all | solution.py:73
  150.2 1.7 copy-start
  152.1 5.7 %collective-permute-start.9 = (f32[16,32,768]{2,1,0:T(8,128)S(1)}, f32[16,32,768]{2,1,0:T(8,128)}, u32[]{:S(2)}, u32[]{:S(2)}) collective-permute-start(f32[16,32,768]{2,1,0:T(8,128)S(1)} %dynamic-slice_bitcast_fusion), channel_id=1, source_target_pairs={{0,16},{16,0},{1,17},{17,1},{2,18},{18,2},{3,19},{19,3},{4,20},{20... | collective-permute-start | bytes 4718600 | tf_op jit(solution)/shard_map/ppermute | solution.py:136
  159.9 52.7 %copy-start.6 = (s32[128,2]{0,1:T(2,128)S(1)}, s32[128,2]{0,1:T(2,128)}, u32[]{:S(2)}) copy-start(s32[128,2]{0,1:T(2,128)} %param.8) | copy-start | bytes 3076
  160.0 21.6 %collective-permute-start.10 = (f32[8,32,768]{2,1,0:T(8,128)S(1)}, f32[8,32,768]{2,1,0:T(8,128)}, u32[]{:S(2)}, u32[]{:S(2)}) collective-permute-start(f32[8,32,768]{2,1,0:T(8,128)S(1)} %dynamic-slice_bitcast_fusion.1), channel_id=1, source_target_pairs={{0,32},{32,0},{1,33},{33,1},{2,34},{34,2},{3,35},{35,3},{4,36},{36... | collective-permute-start | bytes 2359304 | tf_op jit(solution)/shard_map/ppermute | solution.py:42
  182.8 7.0 %collective-permute-start.11 = (f32[32,768]{1,0:T(8,128)S(1)}, f32[32,768]{1,0:T(8,128)S(1)}, u32[]{:S(2)}, u32[]{:S(2)}) collective-permute-start(f32[32,768]{1,0:T(8,128)S(1)} %dynamic-slice_bitcast_fusion.2), channel_id=1, source_target_pairs={{0,64},{64,128},{128,192},{192,256},{256,320},{320,384},{384,448},... | collective-permute-start | bytes 294920 | tf_op jit(solution)/shard_map/ppermute | solution.py:61
  189.8 7.0 %collective-permute-start.12 = (f32[32,768]{1,0:T(8,128)S(1)}, f32[32,768]{1,0:T(8,128)S(1)}, u32[]{:S(2)}, u32[]{:S(2)}) collective-permute-start(f32[32,768]{1,0:T(8,128)S(1)} %bitcast_add_fusion.8), channel_id=1, source_target_pairs={{0,64},{64,128},{128,192},{192,256},{256,320},{320,384},{384,448},... | collective-permute-start | bytes 294920 | tf_op jit(solution)/shard_map/ppermute | solution.py:61
  196.8 7.0 %collective-permute-start.13 = (f32[32,768]{1,0:T(8,128)S(1)}, f32[32,768]{1,0:T(8,128)S(1)}, u32[]{:S(2)}, u32[]{:S(2)}) collective-permute-start(f32[32,768]{1,0:T(8,128)S(1)} %bitcast_add_fusion.7), channel_id=1, source_target_pairs={{0,64},{64,128},{128,192},{192,256},{256,320},{320,384},{384,448},... | collective-permute-start | bytes 294920 | tf_op jit(solution)/shard_map/ppermute | solution.py:61
  203.8 7.0 %collective-permute-start.14 = (f32[32,768]{1,0:T(8,128)S(1)}, f32[32,768]{1,0:T(8,128)S(1)}, u32[]{:S(2)}, u32[]{:S(2)}) collective-permute-start(f32[32,768]{1,0:T(8,128)S(1)} %bitcast_add_fusion.6), channel_id=1, source_target_pairs={{0,64},{64,128},{128,192},{192,256},{256,320},{320,384},{384,448},... | collective-permute-start | bytes 294920 | tf_op jit(solution)/shard_map/ppermute | solution.py:61
  210.8 7.0 %collective-permute-start.15 = (f32[32,768]{1,0:T(8,128)S(1)}, f32[32,768]{1,0:T(8,128)S(1)}, u32[]{:S(2)}, u32[]{:S(2)}) collective-permute-start(f32[32,768]{1,0:T(8,128)S(1)} %bitcast_add_fusion.5), channel_id=1, source_target_pairs={{0,64},{64,128},{128,192},{192,256},{256,320},{320,384},{384,448},... | collective-permute-start | bytes 294920 | tf_op jit(solution)/shard_map/ppermute | solution.py:61
  217.7 7.0 %collective-permute-start.16 = (f32[32,768]{1,0:T(8,128)S(1)}, f32[32,768]{1,0:T(8,128)S(1)}, u32[]{:S(2)}, u32[]{:S(2)}) collective-permute-start(f32[32,768]{1,0:T(8,128)S(1)} %bitcast_add_fusion.4), channel_id=1, source_target_pairs={{0,64},{64,128},{128,192},{192,256},{256,320},{320,384},{384,448},... | collective-permute-start | bytes 294920 | tf_op jit(solution)/shard_map/ppermute | solution.py:61
  224.7 29.9 %collective-permute-start.17 = (f32[32,768]{1,0:T(8,128)S(1)}, f32[32,768]{1,0:T(8,128)S(1)}, u32[]{:S(2)}, u32[]{:S(2)}) collective-permute-start(f32[32,768]{1,0:T(8,128)S(1)} %bitcast_add_fusion.3), channel_id=1, source_target_pairs={{0,64},{64,128},{128,192},{192,256},{256,320},{320,384},{384,448},... | collective-permute-start | bytes 294920 | tf_op jit(solution)/shard_map/ppermute | solution.py:61
  252.7 2.6 %copy-start.2 = (bf16[128,1024]{1,0:T(8,128)(2,1)}, bf16[128,1024]{1,0:T(8,128)(2,1)S(1)}, u32[]{:S(2)}) copy-start(bf16[128,1024]{1,0:T(8,128)(2,1)S(1)} %multiply_reduce_fusion.1) | copy-start | bytes 786436

commit v13 on v11

--- a/solution.py
+++ b/solution.py
@@ -139,16 +139,15 @@
     summed = ring_reduce_scatter(xl_summed, "y", y_size)
     summed = summed.reshape(slice_rows, 2 * hidden_total) / group_total
     row_major = Layout(major_to_minor=(0, 1))
-    back = jnp.concatenate(
-        [with_layout_constraint(results, row_major), with_layout_constraint(input_grads, row_major)],
-        axis=1,
-    )
-    returned = trade_rows(back.reshape(expert_total, capacity, 2 * feature_total)).reshape(
-        expert_total * capacity, 2 * feature_total
-    )
+    returned_out = trade_rows(
+        with_layout_constraint(results, row_major).reshape(expert_total, capacity, feature_total)
+    ).reshape(expert_total * capacity, feature_total)
+    returned_grads = trade_rows(
+        with_layout_constraint(input_grads, row_major).reshape(expert_total, capacity, feature_total)
+    ).reshape(expert_total * capacity, feature_total)
     pick_rows = lax.dot_general(
         select,
-        returned[:, :feature_total],
+        returned_out,
         (((0,), (0,)), ((), ())),
         preferred_element_type=jnp.float32,
     )
@@ -158,7 +157,7 @@
         axis=1,
     ).astype(jnp.bfloat16)
     token_grad = jnp.dot(
-        token_select, returned[:, feature_total:], preferred_element_type=jnp.float32
+        token_select, returned_grads, preferred_element_type=jnp.float32
     ).astype(jnp.bfloat16)
     pick_wide = pick_rows.reshape(tok_count, top_count, feature_total)
     layer_output = jnp.sum(combine[:, :, None] * pick_wide, axis=1).astype(jnp.bfloat16)

time: 248 us -> 252 us (1.016)
  the two profiles are of different devices: /device:TPU:1 before, /device:TPU:28 now
where the time goes in v13:
time: 252 us; the launch traced here: 251 us
  starting transfers between devices  117 us (46%)
  waiting for transfers between devices  87 us (35%)
  matrix products  27.2 us (11%)
  other arithmetic  9.17 us (4%)
  local copies, waits for them, and re-layouts  8.58 us (3%)
    ppermute x7, starting transfers between devices, ring_reduce_scatter(): lax.ppermute(carry, axis, perm=[(i, (i + 1) % size) for i in range(size)])  38.4 us
    ppermute x7, starting transfers between devices, ring_gather(): lax.ppermute(moving, axis, perm=[(i, (i + 1) % size) for i in range(size)])  37.6 us
    all_to_all x3, waiting for transfers between devices, trade_rows(): lax.all_to_all(buffer, EXPERT_AXES, split_axis=0, concat_axis=0, tiled=True)  33.9 us
    all_to_all x3, starting transfers between devices, trade_rows(): lax.all_to_all(buffer, EXPERT_AXES, split_axis=0, concat_axis=0, tiled=True)  31.4 us
    ppermute x3, waiting for transfers between devices, swap_partner(): return lax.ppermute(values, axis, perm=[(0, 1), (1, 0)])  24.3 us
    ppermute x7, waiting for transfers between devices, ring_gather(): lax.ppermute(moving, axis, perm=[(i, (i + 1) % size) for i in range(size)])  13.5 us
    ppermute x7, waiting for transfers between devices, ring_reduce_scatter(): lax.ppermute(carry, axis, perm=[(i, (i + 1) % size) for i in range(size)])  11.8 us
    ppermute x3, starting transfers between devices, swap_partner(): return lax.ppermute(values, axis, perm=[(0, 1), (1, 0)])  7.94 us
  transfers between devices with their start and end apart: 21, of which 18 were waited for; matrix products, arithmetic and copies ran while one was open for 10% of the time, Pallas kernels for 0%

profile of v13, /device:TPU:28, one launch (start us, length us, event | category | flops | bytes accessed | tf_op | source)
XLA Modules:
  0.0 251.2 jit_solution(9419714509280811823)
XLA Ops:
  6.2 3.2 %convolution_convert_fusion = bf16[1024,2048]{1,0:T(8,128)(2,1)} fusion(bf16[256,1024]{1,0:T(8,128)(2,1)S(1)} %multiply_convert_fusion.3, bf16[256,1024]{1,0:T(8,128)(2,1)S(1)} %reshape.159, s32[256]{0:T(256)S(1)} %multiply_add_fusion), kind=kOutput, calls=%fused_computation.1 | convolution fusion | flops 1078198272 | bytes 5243904 | tf_op jit(solution)/shard_map/dot_general | solution.py:117
  9.4 13.4 %all-to-all-start = ((bf16[16,64,2048]{2,1,0:T(8,128)(2,1)}), bf16[16,64,2048]{2,1,0:T(8,128)(2,1)}, u32[]{:S(2)}, u32[]{:S(2)}) async-start(bf16[16,64,2048]{2,1,0:T(8,128)(2,1)} %bitcast.102), calls=%async_computation | async-start | bytes 8388608 | tf_op jit(solution)/shard_map/all_to_all | solution.py:72
  22.9 4.7 %collective-permute-start = (bf16[32,1152]{1,0:T(8,128)(2,1)S(1)}, bf16[32,1152]{1,0:T(8,128)(2,1)S(1)}, u32[]{:S(2)}, u32[]{:S(2)}) collective-permute-start(bf16[32,1152]{1,0:T(8,128)(2,1)S(1)} %pad_maximum_fusion.5), channel_id=1, source_target_pairs={{0,64},{64,128},{128,192},{192,256},{256,320},{320,384},{384,448},... | collective-permute-start | bytes 221192 | tf_op jit(solution)/shard_map/ppermute | solution.py:49
  29.5 5.5 %collective-permute-start.1 = (bf16[32,1152]{1,0:T(8,128)(2,1)S(1)}, bf16[32,1152]{1,0:T(8,128)(2,1)S(1)}, u32[]{:S(2)}, u32[]{:S(2)}) collective-permute-start(bf16[32,1152]{1,0:T(8,128)(2,1)S(1)} %collective-permute-done), channel_id=1, source_target_pairs={{0,64},{64,128},{128,192},{192,256},{256,320},{320,384},{384,448},... | collective-permute-start | bytes 221192 | tf_op jit(solution)/shard_map/ppermute | solution.py:49
  37.0 5.5 %collective-permute-start.2 = (bf16[32,1152]{1,0:T(8,128)(2,1)S(1)}, bf16[32,1152]{1,0:T(8,128)(2,1)S(1)}, u32[]{:S(2)}, u32[]{:S(2)}) collective-permute-start(bf16[32,1152]{1,0:T(8,128)(2,1)S(1)} %collective-permute-done.1), channel_id=1, source_target_pairs={{0,64},{64,128},{128,192},{192,256},{256,320},{320,384},{384,448},... | collective-permute-start | bytes 221192 | tf_op jit(solution)/shard_map/ppermute | solution.py:49
  44.4 5.5 %collective-permute-start.3 = (bf16[32,1152]{1,0:T(8,128)(2,1)S(1)}, bf16[32,1152]{1,0:T(8,128)(2,1)S(1)}, u32[]{:S(2)}, u32[]{:S(2)}) collective-permute-start(bf16[32,1152]{1,0:T(8,128)(2,1)S(1)} %collective-permute-done.2), channel_id=1, source_target_pairs={{0,64},{64,128},{128,192},{192,256},{256,320},{320,384},{384,448},... | collective-permute-start | bytes 221192 | tf_op jit(solution)/shard_map/ppermute | solution.py:49
  51.9 5.5 %collective-permute-start.4 = (bf16[32,1152]{1,0:T(8,128)(2,1)S(1)}, bf16[32,1152]{1,0:T(8,128)(2,1)S(1)}, u32[]{:S(2)}, u32[]{:S(2)}) collective-permute-start(bf16[32,1152]{1,0:T(8,128)(2,1)S(1)} %collective-permute-done.3), channel_id=1, source_target_pairs={{0,64},{64,128},{128,192},{192,256},{256,320},{320,384},{384,448},... | collective-permute-start | bytes 221192 | tf_op jit(solution)/shard_map/ppermute | solution.py:49
  59.3 5.5 %collective-permute-start.5 = (bf16[32,1152]{1,0:T(8,128)(2,1)S(1)}, bf16[32,1152]{1,0:T(8,128)(2,1)S(1)}, u32[]{:S(2)}, u32[]{:S(2)}) collective-permute-start(bf16[32,1152]{1,0:T(8,128)(2,1)S(1)} %collective-permute-done.4), channel_id=1, source_target_pairs={{0,64},{64,128},{128,192},{192,256},{256,320},{320,384},{384,448},... | collective-permute-start | bytes 221192 | tf_op jit(solution)/shard_map/ppermute | solution.py:49
  66.8 5.5 %collective-permute-start.6 = (bf16[32,1152]{1,0:T(8,128)(2,1)S(1)}, bf16[32,1152]{1,0:T(8,128)(2,1)S(1)}, u32[]{:S(2)}, u32[]{:S(2)}) collective-permute-start(bf16[32,1152]{1,0:T(8,128)(2,1)S(1)} %collective-permute-done.5), channel_id=1, source_target_pairs={{0,64},{64,128},{128,192},{192,256},{256,320},{320,384},{384,448},... | collective-permute-start | bytes 221192 | tf_op jit(solution)/shard_map/ppermute | solution.py:49
  75.0 3.1 %collective-permute-start.7 = (bf16[8,32,1152]{2,1,0:T(8,128)(2,1)S(1)}, bf16[8,32,1152]{2,1,0:T(8,128)(2,1)S(1)}, u32[]{:S(2)}, u32[]{:S(2)}) collective-permute-start(bf16[8,32,1152]{2,1,0:T(8,128)(2,1)S(1)} %broadcast_select_fusion), channel_id=1, source_target_pairs={{0,32},{32,0},{1,33},{33,1},{2,34},{34,2},{3,35},{35,3},{4,36},{36... | collective-permute-start | bytes 1769480 | tf_op jit(solution)/shard_map/ppermute | solution.py:41
  78.1 21.3 %collective-permute-done.7 = bf16[8,32,1152]{2,1,0:T(8,128)(2,1)S(1)} collective-permute-done((bf16[8,32,1152]{2,1,0:T(8,128)(2,1)S(1)}, bf16[8,32,1152]{2,1,0:T(8,128)(2,1)S(1)}, u32[]{:S(2)}, u32[]{:S(2)}) %collective-permute-start.7) | collective-permute-done | bytes 589856 | tf_op jit(solution)/shard_map/ppermute | solution.py:41
  102.8 3.0 %collective-permute-done.8 = bf16[2,8,32,1152]{3,2,0,1:T(8,128)(2,1)S(1)} collective-permute-done((bf16[2,8,32,1152]{3,2,0,1:T(8,128)(2,1)}, bf16[2,8,32,1152]{3,2,0,1:T(8,128)(2,1)S(1)}, u32[]{:S(2)}, u32[]{:S(2)}) %collective-permute-start.8) | collective-permute-done | bytes 1179680 | tf_op jit(solution)/shard_map/ppermute | solution.py:41
  107.7 9.0 %all-to-all-done = bf16[16,64,2048]{2,1,0:T(8,128)(2,1)} async-done(((bf16[16,64,2048]{2,1,0:T(8,128)(2,1)}), bf16[16,64,2048]{2,1,0:T(8,128)(2,1)}, u32[]{:S(2)}, u32[]{:S(2)}) %all-to-all-start) | async-done | bytes 4194336 | tf_op jit(solution)/shard_map/all_to_all | solution.py:72
  116.7 3.9 %fusion.4 = f32[1024,768]{0,1:T(8,128)S(1)} fusion(bf16[1024,2048]{1,0:T(8,128)(2,1)} %bitcast.3, bf16[1024,1152]{1,0:T(8,128)(2,1)} %bitcast.108), kind=kOutput, calls=%fused_computation.9 | convolution fusion | flops 1610612736 | bytes 6815744 | tf_op jit(solution)/shard_map/dot_general | solution.py:16
  120.6 4.4 %convolution_convert_fusion.1 = bf16[1024,1024]{1,0:T(8,128)(2,1)} fusion(f32[1024,768]{0,1:T(8,128)S(1)} %fusion.4, bf16[1024,1152]{1,0:T(8,128)(2,1)} %bitcast.109), kind=kOutput, calls=%fused_computation.5 | convolution fusion | flops 808714240 | bytes 6029312 | tf_op jit(solution)/shard_map/dot_general | solution.py:20
  125.0 10.6 %all-to-all-start.1 = ((bf16[16,64,1024]{2,1,0:T(8,128)(2,1)}), bf16[16,64,1024]{2,1,0:T(8,128)(2,1)}, u32[]{:S(2)}, u32[]{:S(2)}) async-start(bf16[16,64,1024]{2,1,0:T(8,128)(2,1)} %bitcast.25), calls=%async_computation.1 | async-start | bytes 4194304 | tf_op jit(solution)/shard_map/all_to_all | solution.py:72
  135.6 4.2 %multiply_convert_fusion.1 = (bf16[1024,384]{0,1:T(8,128)(2,1)S(1)}, bf16[1024,384]{0,1:T(8,128)(2,1)S(1)}) fusion(f32[1024,768]{0,1:T(8,128)} %copy-done.10, bf16[1024,1152]{1,0:T(8,128)(2,1)} %bitcast.110, bf16[1024,2048]{1,0:T(8,128)(2,1)} %bitcast.3), kind=kOutput, calls=%fused_computation.15 | convolution fusion | flops 810418176 | bytes 7602176 | tf_op jit(solution)/shard_map/dot_general | solution.py:27
  139.9 4.0 %fusion.2 = f32[1024,768]{1,0:T(8,128)S(1)} fusion(bf16[1024,2048]{1,0:T(8,128)(2,1)} %bitcast.3, bf16[1024,384]{0,1:T(8,128)(2,1)S(1)} %get-tuple-element.8, bf16[1024,384]{0,1:T(8,128)(2,1)S(1)} %get-tuple-element.7), kind=kOutput, calls=%fused_computation.7 | convolution fusion | flops 1613758464 | bytes 6815744 | tf_op jit(solution)/shard_map/dot_general | solution.py:125
  147.5 3.5 %collective-permute-done.9 = f32[16,32,768]{2,1,0:T(8,128)} collective-permute-done((f32[16,32,768]{2,1,0:T(8,128)S(1)}, f32[16,32,768]{2,1,0:T(8,128)}, u32[]{:S(2)}, u32[]{:S(2)}) %collective-permute-start.9) | collective-permute-done | bytes 1572896 | tf_op jit(solution)/shard_map/ppermute | solution.py:133
  151.0 2.2 bitcast_add_fusion
  153.4 2.9 %collective-permute-start.10 = (f32[8,32,768]{2,1,0:T(8,128)S(1)}, f32[8,32,768]{2,1,0:T(8,128)}, u32[]{:S(2)}, u32[]{:S(2)}) collective-permute-start(f32[8,32,768]{2,1,0:T(8,128)S(1)} %dynamic-slice_bitcast_fusion.1), channel_id=1, source_target_pairs={{0,32},{32,0},{1,33},{33,1},{2,34},{34,2},{3,35},{35,3},{4,36},{36... | collective-permute-start | bytes 2359304 | tf_op jit(solution)/shard_map/ppermute | solution.py:41
  156.3 3.2 %convolution_convert_fusion.2 = bf16[1024,1024]{1,0:T(8,128)(2,1)} fusion(bf16[1024,1152]{1,0:T(8,128)(2,1)S(1)} %bitcast.111, bf16[1024,384]{0,1:T(8,128)(2,1)S(1)} %copy-done.14, bf16[1024,384]{0,1:T(8,128)(2,1)S(1)} %copy-done.12), kind=kOutput, calls=%fused_computation.6 | convolution fusion | flops 1614807040 | bytes 5242880 | tf_op jit(solution)/shard_map/dot_general | solution.py:34
  159.5 24.9 %all-to-all-done.1 = bf16[16,64,1024]{2,1,0:T(8,128)(2,1)} async-done(((bf16[16,64,1024]{2,1,0:T(8,128)(2,1)}), bf16[16,64,1024]{2,1,0:T(8,128)(2,1)}, u32[]{:S(2)}, u32[]{:S(2)}) %all-to-all-start.1) | async-done | bytes 2097184 | tf_op jit(solution)/shard_map/all_to_all | solution.py:72
  184.4 7.4 %all-to-all-start.2 = ((bf16[16,64,1024]{2,1,0:T(8,128)(2,1)}), bf16[16,64,1024]{2,1,0:T(8,128)(2,1)S(1)}, u32[]{:S(2)}, u32[]{:S(2)}) async-start(bf16[16,64,1024]{2,1,0:T(8,128)(2,1)} %bitcast.112), calls=%async_computation.2 | async-start | bytes 4194304 | tf_op jit(solution)/shard_map/all_to_all | solution.py:72
  193.3 5.3 %collective-permute-start.11 = (f32[32,768]{1,0:T(8,128)S(1)}, f32[32,768]{1,0:T(8,128)S(1)}, u32[]{:S(2)}, u32[]{:S(2)}) collective-permute-start(f32[32,768]{1,0:T(8,128)S(1)} %dynamic-slice_bitcast_fusion.2), channel_id=1, source_target_pairs={{0,64},{64,128},{128,192},{192,256},{256,320},{320,384},{384,448},... | collective-permute-start | bytes 294920 | tf_op jit(solution)/shard_map/ppermute | solution.py:60
  200.8 5.5 %collective-permute-start.12 = (f32[32,768]{1,0:T(8,128)S(1)}, f32[32,768]{1,0:T(8,128)S(1)}, u32[]{:S(2)}, u32[]{:S(2)}) collective-permute-start(f32[32,768]{1,0:T(8,128)S(1)} %bitcast_add_fusion.8), channel_id=1, source_target_pairs={{0,64},{64,128},{128,192},{192,256},{256,320},{320,384},{384,448},... | collective-permute-start | bytes 294920 | tf_op jit(solution)/shard_map/ppermute | solution.py:60
  208.5 5.5 %collective-permute-start.13 = (f32[32,768]{1,0:T(8,128)S(1)}, f32[32,768]{1,0:T(8,128)S(1)}, u32[]{:S(2)}, u32[]{:S(2)}) collective-permute-start(f32[32,768]{1,0:T(8,128)S(1)} %bitcast_add_fusion.7), channel_id=1, source_target_pairs={{0,64},{64,128},{128,192},{192,256},{256,320},{320,384},{384,448},... | collective-permute-start | bytes 294920 | tf_op jit(solution)/shard_map/ppermute | solution.py:60
  216.3 5.5 %collective-permute-start.14 = (f32[32,768]{1,0:T(8,128)S(1)}, f32[32,768]{1,0:T(8,128)S(1)}, u32[]{:S(2)}, u32[]{:S(2)}) collective-permute-start(f32[32,768]{1,0:T(8,128)S(1)} %bitcast_add_fusion.6), channel_id=1, source_target_pairs={{0,64},{64,128},{128,192},{192,256},{256,320},{320,384},{384,448},... | collective-permute-start | bytes 294920 | tf_op jit(solution)/shard_map/ppermute | solution.py:60
  224.0 5.5 %collective-permute-start.15 = (f32[32,768]{1,0:T(8,128)S(1)}, f32[32,768]{1,0:T(8,128)S(1)}, u32[]{:S(2)}, u32[]{:S(2)}) collective-permute-start(f32[32,768]{1,0:T(8,128)S(1)} %bitcast_add_fusion.5), channel_id=1, source_target_pairs={{0,64},{64,128},{128,192},{192,256},{256,320},{320,384},{384,448},... | collective-permute-start | bytes 294920 | tf_op jit(solution)/shard_map/ppermute | solution.py:60
  231.8 5.5 %collective-permute-start.16 = (f32[32,768]{1,0:T(8,128)S(1)}, f32[32,768]{1,0:T(8,128)S(1)}, u32[]{:S(2)}, u32[]{:S(2)}) collective-permute-start(f32[32,768]{1,0:T(8,128)S(1)} %bitcast_add_fusion.4), channel_id=1, source_target_pairs={{0,64},{64,128},{128,192},{192,256},{256,320},{320,384},{384,448},... | collective-permute-start | bytes 294920 | tf_op jit(solution)/shard_map/ppermute | solution.py:60
  239.5 5.5 %collective-permute-start.17 = (f32[32,768]{1,0:T(8,128)S(1)}, f32[32,768]{1,0:T(8,128)S(1)}, u32[]{:S(2)}, u32[]{:S(2)}) collective-permute-start(f32[32,768]{1,0:T(8,128)S(1)} %bitcast_add_fusion.3), channel_id=1, source_target_pairs={{0,64},{64,128},{128,192},{192,256},{256,320},{320,384},{384,448},... | collective-permute-start | bytes 294920 | tf_op jit(solution)/shard_map/ppermute | solution.py:60
  245.0 3.1 %multiply_reduce_fusion = (f32[128,2]{0,1:T(2,128)}, bf16[128,1024]{1,0:T(8,128)(2,1)S(1)}) fusion(f32[128,1024]{1,0:T(8,128)} %convert_element_type.42, f32[128,2]{0,1:T(2,128)S(1)} %copy-done.8, bf16[1024,1024,1]{1,0,2:T(8,128)(2,1)} %bitcast.27, s32[128,2]{0,1:T(2,128)S(1)} %multiply_add_fusion.1), kind=kOutput, calls=%fused_computation.28 | convolution fusion | flops 538050304 | bytes 2886656 | tf_op jit(solution)/shard_map/dot_general | solution.py:148
  (102 shorter events, 45.8 us)
Async XLA Ops:
  0.6 4.4 %copy-start.3 = (bf16[128,1024]{1,0:T(8,128)(2,1)S(1)}, bf16[128,1024]{1,0:T(8,128)(2,1)}, u32[]{:S(2)}) copy-start(bf16[128,1024]{1,0:T(8,128)(2,1)} %param.10) | copy-start | bytes 786436
  9.4 13.4 %copy-start.4 = (bf16[1,32,384]{2,1,0:T(8,128)(2,1)S(1)}, bf16[1,32,384]{2,1,0:T(8,128)(2,1)}, u32[]{:S(2)}) copy-start(bf16[1,32,384]{2,1,0:T(8,128)(2,1)} %param.13) | copy-start | bytes 73732
  9.4 13.4 %copy-start.5 = (bf16[1,32,384]{2,1,0:T(8,128)(2,1)S(1)}, bf16[1,32,384]{2,1,0:T(8,128)(2,1)}, u32[]{:S(2)}) copy-start(bf16[1,32,384]{2,1,0:T(8,128)(2,1)} %param.12) | copy-start | bytes 73732
  9.4 13.4 %copy-start.6 = (bf16[1,32,384]{2,1,0:T(8,128)(2,1)S(1)}, bf16[1,32,384]{2,1,0:T(8,128)(2,1)}, u32[]{:S(2)}) copy-start(bf16[1,32,384]{2,1,0:T(8,128)(2,1)} %param.11) | copy-start | bytes 73732
  9.4 107.3 %all-to-all-start = ((bf16[16,64,2048]{2,1,0:T(8,128)(2,1)}), bf16[16,64,2048]{2,1,0:T(8,128)(2,1)}, u32[]{:S(2)}, u32[]{:S(2)}) async-start(bf16[16,64,2048]{2,1,0:T(8,128)(2,1)} %bitcast.102), calls=%async_computation | async-start | bytes 8388608 | tf_op jit(solution)/shard_map/all_to_all | solution.py:72
  22.9 6.7 %collective-permute-start = (bf16[32,1152]{1,0:T(8,128)(2,1)S(1)}, bf16[32,1152]{1,0:T(8,128)(2,1)S(1)}, u32[]{:S(2)}, u32[]{:S(2)}) collective-permute-start(bf16[32,1152]{1,0:T(8,128)(2,1)S(1)} %pad_maximum_fusion.5), channel_id=1, source_target_pairs={{0,64},{64,128},{128,192},{192,256},{256,320},{320,384},{384,448},... | collective-permute-start | bytes 221192 | tf_op jit(solution)/shard_map/ppermute | solution.py:49
  29.5 7.4 %collective-permute-start.1 = (bf16[32,1152]{1,0:T(8,128)(2,1)S(1)}, bf16[32,1152]{1,0:T(8,128)(2,1)S(1)}, u32[]{:S(2)}, u32[]{:S(2)}) collective-permute-start(bf16[32,1152]{1,0:T(8,128)(2,1)S(1)} %collective-permute-done), channel_id=1, source_target_pairs={{0,64},{64,128},{128,192},{192,256},{256,320},{320,384},{384,448},... | collective-permute-start | bytes 221192 | tf_op jit(solution)/shard_map/ppermute | solution.py:49
  37.0 7.4 %collective-permute-start.2 = (bf16[32,1152]{1,0:T(8,128)(2,1)S(1)}, bf16[32,1152]{1,0:T(8,128)(2,1)S(1)}, u32[]{:S(2)}, u32[]{:S(2)}) collective-permute-start(bf16[32,1152]{1,0:T(8,128)(2,1)S(1)} %collective-permute-done.1), channel_id=1, source_target_pairs={{0,64},{64,128},{128,192},{192,256},{256,320},{320,384},{384,448},... | collective-permute-start | bytes 221192 | tf_op jit(solution)/shard_map/ppermute | solution.py:49
  44.4 7.4 %collective-permute-start.3 = (bf16[32,1152]{1,0:T(8,128)(2,1)S(1)}, bf16[32,1152]{1,0:T(8,128)(2,1)S(1)}, u32[]{:S(2)}, u32[]{:S(2)}) collective-permute-start(bf16[32,1152]{1,0:T(8,128)(2,1)S(1)} %collective-permute-done.2), channel_id=1, source_target_pairs={{0,64},{64,128},{128,192},{192,256},{256,320},{320,384},{384,448},... | collective-permute-start | bytes 221192 | tf_op jit(solution)/shard_map/ppermute | solution.py:49
  51.9 7.4 %collective-permute-start.4 = (bf16[32,1152]{1,0:T(8,128)(2,1)S(1)}, bf16[32,1152]{1,0:T(8,128)(2,1)S(1)}, u32[]{:S(2)}, u32[]{:S(2)}) collective-permute-start(bf16[32,1152]{1,0:T(8,128)(2,1)S(1)} %collective-permute-done.3), channel_id=1, source_target_pairs={{0,64},{64,128},{128,192},{192,256},{256,320},{320,384},{384,448},... | collective-permute-start | bytes 221192 | tf_op jit(solution)/shard_map/ppermute | solution.py:49
  59.3 7.4 %collective-permute-start.5 = (bf16[32,1152]{1,0:T(8,128)(2,1)S(1)}, bf16[32,1152]{1,0:T(8,128)(2,1)S(1)}, u32[]{:S(2)}, u32[]{:S(2)}) collective-permute-start(bf16[32,1152]{1,0:T(8,128)(2,1)S(1)} %collective-permute-done.4), channel_id=1, source_target_pairs={{0,64},{64,128},{128,192},{192,256},{256,320},{320,384},{384,448},... | collective-permute-start | bytes 221192 | tf_op jit(solution)/shard_map/ppermute | solution.py:49
  66.8 7.4 %collective-permute-start.6 = (bf16[32,1152]{1,0:T(8,128)(2,1)S(1)}, bf16[32,1152]{1,0:T(8,128)(2,1)S(1)}, u32[]{:S(2)}, u32[]{:S(2)}) collective-permute-start(bf16[32,1152]{1,0:T(8,128)(2,1)S(1)} %collective-permute-done.5), channel_id=1, source_target_pairs={{0,64},{64,128},{128,192},{192,256},{256,320},{320,384},{384,448},... | collective-permute-start | bytes 221192 | tf_op jit(solution)/shard_map/ppermute | solution.py:49
  75.0 24.4 %collective-permute-start.7 = (bf16[8,32,1152]{2,1,0:T(8,128)(2,1)S(1)}, bf16[8,32,1152]{2,1,0:T(8,128)(2,1)S(1)}, u32[]{:S(2)}, u32[]{:S(2)}) collective-permute-start(bf16[8,32,1152]{2,1,0:T(8,128)(2,1)S(1)} %broadcast_select_fusion), channel_id=1, source_target_pairs={{0,32},{32,0},{1,33},{33,1},{2,34},{34,2},{3,35},{35,3},{4,36},{36... | collective-permute-start | bytes 1769480 | tf_op jit(solution)/shard_map/ppermute | solution.py:41
  100.8 4.9 %collective-permute-start.8 = (bf16[2,8,32,1152]{3,2,0,1:T(8,128)(2,1)}, bf16[2,8,32,1152]{3,2,0,1:T(8,128)(2,1)S(1)}, u32[]{:S(2)}, u32[]{:S(2)}) collective-permute-start(bf16[2,8,32,1152]{3,2,0,1:T(8,128)(2,1)} %pad_maximum_fusion.2), channel_id=1, source_target_pairs={{0,16},{16,0},{1,17},{17,1},{2,18},{18,2},{3,19},{19,3},{4,20},{20... | collective-permute-start | bytes 3538952 | tf_op jit(solution)/shard_map/ppermute | solution.py:41
  120.6 4.4 %copy-start.10 = (f32[1024,768]{0,1:T(8,128)}, f32[1024,768]{0,1:T(8,128)S(1)}, u32[]{:S(2)}) copy-start(f32[1024,768]{0,1:T(8,128)S(1)} %fusion.4) | copy-start | bytes 9437188
  125.0 59.4 %all-to-all-start.1 = ((bf16[16,64,1024]{2,1,0:T(8,128)(2,1)}), bf16[16,64,1024]{2,1,0:T(8,128)(2,1)}, u32[]{:S(2)}, u32[]{:S(2)}) async-start(bf16[16,64,1024]{2,1,0:T(8,128)(2,1)} %bitcast.25), calls=%async_computation.1 | async-start | bytes 4194304 | tf_op jit(solution)/shard_map/all_to_all | solution.py:72
  139.8 4.0 %copy-start.11 = (bf16[1024,384]{0,1:T(8,128)(2,1)}, bf16[1024,384]{0,1:T(8,128)(2,1)S(1)}, u32[]{:S(2)}) copy-start(bf16[1024,384]{0,1:T(8,128)(2,1)S(1)} %get-tuple-element.7) | copy-start | bytes 2359300
  139.8 4.0 %copy-start.13 = (bf16[1024,384]{0,1:T(8,128)(2,1)}, bf16[1024,384]{0,1:T(8,128)(2,1)S(1)}, u32[]{:S(2)}) copy-start(bf16[1024,384]{0,1:T(8,128)(2,1)S(1)} %get-tuple-element.8) | copy-start | bytes 2359300
  145.6 5.4 %collective-permute-start.9 = (f32[16,32,768]{2,1,0:T(8,128)S(1)}, f32[16,32,768]{2,1,0:T(8,128)}, u32[]{:S(2)}, u32[]{:S(2)}) collective-permute-start(f32[16,32,768]{2,1,0:T(8,128)S(1)} %dynamic-slice_bitcast_fusion), channel_id=1, source_target_pairs={{0,16},{16,0},{1,17},{17,1},{2,18},{18,2},{3,19},{19,3},{4,20},{20... | collective-permute-start | bytes 4718600 | tf_op jit(solution)/shard_map/ppermute | solution.py:133
  151.0 5.3 %copy-start.2 = (bf16[2,2,8,32,1152]{4,3,0,1,2:T(8,128)(2,1)S(1)}, bf16[2,2,8,32,1152]{4,3,0,1,2:T(8,128)(2,1)}, u32[]{:S(2)}) copy-start(bf16[2,2,8,32,1152]{4,3,0,1,2:T(8,128)(2,1)} %pad_maximum_fusion) | copy-start | bytes 7077892
  153.3 6.3 %copy-start = (f32[16,32,768]{2,1,0:T(8,128)}, f32[16,32,768]{2,1,0:T(8,128)S(1)}, u32[]{:S(2)}) copy-start(f32[16,32,768]{2,1,0:T(8,128)S(1)} %bitcast_add_fusion) | copy-start | bytes 4718596
  153.4 38.4 %collective-permute-start.10 = (f32[8,32,768]{2,1,0:T(8,128)S(1)}, f32[8,32,768]{2,1,0:T(8,128)}, u32[]{:S(2)}, u32[]{:S(2)}) collective-permute-start(f32[8,32,768]{2,1,0:T(8,128)S(1)} %dynamic-slice_bitcast_fusion.1), channel_id=1, source_target_pairs={{0,32},{32,0},{1,33},{33,1},{2,34},{34,2},{3,35},{35,3},{4,36},{36... | collective-permute-start | bytes 2359304 | tf_op jit(solution)/shard_map/ppermute | solution.py:41
  184.4 65.6 %all-to-all-start.2 = ((bf16[16,64,1024]{2,1,0:T(8,128)(2,1)}), bf16[16,64,1024]{2,1,0:T(8,128)(2,1)S(1)}, u32[]{:S(2)}, u32[]{:S(2)}) async-start(bf16[16,64,1024]{2,1,0:T(8,128)(2,1)} %bitcast.112), calls=%async_computation.2 | async-start | bytes 4194304 | tf_op jit(solution)/shard_map/all_to_all | solution.py:72
  191.8 37.8 %copy-start.7 = (s32[128,2]{0,1:T(2,128)S(1)}, s32[128,2]{0,1:T(2,128)}, u32[]{:S(2)}) copy-start(s32[128,2]{0,1:T(2,128)} %param.8) | copy-start | bytes 3076
  193.3 51.8 %copy-start.8 = (f32[128,2]{0,1:T(2,128)S(1)}, f32[128,2]{0,1:T(2,128)}, u32[]{:S(2)}) copy-start(f32[128,2]{0,1:T(2,128)} %param.9) | copy-start | bytes 3076
  193.3 7.5 %collective-permute-start.11 = (f32[32,768]{1,0:T(8,128)S(1)}, f32[32,768]{1,0:T(8,128)S(1)}, u32[]{:S(2)}, u32[]{:S(2)}) collective-permute-start(f32[32,768]{1,0:T(8,128)S(1)} %dynamic-slice_bitcast_fusion.2), channel_id=1, source_target_pairs={{0,64},{64,128},{128,192},{192,256},{256,320},{320,384},{384,448},... | collective-permute-start | bytes 294920 | tf_op jit(solution)/shard_map/ppermute | solution.py:60
  200.8 7.7 %collective-permute-start.12 = (f32[32,768]{1,0:T(8,128)S(1)}, f32[32,768]{1,0:T(8,128)S(1)}, u32[]{:S(2)}, u32[]{:S(2)}) collective-permute-start(f32[32,768]{1,0:T(8,128)S(1)} %bitcast_add_fusion.8), channel_id=1, source_target_pairs={{0,64},{64,128},{128,192},{192,256},{256,320},{320,384},{384,448},... | collective-permute-start | bytes 294920 | tf_op jit(solution)/shard_map/ppermute | solution.py:60
  208.5 7.7 %collective-permute-start.13 = (f32[32,768]{1,0:T(8,128)S(1)}, f32[32,768]{1,0:T(8,128)S(1)}, u32[]{:S(2)}, u32[]{:S(2)}) collective-permute-start(f32[32,768]{1,0:T(8,128)S(1)} %bitcast_add_fusion.7), channel_id=1, source_target_pairs={{0,64},{64,128},{128,192},{192,256},{256,320},{320,384},{384,448},... | collective-permute-start | bytes 294920 | tf_op jit(solution)/shard_map/ppermute | solution.py:60
  216.3 7.7 %collective-permute-start.14 = (f32[32,768]{1,0:T(8,128)S(1)}, f32[32,768]{1,0:T(8,128)S(1)}, u32[]{:S(2)}, u32[]{:S(2)}) collective-permute-start(f32[32,768]{1,0:T(8,128)S(1)} %bitcast_add_fusion.6), channel_id=1, source_target_pairs={{0,64},{64,128},{128,192},{192,256},{256,320},{320,384},{384,448},... | collective-permute-start | bytes 294920 | tf_op jit(solution)/shard_map/ppermute | solution.py:60
  224.0 7.7 %collective-permute-start.15 = (f32[32,768]{1,0:T(8,128)S(1)}, f32[32,768]{1,0:T(8,128)S(1)}, u32[]{:S(2)}, u32[]{:S(2)}) collective-permute-start(f32[32,768]{1,0:T(8,128)S(1)} %bitcast_add_fusion.5), channel_id=1, source_target_pairs={{0,64},{64,128},{128,192},{192,256},{256,320},{320,384},{384,448},... | collective-permute-start | bytes 294920 | tf_op jit(solution)/shard_map/ppermute | solution.py:60
  231.8 7.7 %collective-permute-start.16 = (f32[32,768]{1,0:T(8,128)S(1)}, f32[32,768]{1,0:T(8,128)S(1)}, u32[]{:S(2)}, u32[]{:S(2)}) collective-permute-start(f32[32,768]{1,0:T(8,128)S(1)} %bitcast_add_fusion.4), channel_id=1, source_target_pairs={{0,64},{64,128},{128,192},{192,256},{256,320},{320,384},{384,448},... | collective-permute-start | bytes 294920 | tf_op jit(solution)/shard_map/ppermute | solution.py:60
  239.5 9.9 %collective-permute-start.17 = (f32[32,768]{1,0:T(8,128)S(1)}, f32[32,768]{1,0:T(8,128)S(1)}, u32[]{:S(2)}, u32[]{:S(2)}) collective-permute-start(f32[32,768]{1,0:T(8,128)S(1)} %bitcast_add_fusion.3), channel_id=1, source_target_pairs={{0,64},{64,128},{128,192},{192,256},{256,320},{320,384},{384,448},... | collective-permute-start | bytes 294920 | tf_op jit(solution)/shard_map/ppermute | solution.py:60
  (4 other events, 10.8 us)

commit v14 on v11

--- a/solution.py
+++ b/solution.py
@@ -146,20 +146,15 @@
     returned = trade_rows(back.reshape(expert_total, capacity, 2 * feature_total)).reshape(
         expert_total * capacity, 2 * feature_total
     )
-    pick_rows = lax.dot_general(
-        select,
-        returned[:, :feature_total],
-        (((0,), (0,)), ((), ())),
-        preferred_element_type=jnp.float32,
-    )
     token_select = jnp.any(
         slot_index.reshape(tok_count, top_count)[:, :, None]
         == jnp.arange(expert_total * capacity, dtype=jnp.int32)[None, None, :],
         axis=1,
     ).astype(jnp.bfloat16)
-    token_grad = jnp.dot(
-        token_select, returned[:, feature_total:], preferred_element_type=jnp.float32
-    ).astype(jnp.bfloat16)
+    chooser = jnp.concatenate([select.T, token_select], axis=0)
+    chosen = jnp.dot(chooser, returned, preferred_element_type=jnp.float32)
+    pick_rows = chosen[:pick_total, :feature_total]
+    token_grad = chosen[pick_total:, feature_total:].astype(jnp.bfloat16)
     pick_wide = pick_rows.reshape(tok_count, top_count, feature_total)
     layer_output = jnp.sum(combine[:, :, None] * pick_wide, axis=1).astype(jnp.bfloat16)
     combine_grad = jnp.sum(upstream_wide[:, None, :] * pick_wide, axis=2)

time: 248 us -> 250 us (level)
  local copies, waits for them, and re-layouts: 10.1 us -> 13.3 us
    unnamed x31 -> x33, local copies, waits for them, and re-layouts: 4.1 us -> 5.5 us
    dot_general x2 -> x1, matrix products: 5.18 us -> 3.97 us  [shards(): chosen = jnp.dot(chooser, returned, preferred_element_type=jnp.float32)]
where the time goes in v14:
time: 250 us; the launch traced here: 248 us
  waiting for transfers between devices  138 us (55%)
  starting transfers between devices  63.5 us (25%)
  matrix products  20.4 us (8%)
  local copies, waits for them, and re-layouts  13.3 us (5%)
  other arithmetic  10.7 us (4%)
    ppermute x3, waiting for transfers between devices, swap_partner(): return lax.ppermute(values, axis, perm=[(0, 1), (1, 0)])  50.1 us
    ppermute x7, waiting for transfers between devices, ring_gather(): lax.ppermute(moving, axis, perm=[(i, (i + 1) % size) for i in range(size)])  32.5 us
    ppermute x7, waiting for transfers between devices, ring_reduce_scatter(): lax.ppermute(carry, axis, perm=[(i, (i + 1) % size) for i in range(size)])  28.4 us
    all_to_all x2, waiting for transfers between devices, trade_rows(): lax.all_to_all(buffer, EXPERT_AXES, split_axis=0, concat_axis=0, tiled=True)  23.4 us
    all_to_all x2, starting transfers between devices, trade_rows(): lax.all_to_all(buffer, EXPERT_AXES, split_axis=0, concat_axis=0, tiled=True)  21.4 us
    ppermute x7, starting transfers between devices, ring_reduce_scatter(): lax.ppermute(carry, axis, perm=[(i, (i + 1) % size) for i in range(size)])  15.6 us
    ppermute x7, starting transfers between devices, ring_gather(): lax.ppermute(moving, axis, perm=[(i, (i + 1) % size) for i in range(size)])  14.7 us
    ppermute x3, starting transfers between devices, swap_partner(): return lax.ppermute(values, axis, perm=[(0, 1), (1, 0)])  8.95 us
  transfers between devices with their start and end apart: 20, of which 19 were waited for; matrix products, arithmetic and copies ran while one was open for 8% of the time, Pallas kernels for 0%

profile of v14, /device:TPU:1, one launch (start us, length us, event | category | flops | bytes accessed | tf_op | source)
XLA Modules:
  0.0 247.6 jit_solution(1368300383294932560)
XLA Ops:
  6.2 3.2 %convolution_convert_fusion = bf16[1024,2048]{1,0:T(8,128)(2,1)} fusion(bf16[256,1024]{1,0:T(8,128)(2,1)S(1)} %multiply_convert_fusion.3, bf16[256,1024]{1,0:T(8,128)(2,1)S(1)} %reshape.139, s32[256]{0:T(256)S(1)} %multiply_add_fusion.1), kind=kOutput, calls=%fused_computation.2 | convolution fusion | flops 1078198272 | bytes 5243904 | tf_op jit(solution)/shard_map/dot_general | solution.py:117
  9.4 13.6 %all-to-all-start = ((bf16[16,64,2048]{2,1,0:T(8,128)(2,1)}), bf16[16,64,2048]{2,1,0:T(8,128)(2,1)}, u32[]{:S(2)}, u32[]{:S(2)}) async-start(bf16[16,64,2048]{2,1,0:T(8,128)(2,1)} %bitcast.91), calls=%async_computation | async-start | bytes 8388608 | tf_op jit(solution)/shard_map/all_to_all | solution.py:72
  23.1 3.2 %collective-permute-start = (bf16[32,1152]{1,0:T(8,128)(2,1)S(1)}, bf16[32,1152]{1,0:T(8,128)(2,1)S(1)}, u32[]{:S(2)}, u32[]{:S(2)}) collective-permute-start(bf16[32,1152]{1,0:T(8,128)(2,1)S(1)} %pad_maximum_fusion.6), channel_id=1, source_target_pairs={{0,64},{64,128},{128,192},{192,256},{256,320},{320,384},{384,448},... | collective-permute-start | bytes 221192 | tf_op jit(solution)/shard_map/ppermute | solution.py:49
  26.4 3.9 %collective-permute-done = bf16[32,1152]{1,0:T(8,128)(2,1)S(1)} collective-permute-done((bf16[32,1152]{1,0:T(8,128)(2,1)S(1)}, bf16[32,1152]{1,0:T(8,128)(2,1)S(1)}, u32[]{:S(2)}, u32[]{:S(2)}) %collective-permute-start) | collective-permute-done | bytes 73760 | tf_op jit(solution)/shard_map/ppermute | solution.py:49
  32.3 4.8 %collective-permute-done.1 = bf16[32,1152]{1,0:T(8,128)(2,1)S(1)} collective-permute-done((bf16[32,1152]{1,0:T(8,128)(2,1)S(1)}, bf16[32,1152]{1,0:T(8,128)(2,1)S(1)}, u32[]{:S(2)}, u32[]{:S(2)}) %collective-permute-start.1) | collective-permute-done | bytes 73760 | tf_op jit(solution)/shard_map/ppermute | solution.py:49
  39.0 4.8 %collective-permute-done.2 = bf16[32,1152]{1,0:T(8,128)(2,1)S(1)} collective-permute-done((bf16[32,1152]{1,0:T(8,128)(2,1)S(1)}, bf16[32,1152]{1,0:T(8,128)(2,1)S(1)}, u32[]{:S(2)}, u32[]{:S(2)}) %collective-permute-start.2) | collective-permute-done | bytes 73760 | tf_op jit(solution)/shard_map/ppermute | solution.py:49
  45.6 4.8 %collective-permute-done.3 = bf16[32,1152]{1,0:T(8,128)(2,1)S(1)} collective-permute-done((bf16[32,1152]{1,0:T(8,128)(2,1)S(1)}, bf16[32,1152]{1,0:T(8,128)(2,1)S(1)}, u32[]{:S(2)}, u32[]{:S(2)}) %collective-permute-start.3) | collective-permute-done | bytes 73760 | tf_op jit(solution)/shard_map/ppermute | solution.py:49
  52.3 4.8 %collective-permute-done.4 = bf16[32,1152]{1,0:T(8,128)(2,1)S(1)} collective-permute-done((bf16[32,1152]{1,0:T(8,128)(2,1)S(1)}, bf16[32,1152]{1,0:T(8,128)(2,1)S(1)}, u32[]{:S(2)}, u32[]{:S(2)}) %collective-permute-start.4) | collective-permute-done | bytes 73760 | tf_op jit(solution)/shard_map/ppermute | solution.py:49
  59.0 4.8 %collective-permute-done.5 = bf16[32,1152]{1,0:T(8,128)(2,1)S(1)} collective-permute-done((bf16[32,1152]{1,0:T(8,128)(2,1)S(1)}, bf16[32,1152]{1,0:T(8,128)(2,1)S(1)}, u32[]{:S(2)}, u32[]{:S(2)}) %collective-permute-start.5) | collective-permute-done | bytes 73760 | tf_op jit(solution)/shard_map/ppermute | solution.py:49
  65.7 4.8 %collective-permute-done.6 = bf16[32,1152]{1,0:T(8,128)(2,1)S(1)} collective-permute-done((bf16[32,1152]{1,0:T(8,128)(2,1)S(1)}, bf16[32,1152]{1,0:T(8,128)(2,1)S(1)}, u32[]{:S(2)}, u32[]{:S(2)}) %collective-permute-start.6) | collective-permute-done | bytes 73760 | tf_op jit(solution)/shard_map/ppermute | solution.py:49
  73.4 25.1 %collective-permute-done.7 = bf16[8,32,1152]{2,1,0:T(8,128)(2,1)S(1)} collective-permute-done((bf16[8,32,1152]{2,1,0:T(8,128)(2,1)S(1)}, bf16[8,32,1152]{2,1,0:T(8,128)(2,1)S(1)}, u32[]{:S(2)}, u32[]{:S(2)}) %collective-permute-start.7) | collective-permute-done | bytes 589856 | tf_op jit(solution)/shard_map/ppermute | solution.py:41
  99.8 4.7 %collective-permute-start.8 = (bf16[2,8,32,1152]{3,2,0,1:T(8,128)(2,1)}, bf16[2,8,32,1152]{3,2,0,1:T(8,128)(2,1)S(1)}, u32[]{:S(2)}, u32[]{:S(2)}) collective-permute-start(bf16[2,8,32,1152]{3,2,0,1:T(8,128)(2,1)} %pad_maximum_fusion.3), channel_id=1, source_target_pairs={{0,16},{16,0},{1,17},{17,1},{2,18},{18,2},{3,19},{19,3},{4,20},{20... | collective-permute-start | bytes 3538952 | tf_op jit(solution)/shard_map/ppermute | solution.py:41
  104.5 2.5 collective-permute-done.8
  107.5 11.7 %all-to-all-done = bf16[16,64,2048]{2,1,0:T(8,128)(2,1)} async-done(((bf16[16,64,2048]{2,1,0:T(8,128)(2,1)}), bf16[16,64,2048]{2,1,0:T(8,128)(2,1)}, u32[]{:S(2)}, u32[]{:S(2)}) %all-to-all-start) | async-done | bytes 4194336 | tf_op jit(solution)/shard_map/all_to_all | solution.py:72
  119.3 3.5 %fusion.4 = f32[1024,768]{0,1:T(8,128)S(1)} fusion(bf16[1024,2048]{1,0:T(8,128)(2,1)} %bitcast.2, bf16[1024,1152]{1,0:T(8,128)(2,1)S(1)} %bitcast.97), kind=kOutput, calls=%fused_computation.10 | convolution fusion | flops 1610612736 | bytes 6815744 | tf_op jit(solution)/shard_map/dot_general | solution.py:16
  122.7 3.1 %multiply_convert_fusion.1 = (bf16[1024,384]{0,1:T(8,128)(2,1)S(1)}, bf16[1024,384]{0,1:T(8,128)(2,1)S(1)}) fusion(f32[1024,768]{0,1:T(8,128)S(1)} %fusion.4, bf16[1024,1152]{1,0:T(8,128)(2,1)S(1)} %bitcast.98, bf16[1024,2048]{1,0:T(8,128)(2,1)} %bitcast.2), kind=kOutput, calls=%fused_computation.16 | convolution fusion | flops 810418176 | bytes 7602176 | tf_op jit(solution)/shard_map/dot_general | solution.py:27
  129.1 2.4 pad_maximum_fusion
  131.5 7.8 %all-to-all-start.1 = ((bf16[16,64,2048]{2,1,0:T(8,128)(2,1)}), bf16[16,64,2048]{2,1,0:T(8,128)(2,1)}, u32[]{:S(2)}, u32[]{:S(2)}) async-start(bf16[16,64,2048]{2,1,0:T(8,128)(2,1)} %bitcast.92), calls=%async_computation.1 | async-start | bytes 8388608 | tf_op jit(solution)/shard_map/all_to_all | solution.py:72
  139.3 3.4 %fusion.2 = f32[1024,768]{1,0:T(8,128)S(1)} fusion(bf16[1024,2048]{1,0:T(8,128)(2,1)} %bitcast.2, bf16[1024,384]{0,1:T(8,128)(2,1)S(1)} %copy-done.11, bf16[1024,384]{0,1:T(8,128)(2,1)S(1)} %copy-done.9), kind=kOutput, calls=%fused_computation.8 | convolution fusion | flops 1613758464 | bytes 6815744 | tf_op jit(solution)/shard_map/dot_general | solution.py:125
  144.6 3.0 %collective-permute-start.9 = (f32[16,32,768]{2,1,0:T(8,128)S(1)}, f32[16,32,768]{2,1,0:T(8,128)}, u32[]{:S(2)}, u32[]{:S(2)}) collective-permute-start(f32[16,32,768]{2,1,0:T(8,128)S(1)} %dynamic-slice_bitcast_fusion), channel_id=1, source_target_pairs={{0,16},{16,0},{1,17},{17,1},{2,18},{18,2},{3,19},{19,3},{4,20},{20... | collective-permute-start | bytes 4718600 | tf_op jit(solution)/shard_map/ppermute | solution.py:133
  147.6 3.1 %collective-permute-done.9 = f32[16,32,768]{2,1,0:T(8,128)} collective-permute-done((f32[16,32,768]{2,1,0:T(8,128)S(1)}, f32[16,32,768]{2,1,0:T(8,128)}, u32[]{:S(2)}, u32[]{:S(2)}) %collective-permute-start.9) | collective-permute-done | bytes 1572896 | tf_op jit(solution)/shard_map/ppermute | solution.py:133
  152.9 2.2 collective-permute-start.10
  155.1 22.5 %collective-permute-done.10 = f32[8,32,768]{2,1,0:T(8,128)} collective-permute-done((f32[8,32,768]{2,1,0:T(8,128)S(1)}, f32[8,32,768]{2,1,0:T(8,128)}, u32[]{:S(2)}, u32[]{:S(2)}) %collective-permute-start.10) | collective-permute-done | bytes 786464 | tf_op jit(solution)/shard_map/ppermute | solution.py:41
  178.9 3.8 %collective-permute-start.11 = (f32[32,768]{1,0:T(8,128)S(1)}, f32[32,768]{1,0:T(8,128)S(1)}, u32[]{:S(2)}, u32[]{:S(2)}) collective-permute-start(f32[32,768]{1,0:T(8,128)S(1)} %dynamic-slice_bitcast_fusion.2), channel_id=1, source_target_pairs={{0,64},{64,128},{128,192},{192,256},{256,320},{320,384},{384,448},... | collective-permute-start | bytes 294920 | tf_op jit(solution)/shard_map/ppermute | solution.py:60
  182.7 3.8 %collective-permute-done.11 = f32[32,768]{1,0:T(8,128)S(1)} collective-permute-done((f32[32,768]{1,0:T(8,128)S(1)}, f32[32,768]{1,0:T(8,128)S(1)}, u32[]{:S(2)}, u32[]{:S(2)}) %collective-permute-start.11) | collective-permute-done | bytes 98336 | tf_op jit(solution)/shard_map/ppermute | solution.py:60
  188.5 5.0 %collective-permute-done.12 = f32[32,768]{1,0:T(8,128)S(1)} collective-permute-done((f32[32,768]{1,0:T(8,128)S(1)}, f32[32,768]{1,0:T(8,128)S(1)}, u32[]{:S(2)}, u32[]{:S(2)}) %collective-permute-start.12) | collective-permute-done | bytes 98336 | tf_op jit(solution)/shard_map/ppermute | solution.py:60
  195.5 5.0 %collective-permute-done.13 = f32[32,768]{1,0:T(8,128)S(1)} collective-permute-done((f32[32,768]{1,0:T(8,128)S(1)}, f32[32,768]{1,0:T(8,128)S(1)}, u32[]{:S(2)}, u32[]{:S(2)}) %collective-permute-start.13) | collective-permute-done | bytes 98336 | tf_op jit(solution)/shard_map/ppermute | solution.py:60
  202.9 4.6 %collective-permute-done.14 = f32[32,768]{1,0:T(8,128)S(1)} collective-permute-done((f32[32,768]{1,0:T(8,128)S(1)}, f32[32,768]{1,0:T(8,128)S(1)}, u32[]{:S(2)}, u32[]{:S(2)}) %collective-permute-start.14) | collective-permute-done | bytes 98336 | tf_op jit(solution)/shard_map/ppermute | solution.py:60
  209.5 5.0 %collective-permute-done.15 = f32[32,768]{1,0:T(8,128)S(1)} collective-permute-done((f32[32,768]{1,0:T(8,128)S(1)}, f32[32,768]{1,0:T(8,128)S(1)}, u32[]{:S(2)}, u32[]{:S(2)}) %collective-permute-start.15) | collective-permute-done | bytes 98336 | tf_op jit(solution)/shard_map/ppermute | solution.py:60
  216.6 5.0 %collective-permute-done.16 = f32[32,768]{1,0:T(8,128)S(1)} collective-permute-done((f32[32,768]{1,0:T(8,128)S(1)}, f32[32,768]{1,0:T(8,128)S(1)}, u32[]{:S(2)}, u32[]{:S(2)}) %collective-permute-start.16) | collective-permute-done | bytes 98336 | tf_op jit(solution)/shard_map/ppermute | solution.py:60
  223.8 11.7 %all-to-all-done.1 = bf16[16,64,2048]{2,1,0:T(8,128)(2,1)} async-done(((bf16[16,64,2048]{2,1,0:T(8,128)(2,1)}), bf16[16,64,2048]{2,1,0:T(8,128)(2,1)}, u32[]{:S(2)}, u32[]{:S(2)}) %all-to-all-start.1) | async-done | bytes 4194336 | tf_op jit(solution)/shard_map/all_to_all | solution.py:72
  235.5 4.0 %fusion.7 = f32[384,2048]{1,0:T(8,128)S(1)} fusion(bf16[1024,2048]{1,0:T(8,128)(2,1)} %bitcast.25, pred[128,1024]{1,0:T(8,128)(4,1)S(1)} %fusion.16, pred[256,1024]{1,0:T(32,128)(4,1)S(1)} %iota_compare_fusion.2), kind=kOutput, calls=%fused_computation.20 | convolution fusion | flops 1611005952 | bytes 7733248 | tf_op jit(solution)/shard_map/dot_general | solution.py:155
  (100 shorter events, 50.1 us)
Async XLA Ops:
  0.6 4.4 %copy-start.2 = (bf16[128,1024]{1,0:T(8,128)(2,1)S(1)}, bf16[128,1024]{1,0:T(8,128)(2,1)}, u32[]{:S(2)}) copy-start(bf16[128,1024]{1,0:T(8,128)(2,1)} %param.10) | copy-start | bytes 786436
  9.4 13.6 %copy-start.4 = (bf16[1,32,384]{2,1,0:T(8,128)(2,1)S(1)}, bf16[1,32,384]{2,1,0:T(8,128)(2,1)}, u32[]{:S(2)}) copy-start(bf16[1,32,384]{2,1,0:T(8,128)(2,1)} %param.13) | copy-start | bytes 73732
  9.4 13.6 %copy-start.5 = (bf16[1,32,384]{2,1,0:T(8,128)(2,1)S(1)}, bf16[1,32,384]{2,1,0:T(8,128)(2,1)}, u32[]{:S(2)}) copy-start(bf16[1,32,384]{2,1,0:T(8,128)(2,1)} %param.12) | copy-start | bytes 73732
  9.4 13.6 %copy-start.6 = (bf16[1,32,384]{2,1,0:T(8,128)(2,1)S(1)}, bf16[1,32,384]{2,1,0:T(8,128)(2,1)}, u32[]{:S(2)}) copy-start(bf16[1,32,384]{2,1,0:T(8,128)(2,1)} %param.11) | copy-start | bytes 73732
  9.4 109.8 %all-to-all-start = ((bf16[16,64,2048]{2,1,0:T(8,128)(2,1)}), bf16[16,64,2048]{2,1,0:T(8,128)(2,1)}, u32[]{:S(2)}, u32[]{:S(2)}) async-start(bf16[16,64,2048]{2,1,0:T(8,128)(2,1)} %bitcast.91), calls=%async_computation | async-start | bytes 8388608 | tf_op jit(solution)/shard_map/all_to_all | solution.py:72
  23.1 7.2 %collective-permute-start = (bf16[32,1152]{1,0:T(8,128)(2,1)S(1)}, bf16[32,1152]{1,0:T(8,128)(2,1)S(1)}, u32[]{:S(2)}, u32[]{:S(2)}) collective-permute-start(bf16[32,1152]{1,0:T(8,128)(2,1)S(1)} %pad_maximum_fusion.6), channel_id=1, source_target_pairs={{0,64},{64,128},{128,192},{192,256},{256,320},{320,384},{384,448},... | collective-permute-start | bytes 221192 | tf_op jit(solution)/shard_map/ppermute | solution.py:49
  30.3 6.7 %collective-permute-start.1 = (bf16[32,1152]{1,0:T(8,128)(2,1)S(1)}, bf16[32,1152]{1,0:T(8,128)(2,1)S(1)}, u32[]{:S(2)}, u32[]{:S(2)}) collective-permute-start(bf16[32,1152]{1,0:T(8,128)(2,1)S(1)} %collective-permute-done), channel_id=1, source_target_pairs={{0,64},{64,128},{128,192},{192,256},{256,320},{320,384},{384,448},... | collective-permute-start | bytes 221192 | tf_op jit(solution)/shard_map/ppermute | solution.py:49
  37.0 6.7 %collective-permute-start.2 = (bf16[32,1152]{1,0:T(8,128)(2,1)S(1)}, bf16[32,1152]{1,0:T(8,128)(2,1)S(1)}, u32[]{:S(2)}, u32[]{:S(2)}) collective-permute-start(bf16[32,1152]{1,0:T(8,128)(2,1)S(1)} %collective-permute-done.1), channel_id=1, source_target_pairs={{0,64},{64,128},{128,192},{192,256},{256,320},{320,384},{384,448},... | collective-permute-start | bytes 221192 | tf_op jit(solution)/shard_map/ppermute | solution.py:49
  43.7 6.7 %collective-permute-start.3 = (bf16[32,1152]{1,0:T(8,128)(2,1)S(1)}, bf16[32,1152]{1,0:T(8,128)(2,1)S(1)}, u32[]{:S(2)}, u32[]{:S(2)}) collective-permute-start(bf16[32,1152]{1,0:T(8,128)(2,1)S(1)} %collective-permute-done.2), channel_id=1, source_target_pairs={{0,64},{64,128},{128,192},{192,256},{256,320},{320,384},{384,448},... | collective-permute-start | bytes 221192 | tf_op jit(solution)/shard_map/ppermute | solution.py:49
  50.4 6.7 %collective-permute-start.4 = (bf16[32,1152]{1,0:T(8,128)(2,1)S(1)}, bf16[32,1152]{1,0:T(8,128)(2,1)S(1)}, u32[]{:S(2)}, u32[]{:S(2)}) collective-permute-start(bf16[32,1152]{1,0:T(8,128)(2,1)S(1)} %collective-permute-done.3), channel_id=1, source_target_pairs={{0,64},{64,128},{128,192},{192,256},{256,320},{320,384},{384,448},... | collective-permute-start | bytes 221192 | tf_op jit(solution)/shard_map/ppermute | solution.py:49
  57.1 6.7 %collective-permute-start.5 = (bf16[32,1152]{1,0:T(8,128)(2,1)S(1)}, bf16[32,1152]{1,0:T(8,128)(2,1)S(1)}, u32[]{:S(2)}, u32[]{:S(2)}) collective-permute-start(bf16[32,1152]{1,0:T(8,128)(2,1)S(1)} %collective-permute-done.4), channel_id=1, source_target_pairs={{0,64},{64,128},{128,192},{192,256},{256,320},{320,384},{384,448},... | collective-permute-start | bytes 221192 | tf_op jit(solution)/shard_map/ppermute | solution.py:49
  63.8 6.7 %collective-permute-start.6 = (bf16[32,1152]{1,0:T(8,128)(2,1)S(1)}, bf16[32,1152]{1,0:T(8,128)(2,1)S(1)}, u32[]{:S(2)}, u32[]{:S(2)}) collective-permute-start(bf16[32,1152]{1,0:T(8,128)(2,1)S(1)} %collective-permute-done.5), channel_id=1, source_target_pairs={{0,64},{64,128},{128,192},{192,256},{256,320},{320,384},{384,448},... | collective-permute-start | bytes 221192 | tf_op jit(solution)/shard_map/ppermute | solution.py:49
  71.3 27.2 %collective-permute-start.7 = (bf16[8,32,1152]{2,1,0:T(8,128)(2,1)S(1)}, bf16[8,32,1152]{2,1,0:T(8,128)(2,1)S(1)}, u32[]{:S(2)}, u32[]{:S(2)}) collective-permute-start(bf16[8,32,1152]{2,1,0:T(8,128)(2,1)S(1)} %broadcast_select_fusion), channel_id=1, source_target_pairs={{0,32},{32,0},{1,33},{33,1},{2,34},{34,2},{3,35},{35,3},{4,36},{36... | collective-permute-start | bytes 1769480 | tf_op jit(solution)/shard_map/ppermute | solution.py:41
  99.8 7.2 %collective-permute-start.8 = (bf16[2,8,32,1152]{3,2,0,1:T(8,128)(2,1)}, bf16[2,8,32,1152]{3,2,0,1:T(8,128)(2,1)S(1)}, u32[]{:S(2)}, u32[]{:S(2)}) collective-permute-start(bf16[2,8,32,1152]{3,2,0,1:T(8,128)(2,1)} %pad_maximum_fusion.3), channel_id=1, source_target_pairs={{0,16},{16,0},{1,17},{17,1},{2,18},{18,2},{3,19},{19,3},{4,20},{20... | collective-permute-start | bytes 3538952 | tf_op jit(solution)/shard_map/ppermute | solution.py:41
  125.8 1.4 copy-start.8
  125.8 1.4 copy-start.10
  131.5 7.8 %copy-start.9 = (bf16[1024,384]{0,1:T(8,128)(2,1)S(1)}, bf16[1024,384]{0,1:T(8,128)(2,1)}, u32[]{:S(2)}) copy-start(bf16[1024,384]{0,1:T(8,128)(2,1)} %copy-done.8) | copy-start | bytes 2359300
  131.5 7.8 %copy-start.11 = (bf16[1024,384]{0,1:T(8,128)(2,1)S(1)}, bf16[1024,384]{0,1:T(8,128)(2,1)}, u32[]{:S(2)}) copy-start(bf16[1024,384]{0,1:T(8,128)(2,1)} %copy-done.10) | copy-start | bytes 2359300
  131.5 104.0 %all-to-all-start.1 = ((bf16[16,64,2048]{2,1,0:T(8,128)(2,1)}), bf16[16,64,2048]{2,1,0:T(8,128)(2,1)}, u32[]{:S(2)}, u32[]{:S(2)}) async-start(bf16[16,64,2048]{2,1,0:T(8,128)(2,1)} %bitcast.92), calls=%async_computation.1 | async-start | bytes 8388608 | tf_op jit(solution)/shard_map/all_to_all | solution.py:72
  142.7 1.7 copy-start
  144.6 6.1 %collective-permute-start.9 = (f32[16,32,768]{2,1,0:T(8,128)S(1)}, f32[16,32,768]{2,1,0:T(8,128)}, u32[]{:S(2)}, u32[]{:S(2)}) collective-permute-start(f32[16,32,768]{2,1,0:T(8,128)S(1)} %dynamic-slice_bitcast_fusion), channel_id=1, source_target_pairs={{0,16},{16,0},{1,17},{17,1},{2,18},{18,2},{3,19},{19,3},{4,20},{20... | collective-permute-start | bytes 4718600 | tf_op jit(solution)/shard_map/ppermute | solution.py:133
  152.9 24.7 %collective-permute-start.10 = (f32[8,32,768]{2,1,0:T(8,128)S(1)}, f32[8,32,768]{2,1,0:T(8,128)}, u32[]{:S(2)}, u32[]{:S(2)}) collective-permute-start(f32[8,32,768]{2,1,0:T(8,128)S(1)} %dynamic-slice_bitcast_fusion.1), channel_id=1, source_target_pairs={{0,32},{32,0},{1,33},{33,1},{2,34},{34,2},{3,35},{35,3},{4,36},{36... | collective-permute-start | bytes 2359304 | tf_op jit(solution)/shard_map/ppermute | solution.py:41
  155.1 54.3 %copy-start.7 = (s32[128,2]{0,1:T(2,128)S(1)}, s32[128,2]{0,1:T(2,128)}, u32[]{:S(2)}) copy-start(s32[128,2]{0,1:T(2,128)} %param.8) | copy-start | bytes 3076
  178.9 7.7 %collective-permute-start.11 = (f32[32,768]{1,0:T(8,128)S(1)}, f32[32,768]{1,0:T(8,128)S(1)}, u32[]{:S(2)}, u32[]{:S(2)}) collective-permute-start(f32[32,768]{1,0:T(8,128)S(1)} %dynamic-slice_bitcast_fusion.2), channel_id=1, source_target_pairs={{0,64},{64,128},{128,192},{192,256},{256,320},{320,384},{384,448},... | collective-permute-start | bytes 294920 | tf_op jit(solution)/shard_map/ppermute | solution.py:60
  186.5 7.0 %collective-permute-start.12 = (f32[32,768]{1,0:T(8,128)S(1)}, f32[32,768]{1,0:T(8,128)S(1)}, u32[]{:S(2)}, u32[]{:S(2)}) collective-permute-start(f32[32,768]{1,0:T(8,128)S(1)} %bitcast_add_fusion.8), channel_id=1, source_target_pairs={{0,64},{64,128},{128,192},{192,256},{256,320},{320,384},{384,448},... | collective-permute-start | bytes 294920 | tf_op jit(solution)/shard_map/ppermute | solution.py:60
  193.5 7.0 %collective-permute-start.13 = (f32[32,768]{1,0:T(8,128)S(1)}, f32[32,768]{1,0:T(8,128)S(1)}, u32[]{:S(2)}, u32[]{:S(2)}) collective-permute-start(f32[32,768]{1,0:T(8,128)S(1)} %bitcast_add_fusion.7), channel_id=1, source_target_pairs={{0,64},{64,128},{128,192},{192,256},{256,320},{320,384},{384,448},... | collective-permute-start | bytes 294920 | tf_op jit(solution)/shard_map/ppermute | solution.py:60
  200.5 7.0 %collective-permute-start.14 = (f32[32,768]{1,0:T(8,128)S(1)}, f32[32,768]{1,0:T(8,128)S(1)}, u32[]{:S(2)}, u32[]{:S(2)}) collective-permute-start(f32[32,768]{1,0:T(8,128)S(1)} %bitcast_add_fusion.6), channel_id=1, source_target_pairs={{0,64},{64,128},{128,192},{192,256},{256,320},{320,384},{384,448},... | collective-permute-start | bytes 294920 | tf_op jit(solution)/shard_map/ppermute | solution.py:60
  207.5 7.0 %collective-permute-start.15 = (f32[32,768]{1,0:T(8,128)S(1)}, f32[32,768]{1,0:T(8,128)S(1)}, u32[]{:S(2)}, u32[]{:S(2)}) collective-permute-start(f32[32,768]{1,0:T(8,128)S(1)} %bitcast_add_fusion.5), channel_id=1, source_target_pairs={{0,64},{64,128},{128,192},{192,256},{256,320},{320,384},{384,448},... | collective-permute-start | bytes 294920 | tf_op jit(solution)/shard_map/ppermute | solution.py:60
  214.5 7.1 %collective-permute-start.16 = (f32[32,768]{1,0:T(8,128)S(1)}, f32[32,768]{1,0:T(8,128)S(1)}, u32[]{:S(2)}, u32[]{:S(2)}) collective-permute-start(f32[32,768]{1,0:T(8,128)S(1)} %bitcast_add_fusion.4), channel_id=1, source_target_pairs={{0,64},{64,128},{128,192},{192,256},{256,320},{320,384},{384,448},... | collective-permute-start | bytes 294920 | tf_op jit(solution)/shard_map/ppermute | solution.py:60
  221.7 25.3 %collective-permute-start.17 = (f32[32,768]{1,0:T(8,128)S(1)}, f32[32,768]{1,0:T(8,128)S(1)}, u32[]{:S(2)}, u32[]{:S(2)}) collective-permute-start(f32[32,768]{1,0:T(8,128)S(1)} %bitcast_add_fusion.3), channel_id=1, source_target_pairs={{0,64},{64,128},{128,192},{192,256},{256,320},{320,384},{384,448},... | collective-permute-start | bytes 294920 | tf_op jit(solution)/shard_map/ppermute | solution.py:60
  239.5 1.6 copy-start.1
  243.1 4.5 %copy-start.3 = (bf16[128,1024]{1,0:T(8,128)(2,1)}, bf16[128,1024]{1,0:T(8,128)(2,1)S(1)}, u32[]{:S(2)}) copy-start(bf16[128,1024]{1,0:T(8,128)(2,1)S(1)} %multiply_reduce_fusion.1) | copy-start | bytes 786436

commit v15 on v11

--- a/solution.py
+++ b/solution.py
@@ -163,7 +163,7 @@
     pick_wide = pick_rows.reshape(tok_count, top_count, feature_total)
     layer_output = jnp.sum(combine[:, :, None] * pick_wide, axis=1).astype(jnp.bfloat16)
     combine_grad = jnp.sum(upstream_wide[:, None, :] * pick_wide, axis=2)
-    after_tokens = summed + 0.0 * layer_output[0, 0].astype(jnp.float32)
+    after_tokens = summed
     gate_grad = after_tokens[:, :hidden_total][None]
     up_grad = after_tokens[:, hidden_total:][None]
     return (layer_output, token_grad, combine_grad, gate_grad, up_grad)

time: 248 us -> 251 us (1.012)
  the two profiles are of different devices: /device:TPU:1 before, /device:TPU:388 now
where the time goes in v15:
time: 251 us; the launch traced here: 250 us
  waiting for transfers between devices  148 us (59%)
  starting transfers between devices  58.7 us (23%)
  matrix products  21.6 us (9%)
  other arithmetic  10.9 us (4%)
  local copies, waits for them, and re-layouts  9.54 us (4%)
    ppermute x3, waiting for transfers between devices, swap_partner(): return lax.ppermute(values, axis, perm=[(0, 1), (1, 0)])  68.2 us
    ppermute x7, waiting for transfers between devices, ring_reduce_scatter(): lax.ppermute(carry, axis, perm=[(i, (i + 1) % size) for i in range(size)])  38.9 us
    ppermute x7, waiting for transfers between devices, ring_gather(): lax.ppermute(moving, axis, perm=[(i, (i + 1) % size) for i in range(size)])  37.1 us
    all_to_all x2, starting transfers between devices, trade_rows(): lax.all_to_all(buffer, EXPERT_AXES, split_axis=0, concat_axis=0, tiled=True)  18.1 us
    ppermute x7, starting transfers between devices, ring_reduce_scatter(): lax.ppermute(carry, axis, perm=[(i, (i + 1) % size) for i in range(size)])  15.3 us
    ppermute x7, starting transfers between devices, ring_gather(): lax.ppermute(moving, axis, perm=[(i, (i + 1) % size) for i in range(size)])  15 us
    ppermute x3, starting transfers between devices, swap_partner(): return lax.ppermute(values, axis, perm=[(0, 1), (1, 0)])  8.3 us
  transfers between devices with their start and end apart: 20, of which 18 were waited for; matrix products, arithmetic and copies ran while one was open for 4% of the time, Pallas kernels for 0%

profile of v15, /device:TPU:388, one launch (start us, length us, event | category | flops | bytes accessed | tf_op | source)
XLA Modules:
  0.0 250.0 jit_solution(11051149882688887758)
XLA Ops:
  6.2 3.2 %convolution_convert_fusion = bf16[1024,2048]{1,0:T(8,128)(2,1)} fusion(bf16[256,1024]{1,0:T(8,128)(2,1)S(1)} %multiply_convert_fusion.3, bf16[256,1024]{1,0:T(8,128)(2,1)S(1)} %reshape.136, s32[256]{0:T(256)S(1)} %multiply_add_fusion.1), kind=kOutput, calls=%fused_computation.2 | convolution fusion | flops 1078198272 | bytes 5243904 | tf_op jit(solution)/shard_map/dot_general | solution.py:117
  9.4 8.0 %all-to-all-start = ((bf16[16,64,2048]{2,1,0:T(8,128)(2,1)}), bf16[16,64,2048]{2,1,0:T(8,128)(2,1)}, u32[]{:S(2)}, u32[]{:S(2)}) async-start(bf16[16,64,2048]{2,1,0:T(8,128)(2,1)} %bitcast.88), calls=%async_computation | async-start | bytes 8388608 | tf_op jit(solution)/shard_map/all_to_all | solution.py:72
  17.5 3.5 %collective-permute-start = (bf16[32,1152]{1,0:T(8,128)(2,1)S(1)}, bf16[32,1152]{1,0:T(8,128)(2,1)S(1)}, u32[]{:S(2)}, u32[]{:S(2)}) collective-permute-start(bf16[32,1152]{1,0:T(8,128)(2,1)S(1)} %pad_maximum_fusion.6), channel_id=1, source_target_pairs={{0,64},{64,128},{128,192},{192,256},{256,320},{320,384},{384,448},... | collective-permute-start | bytes 221192 | tf_op jit(solution)/shard_map/ppermute | solution.py:49
  21.0 4.1 %collective-permute-done = bf16[32,1152]{1,0:T(8,128)(2,1)S(1)} collective-permute-done((bf16[32,1152]{1,0:T(8,128)(2,1)S(1)}, bf16[32,1152]{1,0:T(8,128)(2,1)S(1)}, u32[]{:S(2)}, u32[]{:S(2)}) %collective-permute-start) | collective-permute-done | bytes 73760 | tf_op jit(solution)/shard_map/ppermute | solution.py:49
  27.2 5.4 %collective-permute-done.1 = bf16[32,1152]{1,0:T(8,128)(2,1)S(1)} collective-permute-done((bf16[32,1152]{1,0:T(8,128)(2,1)S(1)}, bf16[32,1152]{1,0:T(8,128)(2,1)S(1)}, u32[]{:S(2)}, u32[]{:S(2)}) %collective-permute-start.1) | collective-permute-done | bytes 73760 | tf_op jit(solution)/shard_map/ppermute | solution.py:49
  34.5 5.5 %collective-permute-done.2 = bf16[32,1152]{1,0:T(8,128)(2,1)S(1)} collective-permute-done((bf16[32,1152]{1,0:T(8,128)(2,1)S(1)}, bf16[32,1152]{1,0:T(8,128)(2,1)S(1)}, u32[]{:S(2)}, u32[]{:S(2)}) %collective-permute-start.2) | collective-permute-done | bytes 73760 | tf_op jit(solution)/shard_map/ppermute | solution.py:49
  42.0 5.5 %collective-permute-done.3 = bf16[32,1152]{1,0:T(8,128)(2,1)S(1)} collective-permute-done((bf16[32,1152]{1,0:T(8,128)(2,1)S(1)}, bf16[32,1152]{1,0:T(8,128)(2,1)S(1)}, u32[]{:S(2)}, u32[]{:S(2)}) %collective-permute-start.3) | collective-permute-done | bytes 73760 | tf_op jit(solution)/shard_map/ppermute | solution.py:49
  49.4 5.5 %collective-permute-done.4 = bf16[32,1152]{1,0:T(8,128)(2,1)S(1)} collective-permute-done((bf16[32,1152]{1,0:T(8,128)(2,1)S(1)}, bf16[32,1152]{1,0:T(8,128)(2,1)S(1)}, u32[]{:S(2)}, u32[]{:S(2)}) %collective-permute-start.4) | collective-permute-done | bytes 73760 | tf_op jit(solution)/shard_map/ppermute | solution.py:49
  56.9 5.5 %collective-permute-done.5 = bf16[32,1152]{1,0:T(8,128)(2,1)S(1)} collective-permute-done((bf16[32,1152]{1,0:T(8,128)(2,1)S(1)}, bf16[32,1152]{1,0:T(8,128)(2,1)S(1)}, u32[]{:S(2)}, u32[]{:S(2)}) %collective-permute-start.5) | collective-permute-done | bytes 73760 | tf_op jit(solution)/shard_map/ppermute | solution.py:49
  64.3 5.5 %collective-permute-done.6 = bf16[32,1152]{1,0:T(8,128)(2,1)S(1)} collective-permute-done((bf16[32,1152]{1,0:T(8,128)(2,1)S(1)}, bf16[32,1152]{1,0:T(8,128)(2,1)S(1)}, u32[]{:S(2)}, u32[]{:S(2)}) %collective-permute-start.6) | collective-permute-done | bytes 73760 | tf_op jit(solution)/shard_map/ppermute | solution.py:49
  70.6 3.1 %collective-permute-start.7 = (bf16[8,32,1152]{2,1,0:T(8,128)(2,1)S(1)}, bf16[8,32,1152]{2,1,0:T(8,128)(2,1)S(1)}, u32[]{:S(2)}, u32[]{:S(2)}) collective-permute-start(bf16[8,32,1152]{2,1,0:T(8,128)(2,1)S(1)} %broadcast_select_fusion), channel_id=1, source_target_pairs={{0,32},{32,0},{1,33},{33,1},{2,34},{34,2},{3,35},{35,3},{4,36},{36... | collective-permute-start | bytes 1769480 | tf_op jit(solution)/shard_map/ppermute | solution.py:41
  73.7 30.8 %collective-permute-done.7 = bf16[8,32,1152]{2,1,0:T(8,128)(2,1)S(1)} collective-permute-done((bf16[8,32,1152]{2,1,0:T(8,128)(2,1)S(1)}, bf16[8,32,1152]{2,1,0:T(8,128)(2,1)S(1)}, u32[]{:S(2)}, u32[]{:S(2)}) %collective-permute-start.7) | collective-permute-done | bytes 589856 | tf_op jit(solution)/shard_map/ppermute | solution.py:41
  108.0 2.8 %collective-permute-done.8 = bf16[2,8,32,1152]{3,2,0,1:T(8,128)(2,1)S(1)} collective-permute-done((bf16[2,8,32,1152]{3,2,0,1:T(8,128)(2,1)}, bf16[2,8,32,1152]{3,2,0,1:T(8,128)(2,1)S(1)}, u32[]{:S(2)}, u32[]{:S(2)}) %collective-permute-start.8) | collective-permute-done | bytes 1179680 | tf_op jit(solution)/shard_map/ppermute | solution.py:41
  111.3 3.5 %fusion.8 = f32[1024,768]{0,1:T(8,128)S(1)} fusion(bf16[1024,2048]{1,0:T(8,128)(2,1)} %bitcast.2, bf16[1024,1152]{1,0:T(8,128)(2,1)S(1)} %bitcast.94), kind=kOutput, calls=%fused_computation.14 | convolution fusion | flops 1610612736 | bytes 6815744 | tf_op jit(solution)/shard_map/dot_general | solution.py:16
  114.8 3.1 %multiply_convert_fusion.1 = (bf16[1024,384]{0,1:T(8,128)(2,1)S(1)}, bf16[1024,384]{0,1:T(8,128)(2,1)S(1)}) fusion(f32[1024,768]{0,1:T(8,128)S(1)} %fusion.8, bf16[1024,1152]{1,0:T(8,128)(2,1)S(1)} %bitcast.95, bf16[1024,2048]{1,0:T(8,128)(2,1)} %bitcast.2), kind=kOutput, calls=%fused_computation.20 | convolution fusion | flops 810418176 | bytes 7602176 | tf_op jit(solution)/shard_map/dot_general | solution.py:27
  121.2 2.4 pad_maximum_fusion
  123.6 10.2 %all-to-all-start.1 = ((bf16[16,64,2048]{2,1,0:T(8,128)(2,1)}), bf16[16,64,2048]{2,1,0:T(8,128)(2,1)}, u32[]{:S(2)}, u32[]{:S(2)}) async-start(bf16[16,64,2048]{2,1,0:T(8,128)(2,1)} %bitcast.89), calls=%async_computation.1 | async-start | bytes 8388608 | tf_op jit(solution)/shard_map/all_to_all | solution.py:72
  133.8 3.4 %fusion.6 = f32[1024,768]{1,0:T(8,128)S(1)} fusion(bf16[1024,2048]{1,0:T(8,128)(2,1)} %bitcast.2, bf16[1024,384]{0,1:T(8,128)(2,1)S(1)} %copy-done.9, bf16[1024,384]{0,1:T(8,128)(2,1)S(1)} %copy-done.7), kind=kOutput, calls=%fused_computation.12 | convolution fusion | flops 1613758464 | bytes 6815744 | tf_op jit(solution)/shard_map/dot_general | solution.py:125
  141.0 3.5 %collective-permute-done.9 = f32[16,32,768]{2,1,0:T(8,128)} collective-permute-done((f32[16,32,768]{2,1,0:T(8,128)S(1)}, f32[16,32,768]{2,1,0:T(8,128)}, u32[]{:S(2)}, u32[]{:S(2)}) %collective-permute-start.9) | collective-permute-done | bytes 1572896 | tf_op jit(solution)/shard_map/ppermute | solution.py:133
  146.7 3.1 %collective-permute-start.10 = (f32[8,32,768]{2,1,0:T(8,128)S(1)}, f32[8,32,768]{2,1,0:T(8,128)}, u32[]{:S(2)}, u32[]{:S(2)}) collective-permute-start(f32[8,32,768]{2,1,0:T(8,128)S(1)} %dynamic-slice_bitcast_fusion.1), channel_id=1, source_target_pairs={{0,32},{32,0},{1,33},{33,1},{2,34},{34,2},{3,35},{35,3},{4,36},{36... | collective-permute-start | bytes 2359304 | tf_op jit(solution)/shard_map/ppermute | solution.py:41
  149.8 34.6 %collective-permute-done.10 = f32[8,32,768]{2,1,0:T(8,128)} collective-permute-done((f32[8,32,768]{2,1,0:T(8,128)S(1)}, f32[8,32,768]{2,1,0:T(8,128)}, u32[]{:S(2)}, u32[]{:S(2)}) %collective-permute-start.10) | collective-permute-done | bytes 786464 | tf_op jit(solution)/shard_map/ppermute | solution.py:41
  185.7 3.6 %collective-permute-start.11 = (f32[32,768]{1,0:T(8,128)S(1)}, f32[32,768]{1,0:T(8,128)S(1)}, u32[]{:S(2)}, u32[]{:S(2)}) collective-permute-start(f32[32,768]{1,0:T(8,128)S(1)} %dynamic-slice_bitcast_fusion.2), channel_id=1, source_target_pairs={{0,64},{64,128},{128,192},{192,256},{256,320},{320,384},{384,448},... | collective-permute-start | bytes 294920 | tf_op jit(solution)/shard_map/ppermute | solution.py:60
  189.3 4.9 %collective-permute-done.11 = f32[32,768]{1,0:T(8,128)S(1)} collective-permute-done((f32[32,768]{1,0:T(8,128)S(1)}, f32[32,768]{1,0:T(8,128)S(1)}, u32[]{:S(2)}, u32[]{:S(2)}) %collective-permute-start.11) | collective-permute-done | bytes 98336 | tf_op jit(solution)/shard_map/ppermute | solution.py:60
  196.2 5.8 %collective-permute-done.12 = f32[32,768]{1,0:T(8,128)S(1)} collective-permute-done((f32[32,768]{1,0:T(8,128)S(1)}, f32[32,768]{1,0:T(8,128)S(1)}, u32[]{:S(2)}, u32[]{:S(2)}) %collective-permute-start.12) | collective-permute-done | bytes 98336 | tf_op jit(solution)/shard_map/ppermute | solution.py:60
  203.9 5.8 %collective-permute-done.13 = f32[32,768]{1,0:T(8,128)S(1)} collective-permute-done((f32[32,768]{1,0:T(8,128)S(1)}, f32[32,768]{1,0:T(8,128)S(1)}, u32[]{:S(2)}, u32[]{:S(2)}) %collective-permute-start.13) | collective-permute-done | bytes 98336 | tf_op jit(solution)/shard_map/ppermute | solution.py:60
  211.7 5.8 %collective-permute-done.14 = f32[32,768]{1,0:T(8,128)S(1)} collective-permute-done((f32[32,768]{1,0:T(8,128)S(1)}, f32[32,768]{1,0:T(8,128)S(1)}, u32[]{:S(2)}, u32[]{:S(2)}) %collective-permute-start.14) | collective-permute-done | bytes 98336 | tf_op jit(solution)/shard_map/ppermute | solution.py:60
  219.6 5.6 %collective-permute-done.15 = f32[32,768]{1,0:T(8,128)S(1)} collective-permute-done((f32[32,768]{1,0:T(8,128)S(1)}, f32[32,768]{1,0:T(8,128)S(1)}, u32[]{:S(2)}, u32[]{:S(2)}) %collective-permute-start.15) | collective-permute-done | bytes 98336 | tf_op jit(solution)/shard_map/ppermute | solution.py:60
  227.2 5.7 %collective-permute-done.16 = f32[32,768]{1,0:T(8,128)S(1)} collective-permute-done((f32[32,768]{1,0:T(8,128)S(1)}, f32[32,768]{1,0:T(8,128)S(1)}, u32[]{:S(2)}, u32[]{:S(2)}) %collective-permute-start.16) | collective-permute-done | bytes 98336 | tf_op jit(solution)/shard_map/ppermute | solution.py:60
  232.9 2.1 collective-permute-start.17
  235.2 5.4 %collective-permute-done.17 = f32[32,768]{1,0:T(8,128)S(1)} collective-permute-done((f32[32,768]{1,0:T(8,128)S(1)}, f32[32,768]{1,0:T(8,128)S(1)}, u32[]{:S(2)}, u32[]{:S(2)}) %collective-permute-start.17) | collective-permute-done | bytes 98336 | tf_op jit(solution)/shard_map/ppermute | solution.py:60
  241.3 2.4 multiply_reduce_fusion
  243.7 2.7 %fusion.13 = bf16[128,1024]{1,0:T(8,128)(2,1)} fusion(pred[128,1024]{1,0:T(8,128)(4,1)S(1)} %fusion.19, bf16[1024,2048]{1,0:T(8,128)(2,1)} %bitcast.25), kind=kOutput, calls=%fused_computation.26 | convolution fusion | flops 268566528 | bytes 2490368 | tf_op jit(solution)/shard_map/dot_general | solution.py:160
  (93 shorter events, 46.4 us)
Async XLA Ops:
  0.6 4.4 %copy-start.1 = (bf16[128,1024]{1,0:T(8,128)(2,1)S(1)}, bf16[128,1024]{1,0:T(8,128)(2,1)}, u32[]{:S(2)}) copy-start(bf16[128,1024]{1,0:T(8,128)(2,1)} %param.10) | copy-start | bytes 786436
  9.4 8.0 %copy-start.2 = (bf16[1,32,384]{2,1,0:T(8,128)(2,1)S(1)}, bf16[1,32,384]{2,1,0:T(8,128)(2,1)}, u32[]{:S(2)}) copy-start(bf16[1,32,384]{2,1,0:T(8,128)(2,1)} %param.13) | copy-start | bytes 73732
  9.4 8.0 %copy-start.3 = (bf16[1,32,384]{2,1,0:T(8,128)(2,1)S(1)}, bf16[1,32,384]{2,1,0:T(8,128)(2,1)}, u32[]{:S(2)}) copy-start(bf16[1,32,384]{2,1,0:T(8,128)(2,1)} %param.12) | copy-start | bytes 73732
  9.4 8.0 %copy-start.4 = (bf16[1,32,384]{2,1,0:T(8,128)(2,1)S(1)}, bf16[1,32,384]{2,1,0:T(8,128)(2,1)}, u32[]{:S(2)}) copy-start(bf16[1,32,384]{2,1,0:T(8,128)(2,1)} %param.11) | copy-start | bytes 73732
  9.4 101.9 %all-to-all-start = ((bf16[16,64,2048]{2,1,0:T(8,128)(2,1)}), bf16[16,64,2048]{2,1,0:T(8,128)(2,1)}, u32[]{:S(2)}, u32[]{:S(2)}) async-start(bf16[16,64,2048]{2,1,0:T(8,128)(2,1)} %bitcast.88), calls=%async_computation | async-start | bytes 8388608 | tf_op jit(solution)/shard_map/all_to_all | solution.py:72
  17.5 7.7 %collective-permute-start = (bf16[32,1152]{1,0:T(8,128)(2,1)S(1)}, bf16[32,1152]{1,0:T(8,128)(2,1)S(1)}, u32[]{:S(2)}, u32[]{:S(2)}) collective-permute-start(bf16[32,1152]{1,0:T(8,128)(2,1)S(1)} %pad_maximum_fusion.6), channel_id=1, source_target_pairs={{0,64},{64,128},{128,192},{192,256},{256,320},{320,384},{384,448},... | collective-permute-start | bytes 221192 | tf_op jit(solution)/shard_map/ppermute | solution.py:49
  25.2 7.4 %collective-permute-start.1 = (bf16[32,1152]{1,0:T(8,128)(2,1)S(1)}, bf16[32,1152]{1,0:T(8,128)(2,1)S(1)}, u32[]{:S(2)}, u32[]{:S(2)}) collective-permute-start(bf16[32,1152]{1,0:T(8,128)(2,1)S(1)} %collective-permute-done), channel_id=1, source_target_pairs={{0,64},{64,128},{128,192},{192,256},{256,320},{320,384},{384,448},... | collective-permute-start | bytes 221192 | tf_op jit(solution)/shard_map/ppermute | solution.py:49
  32.6 7.4 %collective-permute-start.2 = (bf16[32,1152]{1,0:T(8,128)(2,1)S(1)}, bf16[32,1152]{1,0:T(8,128)(2,1)S(1)}, u32[]{:S(2)}, u32[]{:S(2)}) collective-permute-start(bf16[32,1152]{1,0:T(8,128)(2,1)S(1)} %collective-permute-done.1), channel_id=1, source_target_pairs={{0,64},{64,128},{128,192},{192,256},{256,320},{320,384},{384,448},... | collective-permute-start | bytes 221192 | tf_op jit(solution)/shard_map/ppermute | solution.py:49
  40.0 7.4 %collective-permute-start.3 = (bf16[32,1152]{1,0:T(8,128)(2,1)S(1)}, bf16[32,1152]{1,0:T(8,128)(2,1)S(1)}, u32[]{:S(2)}, u32[]{:S(2)}) collective-permute-start(bf16[32,1152]{1,0:T(8,128)(2,1)S(1)} %collective-permute-done.2), channel_id=1, source_target_pairs={{0,64},{64,128},{128,192},{192,256},{256,320},{320,384},{384,448},... | collective-permute-start | bytes 221192 | tf_op jit(solution)/shard_map/ppermute | solution.py:49
  47.5 7.4 %collective-permute-start.4 = (bf16[32,1152]{1,0:T(8,128)(2,1)S(1)}, bf16[32,1152]{1,0:T(8,128)(2,1)S(1)}, u32[]{:S(2)}, u32[]{:S(2)}) collective-permute-start(bf16[32,1152]{1,0:T(8,128)(2,1)S(1)} %collective-permute-done.3), channel_id=1, source_target_pairs={{0,64},{64,128},{128,192},{192,256},{256,320},{320,384},{384,448},... | collective-permute-start | bytes 221192 | tf_op jit(solution)/shard_map/ppermute | solution.py:49
  54.9 7.4 %collective-permute-start.5 = (bf16[32,1152]{1,0:T(8,128)(2,1)S(1)}, bf16[32,1152]{1,0:T(8,128)(2,1)S(1)}, u32[]{:S(2)}, u32[]{:S(2)}) collective-permute-start(bf16[32,1152]{1,0:T(8,128)(2,1)S(1)} %collective-permute-done.4), channel_id=1, source_target_pairs={{0,64},{64,128},{128,192},{192,256},{256,320},{320,384},{384,448},... | collective-permute-start | bytes 221192 | tf_op jit(solution)/shard_map/ppermute | solution.py:49
  62.4 7.4 %collective-permute-start.6 = (bf16[32,1152]{1,0:T(8,128)(2,1)S(1)}, bf16[32,1152]{1,0:T(8,128)(2,1)S(1)}, u32[]{:S(2)}, u32[]{:S(2)}) collective-permute-start(bf16[32,1152]{1,0:T(8,128)(2,1)S(1)} %collective-permute-done.5), channel_id=1, source_target_pairs={{0,64},{64,128},{128,192},{192,256},{256,320},{320,384},{384,448},... | collective-permute-start | bytes 221192 | tf_op jit(solution)/shard_map/ppermute | solution.py:49
  70.6 33.9 %collective-permute-start.7 = (bf16[8,32,1152]{2,1,0:T(8,128)(2,1)S(1)}, bf16[8,32,1152]{2,1,0:T(8,128)(2,1)S(1)}, u32[]{:S(2)}, u32[]{:S(2)}) collective-permute-start(bf16[8,32,1152]{2,1,0:T(8,128)(2,1)S(1)} %broadcast_select_fusion), channel_id=1, source_target_pairs={{0,32},{32,0},{1,33},{33,1},{2,34},{34,2},{3,35},{35,3},{4,36},{36... | collective-permute-start | bytes 1769480 | tf_op jit(solution)/shard_map/ppermute | solution.py:41
  105.9 4.9 %collective-permute-start.8 = (bf16[2,8,32,1152]{3,2,0,1:T(8,128)(2,1)}, bf16[2,8,32,1152]{3,2,0,1:T(8,128)(2,1)S(1)}, u32[]{:S(2)}, u32[]{:S(2)}) collective-permute-start(bf16[2,8,32,1152]{3,2,0,1:T(8,128)(2,1)} %pad_maximum_fusion.3), channel_id=1, source_target_pairs={{0,16},{16,0},{1,17},{17,1},{2,18},{18,2},{3,19},{19,3},{4,20},{20... | collective-permute-start | bytes 3538952 | tf_op jit(solution)/shard_map/ppermute | solution.py:41
  117.9 1.4 copy-start.6
  117.9 1.4 copy-start.8
  123.6 10.2 %copy-start.7 = (bf16[1024,384]{0,1:T(8,128)(2,1)S(1)}, bf16[1024,384]{0,1:T(8,128)(2,1)}, u32[]{:S(2)}) copy-start(bf16[1024,384]{0,1:T(8,128)(2,1)} %copy-done.6) | copy-start | bytes 2359300
  123.6 10.2 %copy-start.9 = (bf16[1024,384]{0,1:T(8,128)(2,1)S(1)}, bf16[1024,384]{0,1:T(8,128)(2,1)}, u32[]{:S(2)}) copy-start(bf16[1024,384]{0,1:T(8,128)(2,1)} %copy-done.8) | copy-start | bytes 2359300
  123.6 117.7 %all-to-all-start.1 = ((bf16[16,64,2048]{2,1,0:T(8,128)(2,1)}), bf16[16,64,2048]{2,1,0:T(8,128)(2,1)}, u32[]{:S(2)}, u32[]{:S(2)}) async-start(bf16[16,64,2048]{2,1,0:T(8,128)(2,1)} %bitcast.89), calls=%async_computation.1 | async-start | bytes 8388608 | tf_op jit(solution)/shard_map/all_to_all | solution.py:72
  137.2 1.7 copy-start
  139.1 5.4 %collective-permute-start.9 = (f32[16,32,768]{2,1,0:T(8,128)S(1)}, f32[16,32,768]{2,1,0:T(8,128)}, u32[]{:S(2)}, u32[]{:S(2)}) collective-permute-start(f32[16,32,768]{2,1,0:T(8,128)S(1)} %dynamic-slice_bitcast_fusion), channel_id=1, source_target_pairs={{0,16},{16,0},{1,17},{17,1},{2,18},{18,2},{3,19},{19,3},{4,20},{20... | collective-permute-start | bytes 4718600 | tf_op jit(solution)/shard_map/ppermute | solution.py:133
  146.7 37.8 %collective-permute-start.10 = (f32[8,32,768]{2,1,0:T(8,128)S(1)}, f32[8,32,768]{2,1,0:T(8,128)}, u32[]{:S(2)}, u32[]{:S(2)}) collective-permute-start(f32[8,32,768]{2,1,0:T(8,128)S(1)} %dynamic-slice_bitcast_fusion.1), channel_id=1, source_target_pairs={{0,32},{32,0},{1,33},{33,1},{2,34},{34,2},{3,35},{35,3},{4,36},{36... | collective-permute-start | bytes 2359304 | tf_op jit(solution)/shard_map/ppermute | solution.py:41
  149.8 77.3 %copy-start.5 = (s32[128,2]{0,1:T(2,128)S(1)}, s32[128,2]{0,1:T(2,128)}, u32[]{:S(2)}) copy-start(s32[128,2]{0,1:T(2,128)} %param.8) | copy-start | bytes 3076
  185.7 8.5 %collective-permute-start.11 = (f32[32,768]{1,0:T(8,128)S(1)}, f32[32,768]{1,0:T(8,128)S(1)}, u32[]{:S(2)}, u32[]{:S(2)}) collective-permute-start(f32[32,768]{1,0:T(8,128)S(1)} %dynamic-slice_bitcast_fusion.2), channel_id=1, source_target_pairs={{0,64},{64,128},{128,192},{192,256},{256,320},{320,384},{384,448},... | collective-permute-start | bytes 294920 | tf_op jit(solution)/shard_map/ppermute | solution.py:60
  194.2 7.7 %collective-permute-start.12 = (f32[32,768]{1,0:T(8,128)S(1)}, f32[32,768]{1,0:T(8,128)S(1)}, u32[]{:S(2)}, u32[]{:S(2)}) collective-permute-start(f32[32,768]{1,0:T(8,128)S(1)} %bitcast_add_fusion.8), channel_id=1, source_target_pairs={{0,64},{64,128},{128,192},{192,256},{256,320},{320,384},{384,448},... | collective-permute-start | bytes 294920 | tf_op jit(solution)/shard_map/ppermute | solution.py:60
  202.0 7.7 %collective-permute-start.13 = (f32[32,768]{1,0:T(8,128)S(1)}, f32[32,768]{1,0:T(8,128)S(1)}, u32[]{:S(2)}, u32[]{:S(2)}) collective-permute-start(f32[32,768]{1,0:T(8,128)S(1)} %bitcast_add_fusion.7), channel_id=1, source_target_pairs={{0,64},{64,128},{128,192},{192,256},{256,320},{320,384},{384,448},... | collective-permute-start | bytes 294920 | tf_op jit(solution)/shard_map/ppermute | solution.py:60
  209.7 7.7 %collective-permute-start.14 = (f32[32,768]{1,0:T(8,128)S(1)}, f32[32,768]{1,0:T(8,128)S(1)}, u32[]{:S(2)}, u32[]{:S(2)}) collective-permute-start(f32[32,768]{1,0:T(8,128)S(1)} %bitcast_add_fusion.6), channel_id=1, source_target_pairs={{0,64},{64,128},{128,192},{192,256},{256,320},{320,384},{384,448},... | collective-permute-start | bytes 294920 | tf_op jit(solution)/shard_map/ppermute | solution.py:60
  217.4 7.7 %collective-permute-start.15 = (f32[32,768]{1,0:T(8,128)S(1)}, f32[32,768]{1,0:T(8,128)S(1)}, u32[]{:S(2)}, u32[]{:S(2)}) collective-permute-start(f32[32,768]{1,0:T(8,128)S(1)} %bitcast_add_fusion.5), channel_id=1, source_target_pairs={{0,64},{64,128},{128,192},{192,256},{256,320},{320,384},{384,448},... | collective-permute-start | bytes 294920 | tf_op jit(solution)/shard_map/ppermute | solution.py:60
  225.2 7.7 %collective-permute-start.16 = (f32[32,768]{1,0:T(8,128)S(1)}, f32[32,768]{1,0:T(8,128)S(1)}, u32[]{:S(2)}, u32[]{:S(2)}) collective-permute-start(f32[32,768]{1,0:T(8,128)S(1)} %bitcast_add_fusion.4), channel_id=1, source_target_pairs={{0,64},{64,128},{128,192},{192,256},{256,320},{320,384},{384,448},... | collective-permute-start | bytes 294920 | tf_op jit(solution)/shard_map/ppermute | solution.py:60
  232.9 7.7 %collective-permute-start.17 = (f32[32,768]{1,0:T(8,128)S(1)}, f32[32,768]{1,0:T(8,128)S(1)}, u32[]{:S(2)}, u32[]{:S(2)}) collective-permute-start(f32[32,768]{1,0:T(8,128)S(1)} %bitcast_add_fusion.3), channel_id=1, source_target_pairs={{0,64},{64,128},{128,192},{192,256},{256,320},{320,384},{384,448},... | collective-permute-start | bytes 294920 | tf_op jit(solution)/shard_map/ppermute | solution.py:60
